TPU v7x, 128 devices: a whole 4x4x4 slice. The times are simulated.
128 devices in a mesh: dp: 8 (over y, core), tensor: 16 (over z, x).
Axes of the slice: x: 4, y: 4, z: 4, core: 2. Of those that a mesh axis runs over, the one named last changes fastest.
Arguments:
- features: bfloat16 [1024, 4096], P('dp'), may hold values from -6 to 6
- enc_in: bfloat16 [4096, 2048], P(None, 'tensor'), may hold values from -0.09375 to 0.09375
- enc_out: bfloat16 [2048, 8192], P('tensor'), may hold values from -0.125 to 0.125
- noise: bfloat16 [1024, 4096], P('dp', 'tensor'), may hold values from -6 to 6
- in_weight: bfloat16 [4096, 16384], P('dp', 'tensor'), may hold values from -0.09375 to 0.09375
- out_weight: bfloat16 [4096, 16384], P('dp', 'tensor'), may hold values from -0.046875 to 0.046875
- probes: bfloat16 [2, 1024, 4096], P(None, 'dp'), may hold values from -6 to 6
Outputs:
- flowed: float32 [1024, 4096], P('dp', 'tensor')
- logdet: float32 [1024], P('dp')
All inputs are finite; a program needn't handle non-finite values.
Results may differ from a plain program's by a relative error of at most 0.017.
Values may be sent and summed in bfloat16 or wider, within the bound.
No kernel may reach another device: no remote copies, remote signals or barrier semaphores. Data moves between devices by JAX's collectives and lax.ppermute only.
A program may use at most 128 MiB of HBM per device.

v0:
```python
import jax
import jax.numpy as jnp
from jax import lax
from jax.sharding import PartitionSpec as P

L = 4096
PROBES = 2
TERMS = 3


def gather_dp(block):
    n = lax.axis_size("dp")
    ny = n // 2

    def perm(fn):
        return [(d, fn(d // 2, d % 2)) for d in range(n)]

    up = perm(lambda y, c: 2 * ((y + 1) % ny) + c)
    down = perm(lambda y, c: 2 * ((y - 1) % ny) + c)
    swap = perm(lambda y, c: 2 * y + 1 - c)
    fwd = perm(lambda y, c: 2 * ((y + 1) % ny) if c == 0 else 2 * ((y - 1) % ny) + 1)

    from_below = lax.ppermute(block, "dp", up)
    from_above = lax.ppermute(block, "dp", down)
    partner = lax.ppermute(block, "dp", swap)
    d = lax.axis_index("dp")
    y, c = d // 2, d % 2
    relay = jnp.where(c == 0, from_below, from_above)
    far = lax.ppermute(relay, "dp", fwd)
    partner_near = lax.ppermute(jnp.stack([from_below, from_above]), "dp", swap)
    partner_far = lax.ppermute(far, "dp", swap)
    stacked = jnp.stack(
        [block, partner, from_below, from_above, far, partner_near[0], partner_near[1], partner_far]
    )
    target = jnp.arange(n)
    rel = (target // 2 - y) % ny
    same_pos = jnp.array([0, 3, 4, 2], jnp.int32)[rel]
    other_pos = jnp.array([1, 6, 7, 5], jnp.int32)[rel]
    order = jnp.where(target % 2 == c, same_pos, other_pos)
    return jnp.take(stacked, order, axis=0)


def reduce_scatter_pieces(pieces):
    received = lax.all_to_all(pieces.astype(jnp.bfloat16), "tensor", 0, 0)
    return jnp.sum(received.astype(jnp.float32), axis=0)


def all_gather_pieces(piece):
    n = lax.axis_size("tensor")
    return lax.all_to_all(jnp.broadcast_to(piece[None], (n,) + piece.shape), "tensor", 0, 0)


def psum_butterfly(value):
    n = lax.axis_size("tensor")
    step = 1
    while step < n:
        value = value + lax.ppermute(value, "tensor", [(t, t ^ step) for t in range(n)])
        step *= 2
    return value


def series(start, w_in_p, w_out_p, slope, side):
    n, cols = w_in_p.shape[0], w_in_p.shape[1]
    t = lax.axis_index("tensor")
    start_p = start.reshape(start.shape[0], start.shape[1], n, cols)
    pulled = jnp.einsum("pbsc,sch->pbh", start_p, w_out_p, preferred_element_type=jnp.float32)
    scaled = (pulled * slope[None]).astype(jnp.bfloat16)
    part_u = jnp.einsum("pbh,sch->spbc", scaled, w_in_p, preferred_element_type=jnp.float32)
    with_side = reduce_scatter_pieces(jnp.concatenate([part_u, side[:, None]], axis=1))
    u_here = with_side[:-1].astype(jnp.bfloat16)
    side = with_side[-1]
    pushed = jnp.einsum("pbsc,sch->pbh", start_p, w_in_p, preferred_element_type=jnp.float32)
    scaled_t = (pushed * slope[None]).astype(jnp.bfloat16)
    part_v = jnp.einsum("pbh,sch->spbc", scaled_t, w_out_p, preferred_element_type=jnp.float32)
    v_here = reduce_scatter_pieces(part_v).astype(jnp.bfloat16)
    u_pieces = all_gather_pieces(u_here)
    v_pieces = all_gather_pieces(v_here)
    start_here = lax.dynamic_index_in_dim(start_p, t, axis=2, keepdims=False).astype(jnp.float32)
    first = jnp.sum(start_here * u_here.astype(jnp.float32), axis=(0, 2))
    second = jnp.sum(v_here.astype(jnp.float32) * u_here.astype(jnp.float32), axis=(0, 2))
    pulled3 = jnp.einsum("spbc,sch->pbh", u_pieces, w_out_p, preferred_element_type=jnp.float32)
    scaled3 = (pulled3 * slope[None]).astype(jnp.bfloat16)
    part3 = jnp.einsum("pbh,sch->spbc", scaled3, w_in_p, preferred_element_type=jnp.float32)
    third = jnp.sum(v_pieces.astype(jnp.float32) * part3, axis=(0, 1, 3))
    coeffs = [(-1.0) ** k / (k + 1) for k in range(TERMS)]
    local_sum = coeffs[0] * first + coeffs[1] * second + coeffs[2] * third
    return psum_butterfly(local_sum), side


def local(features, enc_in, enc_out, noise, in_weight, out_weight, probes):
    n = lax.axis_size("tensor")
    w_in = gather_dp(in_weight).reshape(n, -1, in_weight.shape[-1])
    w_out = gather_dp(out_weight).reshape(n, -1, out_weight.shape[-1])
    hidden = jax.nn.silu(jnp.dot(features, enc_in, preferred_element_type=jnp.float32)).astype(
        jnp.bfloat16
    )
    enc_out_p = enc_out.reshape(enc_out.shape[0], 2, n, -1)
    stats_p = jnp.einsum("bk,kmsc->sbmc", hidden, enc_out_p, preferred_element_type=jnp.float32)
    moments = reduce_scatter_pieces(stats_p)
    u_slice = (moments[:, 0] + jax.nn.softplus(moments[:, 1]) * noise.astype(jnp.float32)).astype(
        jnp.bfloat16
    )
    u_pieces = all_gather_pieces(u_slice)
    pre_act = jnp.einsum("sbc,sch->bh", u_pieces, w_in, preferred_element_type=jnp.float32)
    tanh_val = jnp.tanh(pre_act)
    squash = tanh_val.astype(jnp.bfloat16)
    slope = 1.0 - tanh_val * tanh_val
    branch_part = jnp.einsum("bh,sch->sbc", squash, w_out, preferred_element_type=jnp.float32)
    running, branch = series(probes, w_in, w_out, slope, branch_part)
    flowed = u_slice.astype(jnp.float32) + branch
    logdet = running / PROBES
    return (flowed, logdet)


def solution(mesh):
    in_specs = (
        P("dp", None),
        P(None, "tensor"),
        P("tensor", None),
        P("dp", "tensor"),
        P("dp", "tensor"),
        P("dp", "tensor"),
        P(None, "dp", None),
    )
    out_specs = (P("dp", "tensor"), P("dp"))
    return jax.shard_map(local, mesh=mesh, in_specs=in_specs, out_specs=out_specs, check_vma=False)
```

profile of v0, /device:TPU:0, one launch (start us, length us, event | category | flops | bytes accessed | tf_op | source)
XLA Modules:
  0.0 323.9 jit_solution(17380862790037617888)
XLA Ops:
  10.8 5.3 %convert_bitcast_fusion.2 = bf16[16,128,2,256]{3,1,0,2:T(8,128)(2,1)} fusion(bf16[128,2,16,256]{3,2,1,0:T(8,128)(2,1)} %bitcast.150, bf16[128,4096]{1,0:T(8,128)(2,1)S(1)} %copy-done, bf16[4096,128]{1,0:T(8,128)(2,1)} %param.14), kind=kOutput, calls=%fused_computation.17 | convolution fusion | flops 403783680 | bytes 6291456 | tf_op jit(solution)/shard_map/bk,kmsc->sbmc/dot_general | solution.py:98
  19.3 8.0 %all-to-all-start = ((bf16[16,128,2,256]{3,1,2,0:T(8,128)(2,1)}), bf16[16,128,2,256]{3,1,2,0:T(8,128)(2,1)}, u32[]{:S(2)}, u32[]{:S(2)}) async-start(bf16[16,128,2,256]{3,1,2,0:T(8,128)(2,1)} %copy.37), calls=%async_computation | async-start | bytes 4194304 | tf_op jit(solution)/shard_map/all_to_all | solution.py:44
  28.7 4.1 %copy.39 = bf16[2,128,4096]{1,2,0:T(8,128)(2,1)} copy(bf16[2,128,4096]{2,1,0:T(8,128)(2,1)} %param.19) | data formatting | bytes 4194304 | tf_op args[6]
  40.9 9.5 %collective-permute-done.7 = bf16[512,1024]{1,0:T(8,128)(2,1)S(1)} collective-permute-done((bf16[512,1024]{1,0:T(8,128)(2,1)}, bf16[512,1024]{1,0:T(8,128)(2,1)S(1)}, u32[]{:S(2)}, u32[]{:S(2)}) %collective-permute-start.7) | collective-permute-done | bytes 1048608 | tf_op jit(solution)/shard_map/ppermute | solution.py:23
  69.0 7.9 %all-to-all-start.1 = ((bf16[16,128,256]{2,1,0:T(8,128)(2,1)}), bf16[16,128,256]{2,1,0:T(8,128)(2,1)S(1)}, u32[]{:S(2)}, u32[]{:S(2)}) async-start(bf16[16,128,256]{2,1,0:T(8,128)(2,1)} %broadcast_in_dim.18), calls=%async_computation.1 | async-start | bytes 2097152 | tf_op jit(solution)/shard_map/all_to_all | solution.py:50
  85.9 8.1 %gather_fusion.2 = bf16[8,512,1024]{2,1,0:T(8,128)(2,1)} fusion(bf16[8,512,1024]{2,1,0:T(8,128)(2,1)} %bitcast_dynamic-update-slice_fusion.4, s32[1024]{0:T(1024)S(1)} %pad_clamp_fusion), kind=kCustom, calls=%fused_computation.clone | custom fusion | bytes 16777248 | tf_op jit(solution)/shard_map/jit(_take)/gather | solution.py:40
  98.2 8.0 %gather_fusion.3 = bf16[8,512,1024]{2,1,0:T(8,128)(2,1)} fusion(bf16[8,512,1024]{2,1,0:T(8,128)(2,1)} %bitcast_dynamic-update-slice_fusion, s32[1024]{0:T(1024)S(1)} %pad_clamp_fusion), kind=kCustom, calls=%fused_computation.1.clone | custom fusion | bytes 16777248 | tf_op jit(solution)/shard_map/jit(_take)/gather | solution.py:40
  106.3 11.7 %broadcast_select_fusion.1 = (bf16[8,512,1024]{2,1,0:T(8,128)(2,1)}, bf16[8,512,1024]{2,1,0:T(8,128)(2,1)}) fusion(bf16[8,512,1024]{2,1,0:T(8,128)(2,1)} %gather_fusion.2, pred[8]{0:T(512)(128)(4,1)S(1)} %get-tuple-element.8, bf16[8,512,1024]{2,1,0:T(8,128)(2,1)} %gather_fusion.3), kind=kLoop, calls=%fused_computation.5 | loop fusion | flops 8388608 | bytes 33554440 | tf_op jit(solution)/shard_map/jit(_take)/select_n | solution.py:40
  118.0 5.6 %multiply_subtract_fusion = (f32[128,1024]{1,0:T(8,128)}, bf16[128,1024]{1,0:T(8,128)(2,1)S(1)}) fusion(bf16[16,128,256]{2,1,0:T(8,128)(2,1)S(1)} %all-to-all-done.1, bf16[16,256,1024]{2,1,0:T(8,128)(2,1)} %bitcast.138), kind=kOutput, calls=%fused_computation.44 | convolution fusion | flops 1074135040 | bytes 10223616 | tf_op jit(solution)/shard_map/sbc,sch->bh/dot_general | solution.py:104
  124.8 5.9 %fusion.13 = bf16[2,128,1024,1]{1,2,0,3:T(8,128)(2,1)S(1)} fusion(bf16[16,256,1024,1]{2,1,0,3:T(8,128)(2,1)} %bitcast.139, bf16[2,128,16,256]{1,3,2,0:T(8,128)(2,1)S(1)} %bitcast.152, f32[128,1024]{0,1:T(8,128)S(1)} %copy.42), kind=kOutput, calls=%fused_computation.31 | convolution fusion | flops 2148007936 | bytes 11534336 | tf_op jit(solution)/shard_map/pbsc,sch->pbh/dot_general | solution.py:72
  130.8 7.1 %convert_bitcast_fusion = bf16[16,2,128,256]{2,3,1,0:T(8,128)(2,1)} fusion(bf16[16,256,1024,1]{2,1,3,0:T(8,128)(2,1)} %bitcast.146, bf16[2,128,1024,1]{1,2,0,3:T(8,128)(2,1)S(1)} %fusion.13), kind=kOutput, calls=%fused_computation.15 | convolution fusion | flops 2148532224 | bytes 11010048 | tf_op jit(solution)/shard_map/pbh,sch->spbc/dot_general | solution.py:74
  137.9 7.2 %all-to-all-start.3 = ((bf16[16,2,128,256]{2,3,1,0:T(8,128)(2,1)}), bf16[16,2,128,256]{2,3,1,0:T(8,128)(2,1)S(1)}, u32[]{:S(2)}, u32[]{:S(2)}) async-start(bf16[16,2,128,256]{2,3,1,0:T(8,128)(2,1)} %convert_bitcast_fusion), calls=%async_computation.3 | async-start | bytes 4194304 | tf_op jit(solution)/shard_map/all_to_all | solution.py:44
  145.2 5.9 %fusion.5 = bf16[16,1,128,256]{2,3,1,0:T(8,128)(2,1)S(1)} fusion(bf16[16,256,1024]{2,1,0:T(8,128)(2,1)} %bitcast.147, bf16[128,1024]{1,0:T(8,128)(2,1)S(1)} %get-tuple-element.13), kind=kOutput, calls=%fused_computation.19 | convolution fusion | flops 1074266112 | bytes 9699328 | tf_op jit(solution)/shard_map/bh,sch->sbc/dot_general | solution.py:108
  151.1 5.9 %fusion.14 = bf16[2,128,1024,1]{1,2,0,3:T(8,128)(2,1)S(1)} fusion(bf16[16,256,1024,1]{2,1,0,3:T(8,128)(2,1)} %bitcast.148, bf16[2,128,16,256]{1,3,2,0:T(8,128)(2,1)S(1)} %bitcast.153, f32[128,1024]{0,1:T(8,128)S(1)} %copy-done.9), kind=kOutput, calls=%fused_computation.32 | convolution fusion | flops 2148007936 | bytes 11534336 | tf_op jit(solution)/shard_map/pbsc,sch->pbh/dot_general | solution.py:66
  161.3 18.0 %all-to-all-done.3 = bf16[16,2,128,256]{2,3,1,0:T(8,128)(2,1)S(1)} async-done(((bf16[16,2,128,256]{2,3,1,0:T(8,128)(2,1)}), bf16[16,2,128,256]{2,3,1,0:T(8,128)(2,1)S(1)}, u32[]{:S(2)}, u32[]{:S(2)}) %all-to-all-start.3) | async-done | bytes 2097184 | tf_op jit(solution)/shard_map/all_to_all | solution.py:44
  179.3 4.5 %all-to-all-start.2 = ((bf16[16,3,128,256]{2,3,1,0:T(8,128)(2,1)}), bf16[16,3,128,256]{2,3,1,0:T(8,128)(2,1)}, u32[]{:S(2)}, u32[]{:S(2)}) async-start(bf16[16,3,128,256]{2,3,1,0:T(8,128)(2,1)} %pad_maximum_fusion), calls=%async_computation.2 | async-start | bytes 6291456 | tf_op jit(solution)/shard_map/all_to_all | solution.py:44
  184.0 46.8 %all-to-all-done.2 = bf16[16,3,128,256]{2,3,1,0:T(8,128)(2,1)} async-done(((bf16[16,3,128,256]{2,3,1,0:T(8,128)(2,1)}), bf16[16,3,128,256]{2,3,1,0:T(8,128)(2,1)}, u32[]{:S(2)}, u32[]{:S(2)}) %all-to-all-start.2) | async-done | bytes 3145760 | tf_op jit(solution)/shard_map/all_to_all | solution.py:44
  234.7 32.1 %all_to_all.30 = bf16[16,2,128,256]{3,2,1,0:T(8,128)(2,1)} all-to-all(bf16[16,2,128,256]{3,2,1,0:T(8,128)(2,1)S(1)} %broadcast_in_dim.21), channel_id=1, replica_groups=mesh['dp'=8,'tensor'=16] {'tensor'}, dimensions={0} | all-to-all | bytes 4194304 | tf_op jit(solution)/shard_map/all_to_all | solution.py:50
  268.6 4.0 %all-to-all-start.4 = ((bf16[16,2,128,256]{2,3,1,0:T(8,128)(2,1)}), bf16[16,2,128,256]{2,3,1,0:T(8,128)(2,1)S(1)}, u32[]{:S(2)}, u32[]{:S(2)}) async-start(bf16[16,2,128,256]{2,3,1,0:T(8,128)(2,1)} %broadcast_in_dim.20), calls=%async_computation.4 | async-start | bytes 4194304 | tf_op jit(solution)/shard_map/all_to_all | solution.py:50
  272.6 8.3 %fusion.15 = bf16[2,128,1024,1]{1,2,0,3:T(8,128)(2,1)} fusion(bf16[16,2,128,256]{3,2,1,0:T(8,128)(2,1)} %all_to_all.30, bf16[16,256,1024,1]{2,1,3,0:T(8,128)(2,1)} %bitcast.149, f32[128,1024]{0,1:T(8,128)} %copy-done.8), kind=kOutput, calls=%fused_computation.33 | convolution fusion | flops 2148007936 | bytes 11534336 | tf_op jit(solution)/shard_map/spbc,sch->pbh/dot_general | solution.py:81
  280.9 19.3 %all-to-all-done.4 = bf16[16,2,128,256]{2,3,1,0:T(8,128)(2,1)S(1)} async-done(((bf16[16,2,128,256]{2,3,1,0:T(8,128)(2,1)}), bf16[16,2,128,256]{2,3,1,0:T(8,128)(2,1)S(1)}, u32[]{:S(2)}, u32[]{:S(2)}) %all-to-all-start.4) | async-done | bytes 2097184 | tf_op jit(solution)/shard_map/all_to_all | solution.py:50
  300.2 5.8 %fusion = f32[128]{0:T(128)S(1)} fusion(bf16[16,2,128,256]{2,3,1,0:T(8,128)(2,1)S(1)} %all-to-all-done.4, bf16[16,256,1024,1]{2,1,3,0:T(8,128)(2,1)} %bitcast.140, bf16[2,128,1024,1]{1,2,0,3:T(8,128)(2,1)} %fusion.15), kind=kOutput, calls=%fused_computation.8 | convolution fusion | flops 2150629376 | bytes 11010560 | tf_op jit(solution)/shard_map/pbh,sch->spbc/dot_general | solution.py:83
  306.1 3.6 %collective-permute-done.12 = f32[128]{0:T(128)S(1)} collective-permute-done((f32[128]{0:T(128)S(1)}, f32[128]{0:T(128)S(1)}, u32[]{:S(2)}, u32[]{:S(2)}) %collective-permute-start.12) | collective-permute-done | bytes 544 | tf_op jit(solution)/shard_map/ppermute | solution.py:57
  309.6 5.1 %collective-permute-done.13 = f32[128]{0:T(128)S(1)} collective-permute-done((f32[128]{0:T(128)S(1)}, f32[128]{0:T(128)S(1)}, u32[]{:S(2)}, u32[]{:S(2)}) %collective-permute-start.13) | collective-permute-done | bytes 544 | tf_op jit(solution)/shard_map/ppermute | solution.py:57
  (104 shorter events, 75.2 us)
Async XLA Ops:
  0.6 54.7 %collective-permute-start = (bf16[512,1024]{1,0:T(8,128)(2,1)}, bf16[512,1024]{1,0:T(8,128)(2,1)}, u32[]{:S(2)}, u32[]{:S(2)}) collective-permute-start(bf16[512,1024]{1,0:T(8,128)(2,1)} %param.17), channel_id=1, source_target_pairs={{0,16},{16,0},{32,48},{48,32},{64,80},{80,64},{96,112},{112,96},{1... | collective-permute-start | bytes 3145736 | tf_op jit(solution)/shard_map/ppermute | solution.py:25
  0.7 35.5 %collective-permute-start.1 = (bf16[512,1024]{1,0:T(8,128)(2,1)}, bf16[512,1024]{1,0:T(8,128)(2,1)}, u32[]{:S(2)}, u32[]{:S(2)}) collective-permute-start(bf16[512,1024]{1,0:T(8,128)(2,1)} %param.17), channel_id=1, source_target_pairs={{0,32},{16,48},{32,64},{48,80},{64,96},{80,112},{96,0},{112,16},{1... | collective-permute-start | bytes 3145736 | tf_op jit(solution)/shard_map/ppermute | solution.py:23
  2.5 33.9 %collective-permute-start.2 = (bf16[512,1024]{1,0:T(8,128)(2,1)}, bf16[512,1024]{1,0:T(8,128)(2,1)}, u32[]{:S(2)}, u32[]{:S(2)}) collective-permute-start(bf16[512,1024]{1,0:T(8,128)(2,1)} %param.17), channel_id=1, source_target_pairs={{0,96},{16,112},{32,0},{48,16},{64,32},{80,48},{96,64},{112,80},{1... | collective-permute-start | bytes 3145736 | tf_op jit(solution)/shard_map/ppermute | solution.py:24
  4.0 46.3 %collective-permute-start.7 = (bf16[512,1024]{1,0:T(8,128)(2,1)}, bf16[512,1024]{1,0:T(8,128)(2,1)S(1)}, u32[]{:S(2)}, u32[]{:S(2)}) collective-permute-start(bf16[512,1024]{1,0:T(8,128)(2,1)} %param.18), channel_id=1, source_target_pairs={{0,32},{16,48},{32,64},{48,80},{64,96},{80,112},{96,0},{112,16},{1... | collective-permute-start | bytes 3145736 | tf_op jit(solution)/shard_map/ppermute | solution.py:23
  4.5 46.7 %collective-permute-start.8 = (bf16[512,1024]{1,0:T(8,128)(2,1)}, bf16[512,1024]{1,0:T(8,128)(2,1)S(1)}, u32[]{:S(2)}, u32[]{:S(2)}) collective-permute-start(bf16[512,1024]{1,0:T(8,128)(2,1)} %param.18), channel_id=1, source_target_pairs={{0,96},{16,112},{32,0},{48,16},{64,32},{80,48},{96,64},{112,80},{1... | collective-permute-start | bytes 3145736 | tf_op jit(solution)/shard_map/ppermute | solution.py:24
  10.8 17.3 %copy-start.2 = (s32[4]{0:T(128)S(1)}, s32[4]{0:T(128)}, u32[]{:S(2)}) copy-start(s32[4]{0:T(128)} %constant.116.clone) | copy-start | bytes 52
  16.1 16.8 %copy-start.6 = (bf16[512,1024]{1,0:T(8,128)(2,1)S(1)}, bf16[512,1024]{1,0:T(8,128)(2,1)}, u32[]{:S(2)}) copy-start(bf16[512,1024]{1,0:T(8,128)(2,1)} %param.17) | copy-start | bytes 3145732
  19.3 46.5 %all-to-all-start = ((bf16[16,128,2,256]{3,1,2,0:T(8,128)(2,1)}), bf16[16,128,2,256]{3,1,2,0:T(8,128)(2,1)}, u32[]{:S(2)}, u32[]{:S(2)}) async-start(bf16[16,128,2,256]{3,1,2,0:T(8,128)(2,1)} %copy.37), calls=%async_computation | async-start | bytes 4194304 | tf_op jit(solution)/shard_map/all_to_all | solution.py:44
  36.3 26.0 %collective-permute-start.6 = (bf16[512,1024]{1,0:T(8,128)(2,1)}, bf16[512,1024]{1,0:T(8,128)(2,1)S(1)}, u32[]{:S(2)}, u32[]{:S(2)}) collective-permute-start(bf16[512,1024]{1,0:T(8,128)(2,1)} %param.18), channel_id=1, source_target_pairs={{0,16},{16,0},{32,48},{48,32},{64,80},{80,64},{96,112},{112,96},{1... | collective-permute-start | bytes 3145736 | tf_op jit(solution)/shard_map/ppermute | solution.py:25
  37.7 27.6 %collective-permute-start.3 = (bf16[512,1024]{1,0:T(8,128)(2,1)S(1)}, bf16[512,1024]{1,0:T(8,128)(2,1)}, u32[]{:S(2)}, u32[]{:S(2)}) collective-permute-start(bf16[512,1024]{1,0:T(8,128)(2,1)S(1)} %broadcast_select_fusion.3), channel_id=1, source_target_pairs={{0,32},{16,112},{32,64},{48,16},{64,96},{80,48},{96,0},{112,80},{1... | collective-permute-start | bytes 3145736 | tf_op jit(solution)/shard_map/ppermute | solution.py:29
  50.4 31.4 %collective-permute-start.4 = (bf16[2,512,1024]{2,1,0:T(8,128)(2,1)}, bf16[2,512,1024]{2,1,0:T(8,128)(2,1)}, u32[]{:S(2)}, u32[]{:S(2)}) collective-permute-start(bf16[2,512,1024]{2,1,0:T(8,128)(2,1)} %pad_maximum_fusion.1), channel_id=1, source_target_pairs={{0,16},{16,0},{32,48},{48,32},{64,80},{80,64},{96,112},{112,96},{1... | collective-permute-start | bytes 6291464 | tf_op jit(solution)/shard_map/ppermute | solution.py:30
  52.3 24.6 %collective-permute-start.9 = (bf16[512,1024]{1,0:T(8,128)(2,1)}, bf16[512,1024]{1,0:T(8,128)(2,1)}, u32[]{:S(2)}, u32[]{:S(2)}) collective-permute-start(bf16[512,1024]{1,0:T(8,128)(2,1)} %broadcast_select_fusion.2), channel_id=1, source_target_pairs={{0,32},{16,112},{32,64},{48,16},{64,96},{80,48},{96,0},{112,80},{1... | collective-permute-start | bytes 3145736 | tf_op jit(solution)/shard_map/ppermute | solution.py:29
  55.4 38.6 %collective-permute-start.10 = (bf16[2,512,1024]{2,1,0:T(8,128)(2,1)}, bf16[2,512,1024]{2,1,0:T(8,128)(2,1)}, u32[]{:S(2)}, u32[]{:S(2)}) collective-permute-start(bf16[2,512,1024]{2,1,0:T(8,128)(2,1)} %pad_maximum_fusion.2), channel_id=1, source_target_pairs={{0,16},{16,0},{32,48},{48,32},{64,80},{80,64},{96,112},{112,96},{1... | collective-permute-start | bytes 6291464 | tf_op jit(solution)/shard_map/ppermute | solution.py:30
  65.4 19.5 %collective-permute-start.5 = (bf16[512,1024]{1,0:T(8,128)(2,1)}, bf16[512,1024]{1,0:T(8,128)(2,1)S(1)}, u32[]{:S(2)}, u32[]{:S(2)}) collective-permute-start(bf16[512,1024]{1,0:T(8,128)(2,1)} %collective-permute-done.3), channel_id=1, source_target_pairs={{0,16},{16,0},{32,48},{48,32},{64,80},{80,64},{96,112},{112,96},{1... | collective-permute-start | bytes 3145736 | tf_op jit(solution)/shard_map/ppermute | solution.py:31
  69.0 49.0 %all-to-all-start.1 = ((bf16[16,128,256]{2,1,0:T(8,128)(2,1)}), bf16[16,128,256]{2,1,0:T(8,128)(2,1)S(1)}, u32[]{:S(2)}, u32[]{:S(2)}) async-start(bf16[16,128,256]{2,1,0:T(8,128)(2,1)} %broadcast_in_dim.18), calls=%async_computation.1 | async-start | bytes 2097152 | tf_op jit(solution)/shard_map/all_to_all | solution.py:50
  76.9 20.2 %collective-permute-start.11 = (bf16[512,1024]{1,0:T(8,128)(2,1)}, bf16[512,1024]{1,0:T(8,128)(2,1)S(1)}, u32[]{:S(2)}, u32[]{:S(2)}) collective-permute-start(bf16[512,1024]{1,0:T(8,128)(2,1)} %collective-permute-done.9), channel_id=1, source_target_pairs={{0,16},{16,0},{32,48},{48,32},{64,80},{80,64},{96,112},{112,96},{1... | collective-permute-start | bytes 3145736 | tf_op jit(solution)/shard_map/ppermute | solution.py:31
  137.9 41.3 %all-to-all-start.3 = ((bf16[16,2,128,256]{2,3,1,0:T(8,128)(2,1)}), bf16[16,2,128,256]{2,3,1,0:T(8,128)(2,1)S(1)}, u32[]{:S(2)}, u32[]{:S(2)}) async-start(bf16[16,2,128,256]{2,3,1,0:T(8,128)(2,1)} %convert_bitcast_fusion), calls=%async_computation.3 | async-start | bytes 4194304 | tf_op jit(solution)/shard_map/all_to_all | solution.py:44
  179.3 51.6 %all-to-all-start.2 = ((bf16[16,3,128,256]{2,3,1,0:T(8,128)(2,1)}), bf16[16,3,128,256]{2,3,1,0:T(8,128)(2,1)}, u32[]{:S(2)}, u32[]{:S(2)}) async-start(bf16[16,3,128,256]{2,3,1,0:T(8,128)(2,1)} %pad_maximum_fusion), calls=%async_computation.2 | async-start | bytes 6291456 | tf_op jit(solution)/shard_map/all_to_all | solution.py:44
  268.6 31.6 %all-to-all-start.4 = ((bf16[16,2,128,256]{2,3,1,0:T(8,128)(2,1)}), bf16[16,2,128,256]{2,3,1,0:T(8,128)(2,1)S(1)}, u32[]{:S(2)}, u32[]{:S(2)}) async-start(bf16[16,2,128,256]{2,3,1,0:T(8,128)(2,1)} %broadcast_in_dim.20), calls=%async_computation.4 | async-start | bytes 4194304 | tf_op jit(solution)/shard_map/all_to_all | solution.py:50
  272.6 51.3 %copy-start.1 = (bf16[128,4096]{1,0:T(8,128)(2,1)S(1)}, bf16[128,4096]{1,0:T(8,128)(2,1)}, u32[]{:S(2)}) copy-start(bf16[128,4096]{1,0:T(8,128)(2,1)} %param.13) | copy-start | bytes 3145732
  306.0 3.6 %collective-permute-start.12 = (f32[128]{0:T(128)S(1)}, f32[128]{0:T(128)S(1)}, u32[]{:S(2)}, u32[]{:S(2)}) collective-permute-start(f32[128]{0:T(128)S(1)} %multiply_add_fusion), channel_id=1, source_target_pairs={{0,1},{1,0},{2,3},{3,2},{4,5},{5,4},{6,7},{7,6},{8,9},{9,8},{10,11... | collective-permute-start | bytes 1544 | tf_op jit(solution)/shard_map/ppermute | solution.py:57
  309.6 5.1 %collective-permute-start.13 = (f32[128]{0:T(128)S(1)}, f32[128]{0:T(128)S(1)}, u32[]{:S(2)}, u32[]{:S(2)}) collective-permute-start(f32[128]{0:T(128)S(1)} %add.98), channel_id=1, source_target_pairs={{0,2},{1,3},{2,0},{3,1},{4,6},{5,7},{6,4},{7,5},{8,10},{9,11},{10,... | collective-permute-start | bytes 1544 | tf_op jit(solution)/shard_map/ppermute | solution.py:57
  314.7 3.6 %collective-permute-start.14 = (f32[128]{0:T(128)S(1)}, f32[128]{0:T(128)S(1)}, u32[]{:S(2)}, u32[]{:S(2)}) collective-permute-start(f32[128]{0:T(128)S(1)} %add.99), channel_id=1, source_target_pairs={{0,4},{1,5},{2,6},{3,7},{4,0},{5,1},{6,2},{7,3},{8,12},{9,13},{10,... | collective-permute-start | bytes 1544 | tf_op jit(solution)/shard_map/ppermute | solution.py:57
  318.3 5.1 %collective-permute-start.15 = (f32[128]{0:T(128)S(1)}, f32[128]{0:T(128)S(1)}, u32[]{:S(2)}, u32[]{:S(2)}) collective-permute-start(f32[128]{0:T(128)S(1)} %add.100), channel_id=1, source_target_pairs={{0,8},{1,9},{2,10},{3,11},{4,12},{5,13},{6,14},{7,15},{8,0},{9,1},... | collective-permute-start | bytes 1544 | tf_op jit(solution)/shard_map/ppermute | solution.py:57
  (10 other events, 82.8 us)
where the time goes:
time: 325 us; the launch traced here: 324 us
  waiting for transfers between devices  109 us (34%)
  local copies, waits for them, and re-layouts  59.3 us (18%)
  matrix products  52.2 us (16%)
  starting transfers between devices  41.6 us (13%)
  blocking collectives  32.1 us (10%)
  other arithmetic  28.3 us (9%)
    all_to_all x3, waiting for transfers between devices, reduce_scatter_pieces(): received = lax.all_to_all(pieces.astype(jnp.bfloat16), 'tensor', 0, 0)  64.8 us
    all_to_all x1, blocking collectives, all_gather_pieces(): lax.all_to_all(jnp.broadcast_to(piece[None], (n,) + piece.shape), 'tensor...  32.1 us
    unnamed x41, local copies, waits for them, and re-layouts  31.9 us
    all_to_all x3, starting transfers between devices, reduce_scatter_pieces(): received = lax.all_to_all(pieces.astype(jnp.bfloat16), 'tensor', 0, 0)  19.7 us
    all_to_all x2, waiting for transfers between devices, all_gather_pieces(): lax.all_to_all(jnp.broadcast_to(piece[None], (n,) + piece.shape), 'tensor...  19.3 us
    gather x2, local copies, waits for them, and re-layouts, gather_dp(): return jnp.take(stacked, order, axis=0)  16.2 us
    ppermute x4, waiting for transfers between devices, psum_butterfly(): lax.ppermute(value, 'tensor', [(t, t ^ step) for t in range(n)])  14.8 us
    all_to_all x2, starting transfers between devices, all_gather_pieces(): lax.all_to_all(jnp.broadcast_to(piece[None], (n,) + piece.shape), 'tensor...  11.9 us
  transfers between devices with their start and end apart: 21, of which 9 were waited for; matrix products, arithmetic and copies ran while one was open for 33% of the time, Pallas kernels for 0%

commit v1 on v0

v1 whole, which is shorter than its diff:
```python
import jax
import jax.numpy as jnp
from jax import lax
from jax.sharding import PartitionSpec as P

L = 4096
PROBES = 2
TERMS = 3


def gather_dp(block):
    n = lax.axis_size("dp")
    ny = n // 2

    def perm(fn):
        return [(d, fn(d // 2, d % 2)) for d in range(n)]

    up = perm(lambda y, c: 2 * ((y + 1) % ny) + c)
    down = perm(lambda y, c: 2 * ((y - 1) % ny) + c)
    swap = perm(lambda y, c: 2 * y + 1 - c)
    fwd = perm(lambda y, c: 2 * ((y + 1) % ny) if c == 0 else 2 * ((y - 1) % ny) + 1)

    from_below = lax.ppermute(block, "dp", up)
    from_above = lax.ppermute(block, "dp", down)
    partner = lax.ppermute(block, "dp", swap)
    d = lax.axis_index("dp")
    y, c = d // 2, d % 2
    relay = jnp.where(c == 0, from_below, from_above)
    far = lax.ppermute(relay, "dp", fwd)
    partner_near = lax.ppermute(jnp.stack([from_below, from_above]), "dp", swap)
    partner_far = lax.ppermute(far, "dp", swap)
    joined = jnp.concatenate(
        [block, partner, from_below, from_above, far, partner_near[0], partner_near[1], partner_far]
    )
    rel_y = jnp.array([0, 0, -1, 1, 2, -1, 1, 2], jnp.int32)
    flip = jnp.array([0, 1, 0, 0, 0, 1, 1, 1], jnp.int32)
    block_ids = 2 * ((y + rel_y) % ny) + (c ^ flip)
    return joined, block_ids


def reduce_scatter_pieces(pieces):
    received = lax.all_to_all(pieces.astype(jnp.bfloat16), "tensor", 0, 0)
    return jnp.sum(received.astype(jnp.float32), axis=0)


def all_gather_pieces(piece):
    n = lax.axis_size("tensor")
    return lax.all_to_all(jnp.broadcast_to(piece[None], (n,) + piece.shape), "tensor", 0, 0)


def psum_groups(value):
    n = lax.axis_size("tensor")
    step = 1
    while step < n:
        others = [lax.ppermute(value, "tensor", [(t, t ^ (k * step)) for t in range(n)]) for k in (1, 2, 3)]
        value = (value + others[0]) + (others[1] + others[2])
        step *= 4
    return value


def series(start_p, w_in_p, w_out_p, slope, side):
    t = lax.axis_index("tensor")
    pulled = jnp.einsum("pbsc,sch->pbh", start_p, w_out_p, preferred_element_type=jnp.float32)
    scaled = (pulled * slope[None]).astype(jnp.bfloat16)
    part_u = jnp.einsum("pbh,sch->spbc", scaled, w_in_p, preferred_element_type=jnp.float32)
    pushed = jnp.einsum("pbsc,sch->pbh", start_p, w_in_p, preferred_element_type=jnp.float32)
    scaled_t = (pushed * slope[None]).astype(jnp.bfloat16)
    part_v = jnp.einsum("pbh,sch->spbc", scaled_t, w_out_p, preferred_element_type=jnp.float32)
    summed = reduce_scatter_pieces(jnp.concatenate([part_u, part_v, side[:, None]], axis=1))
    probes_n = start_p.shape[0]
    uv_here = summed[: 2 * probes_n].astype(jnp.bfloat16)
    side = summed[2 * probes_n]
    u_here = uv_here[:probes_n].astype(jnp.float32)
    v_here = uv_here[probes_n:].astype(jnp.float32)
    uv_pieces = all_gather_pieces(uv_here)
    start_here = lax.dynamic_index_in_dim(start_p, t, axis=2, keepdims=False).astype(jnp.float32)
    first = jnp.sum(start_here * u_here, axis=(0, 2))
    second = jnp.sum(v_here * u_here, axis=(0, 2))
    pulled3 = jnp.einsum(
        "spbc,sch->pbh", uv_pieces[:, :probes_n], w_out_p, preferred_element_type=jnp.float32
    )
    scaled3 = (pulled3 * slope[None]).astype(jnp.bfloat16)
    part3 = jnp.einsum("pbh,sch->spbc", scaled3, w_in_p, preferred_element_type=jnp.float32)
    third = jnp.sum(uv_pieces[:, probes_n:].astype(jnp.float32) * part3, axis=(0, 1, 3))
    coeffs = [(-1.0) ** k / (k + 1) for k in range(TERMS)]
    local_sum = coeffs[0] * first + coeffs[1] * second + coeffs[2] * third
    return psum_groups(local_sum), side


def local(features, enc_in, enc_out, noise, in_weight, out_weight, probes):
    n = lax.axis_size("tensor")
    w_in, block_ids = gather_dp(in_weight)
    w_out, _ = gather_dp(out_weight)
    w_in = w_in.reshape(n, -1, in_weight.shape[-1])
    w_out = w_out.reshape(n, -1, out_weight.shape[-1])
    halves = n // block_ids.shape[0]
    order = (halves * block_ids[:, None] + jnp.arange(halves)[None, :]).reshape(-1)
    back = jnp.argsort(order)
    hidden = jax.nn.silu(jnp.dot(features, enc_in, preferred_element_type=jnp.float32)).astype(
        jnp.bfloat16
    )
    enc_out_p = enc_out.reshape(enc_out.shape[0], 2, n, -1)
    stats_p = jnp.einsum("bk,kmsc->sbmc", hidden, enc_out_p, preferred_element_type=jnp.float32)
    moments = reduce_scatter_pieces(stats_p)
    u_slice = (moments[:, 0] + jax.nn.softplus(moments[:, 1]) * noise.astype(jnp.float32)).astype(
        jnp.bfloat16
    )
    u_pieces = jnp.take(all_gather_pieces(u_slice), order, axis=0, mode="clip")
    pre_act = jnp.einsum("sbc,sch->bh", u_pieces, w_in, preferred_element_type=jnp.float32)
    tanh_val = jnp.tanh(pre_act)
    squash = tanh_val.astype(jnp.bfloat16)
    slope = 1.0 - tanh_val * tanh_val
    branch_part = jnp.einsum("bh,sch->sbc", squash, w_out, preferred_element_type=jnp.float32)
    branch_part = jnp.take(branch_part, back, axis=0, mode="clip")
    start_p = probes.reshape(probes.shape[0], probes.shape[1], n, -1)
    start_p = jnp.take(start_p, order, axis=2, mode="clip")
    running, branch = series(start_p, w_in, w_out, slope, branch_part)
    flowed = u_slice.astype(jnp.float32) + branch
    logdet = running / PROBES
    return (flowed, logdet)


def solution(mesh):
    in_specs = (
        P("dp", None),
        P(None, "tensor"),
        P("tensor", None),
        P("dp", "tensor"),
        P("dp", "tensor"),
        P("dp", "tensor"),
        P(None, "dp", None),
    )
    out_specs = (P("dp", "tensor"), P("dp"))
    return jax.shard_map(local, mesh=mesh, in_specs=in_specs, out_specs=out_specs, check_vma=False)
```

time: 325 us -> 303 us (0.932)
  blocking collectives: 32.1 us -> 65.9 us
  waiting for transfers between devices: 109 us -> 79.9 us
  other arithmetic: 28.3 us -> 17.7 us
  local copies, waits for them, and re-layouts: 59.3 us -> 50.3 us
  matrix products: 52.2 us -> 46.4 us
    all_to_all x3 -> x1, waiting for transfers between devices: 64.8 us -> 0.01 us  [reduce_scatter_pieces(): received = lax.all_to_all(pieces.astype(jnp.bfloat16), 'tensor', 0, 0)]
    all_to_all x2, waiting for transfers between devices: 19.3 us -> 64.5 us  [all_gather_pieces(): lax.all_to_all(jnp.broadcast_to(piece[None], (n,) + piece.shape), 'tensor...]
    all_to_all x1, blocking collectives: 32.1 us -> 65.9 us  [reduce_scatter_pieces(): received = lax.all_to_all(pieces.astype(jnp.bfloat16), 'tensor', 0, 0)]
    all_to_all x3 -> x1, starting transfers between devices: 19.7 us -> 8.04 us  [reduce_scatter_pieces(): received = lax.all_to_all(pieces.astype(jnp.bfloat16), 'tensor', 0, 0)]
    select_n x2 -> x0, other arithmetic: 11.7 us -> none  [the longest x1 11.7 us: gather_dp(): return jnp.take(stacked, order, axis=0)]
    gather x4 -> x3, local copies, waits for them, and re-layouts: 17.4 us -> 5.85 us  [the longest x1 2.05 us: local(): start_p = jnp.take(start_p, order, axis=2, mode='clip')]
    ppermute x4 -> x6, waiting for transfers between devices: 14.8 us -> 5.17 us  [psum_groups(): lax.ppermute(value, 'tensor', [(t, t ^ k * step) for t in range(n)])]
    ppermute x4 -> x6, starting transfers between devices: 0.9 us -> 9.47 us  [psum_groups(): lax.ppermute(value, 'tensor', [(t, t ^ k * step) for t in range(n)])]
  transfers between devices with their start and end apart: 21 -> 21, of which waited for: 9 -> 7; matrix products, arithmetic and copies ran while one was open for 33% -> 21% of each run, Pallas kernels for 0% -> 0%
where the time goes in v1:
time: 303 us; the launch traced here: 302 us
  waiting for transfers between devices  79.9 us (26%)
  blocking collectives  65.9 us (22%)
  local copies, waits for them, and re-layouts  50.3 us (17%)
  matrix products  46.4 us (15%)
  starting transfers between devices  40.6 us (13%)
  other arithmetic  17.7 us (6%)
    all_to_all x1, blocking collectives, reduce_scatter_pieces(): received = lax.all_to_all(pieces.astype(jnp.bfloat16), 'tensor', 0, 0)  65.9 us
    all_to_all x2, waiting for transfers between devices, all_gather_pieces(): lax.all_to_all(jnp.broadcast_to(piece[None], (n,) + piece.shape), 'tensor...  64.5 us
    unnamed x36, local copies, waits for them, and re-layouts  33.4 us
    all_to_all x2, starting transfers between devices, all_gather_pieces(): lax.all_to_all(jnp.broadcast_to(piece[None], (n,) + piece.shape), 'tensor...  12.5 us
    ppermute x6, starting transfers between devices, psum_groups(): lax.ppermute(value, 'tensor', [(t, t ^ k * step) for t in range(n)])  9.47 us
    ppermute x2, waiting for transfers between devices, gather_dp(): from_below = lax.ppermute(block, 'dp', up)  9.28 us
    dot_general x1, matrix products, series(): jnp.einsum('pbh,sch->spbc', scaled, w_in_p, preferred_element_type=jnp.fl...  8.12 us
    all_to_all x1, starting transfers between devices, reduce_scatter_pieces(): received = lax.all_to_all(pieces.astype(jnp.bfloat16), 'tensor', 0, 0)  8.04 us
  transfers between devices with their start and end apart: 21, of which 7 were waited for; matrix products, arithmetic and copies ran while one was open for 21% of the time, Pallas kernels for 0%

profile of v1, /device:TPU:0, one launch (start us, length us, event | category | flops | bytes accessed | tf_op | source)
XLA Modules:
  0.0 301.8 jit_solution(14363086776114641038)
XLA Ops:
  4.0 3.5 %copy.39 = bf16[16,8,32,256]{3,2,1,0:T(8,128)(2,1)} copy(bf16[16,8,32,256]{3,1,2,0:T(8,128)(2,1)} %bitcast.148) | data formatting | bytes 4194304
  7.6 5.3 %convert_bitcast_fusion.2 = bf16[16,128,2,256]{3,1,0,2:T(8,128)(2,1)} fusion(bf16[128,2,16,256]{3,2,1,0:T(8,128)(2,1)} %bitcast.144, bf16[128,4096]{1,0:T(8,128)(2,1)S(1)} %copy-done, bf16[4096,128]{1,0:T(8,128)(2,1)} %param.10), kind=kOutput, calls=%fused_computation.18 | convolution fusion | flops 403783680 | bytes 6291456 | tf_op jit(solution)/shard_map/bk,kmsc->sbmc/dot_general | solution.py:103
  12.8 3.2 %copy.29 = bf16[16,128,2,256]{3,1,2,0:T(8,128)(2,1)} copy(bf16[16,128,2,256]{3,1,0,2:T(8,128)(2,1)} %convert_bitcast_fusion.2) | data formatting | bytes 4194304 | tf_op jit(solution)/shard_map/convert_element_type | solution.py:42
  16.0 8.0 %all-to-all-start = ((bf16[16,128,2,256]{3,1,2,0:T(8,128)(2,1)}), bf16[16,128,2,256]{3,1,2,0:T(8,128)(2,1)}, u32[]{:S(2)}, u32[]{:S(2)}) async-start(bf16[16,128,2,256]{3,1,2,0:T(8,128)(2,1)} %copy.29), calls=%async_computation | async-start | bytes 4194304 | tf_op jit(solution)/shard_map/all_to_all | solution.py:42
  24.5 2.9 collective-permute-start.8
  34.4 3.1 %broadcast_select_fusion.1 = (bf16[512,1024]{1,0:T(8,128)(2,1)}, bf16[4096,1024]{1,0:T(8,128)(2,1)}) fusion(bf16[512,1024]{1,0:T(8,128)(2,1)S(1)} %collective-permute-done.1, bf16[512,1024]{1,0:T(8,128)(2,1)} %collective-permute-done.2, pred[]{:T(512)S(6)} %eq.9, bf16[4096,1024]{1,0:T(8,128)(2,1)} %constant_dynamic-update-slice_fusion.3), kind=kLoop, calls=%fused_computation.44 | loop fusion | flops 524288 | bytes 4194305 | tf_op jit(solution)/shard_map/jit(_where)/select_n | solution.py:28
  37.5 2.8 pad_maximum_fusion.1
  41.1 9.3 %collective-permute-done.7 = bf16[512,1024]{1,0:T(8,128)(2,1)S(1)} collective-permute-done((bf16[512,1024]{1,0:T(8,128)(2,1)}, bf16[512,1024]{1,0:T(8,128)(2,1)S(1)}, u32[]{:S(2)}, u32[]{:S(2)}) %collective-permute-start.7) | collective-permute-done | bytes 1048608 | tf_op jit(solution)/shard_map/ppermute | solution.py:23
  54.4 3.2 %copy-done.5 = bf16[4096,1024]{1,0:T(8,128)(2,1)} copy-done((bf16[4096,1024]{1,0:T(8,128)(2,1)}, bf16[4096,1024]{1,0:T(8,128)(2,1)S(1)}, u32[]{:S(2)}) %copy-start.5) | copy-done | bytes 8388632
  62.3 7.9 %all-to-all-start.1 = ((bf16[16,128,256]{2,1,0:T(8,128)(2,1)}), bf16[16,128,256]{2,1,0:T(8,128)(2,1)}, u32[]{:S(2)}, u32[]{:S(2)}) async-start(bf16[16,128,256]{2,1,0:T(8,128)(2,1)} %broadcast_in_dim.15), calls=%async_computation.1 | async-start | bytes 2097152 | tf_op jit(solution)/shard_map/all_to_all | solution.py:48
  70.4 4.1 %copy.30 = bf16[2,128,4096]{1,2,0:T(8,128)(2,1)} copy(bf16[2,128,4096]{2,1,0:T(8,128)(2,1)} %param.15) | data formatting | bytes 4194304 | tf_op args[6]
  74.5 2.9 copy.31
  86.9 4.1 %all-to-all-done.1 = bf16[16,128,256]{2,1,0:T(8,128)(2,1)} async-done(((bf16[16,128,256]{2,1,0:T(8,128)(2,1)}), bf16[16,128,256]{2,1,0:T(8,128)(2,1)}, u32[]{:S(2)}, u32[]{:S(2)}) %all-to-all-start.1) | async-done | bytes 1048608 | tf_op jit(solution)/shard_map/all_to_all | solution.py:48
  103.0 4.8 %multiply_subtract_fusion = (f32[128,1024]{1,0:T(8,128)S(1)}, bf16[128,1024]{1,0:T(8,128)(2,1)S(1)}) fusion(bf16[16,128,256]{2,1,0:T(8,128)(2,1)S(1)} %gather_fusion.1, bf16[16,256,1024]{2,1,0:T(8,128)(2,1)} %bitcast.9), kind=kOutput, calls=%fused_computation.45 | convolution fusion | flops 1074135040 | bytes 10223616 | tf_op jit(solution)/shard_map/sbc,sch->bh/dot_general | solution.py:109
  112.0 5.8 %fusion.34 = bf16[2,128,1024,1]{2,1,0,3:T(8,128)(2,1)S(1)} fusion(bf16[16,256,1024,1]{2,1,3,0:T(8,128)(2,1)} %bitcast.11, bf16[16,2,128,256]{3,2,1,0:T(8,128)(2,1)S(1)} %copy-done.2, f32[128,1024]{1,0:T(8,128)S(1)} %get-tuple-element.12), kind=kOutput, calls=%fused_computation.33 | convolution fusion | flops 2148007936 | bytes 11534336 | tf_op jit(solution)/shard_map/pbsc,sch->pbh/dot_general | solution.py:66
  117.8 8.1 %convert_bitcast_fusion.1 = bf16[16,2,128,256]{2,3,1,0:T(8,128)(2,1)S(1)} fusion(bf16[16,256,1024,1]{2,1,3,0:T(8,128)(2,1)} %bitcast.11, bf16[2,128,1024,1]{2,1,0,3:T(8,128)(2,1)S(1)} %fusion.31), kind=kOutput, calls=%fused_computation.17 | convolution fusion | flops 2148532224 | bytes 11010048 | tf_op jit(solution)/shard_map/pbh,sch->spbc/dot_general | solution.py:65
  125.9 3.6 %convert_bitcast_fusion = bf16[16,2,128,256]{2,3,1,0:T(8,128)(2,1)} fusion(bf16[16,256,1024,1]{2,1,3,0:T(8,128)(2,1)S(1)} %bitcast.150, bf16[2,128,1024,1]{2,1,0,3:T(8,128)(2,1)S(1)} %fusion.34), kind=kOutput, calls=%fused_computation.16 | convolution fusion | flops 2148532224 | bytes 11010048 | tf_op jit(solution)/shard_map/pbh,sch->spbc/dot_general | solution.py:68
  129.6 3.3 %convolution_bitcast_fusion = bf16[16,128,256]{1,2,0:T(8,128)(2,1)} fusion(bf16[16,256,1024]{2,1,0:T(8,128)(2,1)S(1)} %bitcast.151, bf16[128,1024]{1,0:T(8,128)(2,1)S(1)} %get-tuple-element.13), kind=kOutput, calls=%fused_computation.19 | convolution fusion | flops 1073741824 | bytes 9699328 | tf_op jit(solution)/shard_map/bh,sch->sbc/dot_general | solution.py:113
  137.1 65.9 %all_to_all.20 = bf16[16,5,128,256]{2,3,1,0:T(8,128)(2,1)S(1)} all-to-all(bf16[16,5,128,256]{2,3,1,0:T(8,128)(2,1)S(1)} %pad_maximum_fusion), channel_id=1, replica_groups=mesh['dp'=8,'tensor'=16] {'tensor'}, dimensions={0} | all-to-all | bytes 10485760 | tf_op jit(solution)/shard_map/all_to_all | solution.py:42
  206.8 4.5 %all-to-all-start.3 = ((bf16[16,4,128,256]{3,2,1,0:T(8,128)(2,1)}), bf16[16,4,128,256]{3,2,1,0:T(8,128)(2,1)}, u32[]{:S(2)}, u32[]{:S(2)}) async-start(bf16[16,4,128,256]{3,2,1,0:T(8,128)(2,1)} %broadcast_in_dim.18), calls=%async_computation.3 | async-start | bytes 8388608 | tf_op jit(solution)/shard_map/all_to_all | solution.py:48
  212.4 60.5 %all-to-all-done.3 = bf16[16,4,128,256]{3,2,1,0:T(8,128)(2,1)} async-done(((bf16[16,4,128,256]{3,2,1,0:T(8,128)(2,1)}), bf16[16,4,128,256]{3,2,1,0:T(8,128)(2,1)}, u32[]{:S(2)}, u32[]{:S(2)}) %all-to-all-start.3) | async-done | bytes 4194336 | tf_op jit(solution)/shard_map/all_to_all | solution.py:48
  272.9 6.4 %fusion.30 = bf16[2,128,1024,1]{2,1,0,3:T(8,128)(2,1)S(1)} fusion(bf16[16,4,128,256]{3,2,1,0:T(8,128)(2,1)} %all-to-all-done.3, bf16[16,256,1024,1]{2,1,3,0:T(8,128)(2,1)} %bitcast.152, f32[128,1024]{1,0:T(8,128)S(1)} %copy-done.4), kind=kOutput, calls=%fused_computation.31 | convolution fusion | flops 2148007936 | bytes 13631488 | tf_op jit(solution)/shard_map/spbc,sch->pbh/dot_general | solution.py:79
  279.4 6.6 %fusion = f32[128]{0:T(128)S(1)} fusion(bf16[16,256,1024,1]{2,1,3,0:T(8,128)(2,1)} %bitcast.11, bf16[2,128,1024,1]{2,1,0,3:T(8,128)(2,1)S(1)} %fusion.30, bf16[16,4,128,256]{3,2,1,0:T(8,128)(2,1)} %all-to-all-done.3), kind=kOutput, calls=%fused_computation.6 | convolution fusion | flops 2150629376 | bytes 11010560 | tf_op jit(solution)/shard_map/pbh,sch->spbc/dot_general | solution.py:83
  293.4 3.1 %collective-permute-start.16 = (f32[128]{0:T(128)S(1)}, f32[128]{0:T(128)S(1)}, u32[]{:S(2)}, u32[]{:S(2)}) collective-permute-start(f32[128]{0:T(128)S(1)} %add_add_fusion), channel_id=1, source_target_pairs={{0,8},{1,9},{2,10},{3,11},{4,12},{5,13},{6,14},{7,15},{8,0},{9,1},... | collective-permute-start | bytes 1544 | tf_op jit(solution)/shard_map/ppermute | solution.py:55
  (96 shorter events, 67.9 us)
Async XLA Ops:
  0.6 29.1 %collective-permute-start = (bf16[512,1024]{1,0:T(8,128)(2,1)}, bf16[512,1024]{1,0:T(8,128)(2,1)}, u32[]{:S(2)}, u32[]{:S(2)}) collective-permute-start(bf16[512,1024]{1,0:T(8,128)(2,1)} %param.13), channel_id=1, source_target_pairs={{0,16},{16,0},{32,48},{48,32},{64,80},{80,64},{96,112},{112,96},{1... | collective-permute-start | bytes 3145736 | tf_op jit(solution)/shard_map/ppermute | solution.py:25
  0.7 32.6 %collective-permute-start.1 = (bf16[512,1024]{1,0:T(8,128)(2,1)}, bf16[512,1024]{1,0:T(8,128)(2,1)S(1)}, u32[]{:S(2)}, u32[]{:S(2)}) collective-permute-start(bf16[512,1024]{1,0:T(8,128)(2,1)} %param.13), channel_id=1, source_target_pairs={{0,32},{16,48},{32,64},{48,80},{64,96},{80,112},{96,0},{112,16},{1... | collective-permute-start | bytes 3145736 | tf_op jit(solution)/shard_map/ppermute | solution.py:23
  2.5 31.9 %collective-permute-start.2 = (bf16[512,1024]{1,0:T(8,128)(2,1)}, bf16[512,1024]{1,0:T(8,128)(2,1)}, u32[]{:S(2)}, u32[]{:S(2)}) collective-permute-start(bf16[512,1024]{1,0:T(8,128)(2,1)} %param.13), channel_id=1, source_target_pairs={{0,96},{16,112},{32,0},{48,16},{64,32},{80,48},{96,64},{112,80},{1... | collective-permute-start | bytes 3145736 | tf_op jit(solution)/shard_map/ppermute | solution.py:24
  16.0 43.1 %all-to-all-start = ((bf16[16,128,2,256]{3,1,2,0:T(8,128)(2,1)}), bf16[16,128,2,256]{3,1,2,0:T(8,128)(2,1)}, u32[]{:S(2)}, u32[]{:S(2)}) async-start(bf16[16,128,2,256]{3,1,2,0:T(8,128)(2,1)} %copy.29), calls=%async_computation | async-start | bytes 4194304 | tf_op jit(solution)/shard_map/all_to_all | solution.py:42
  24.1 26.3 %collective-permute-start.7 = (bf16[512,1024]{1,0:T(8,128)(2,1)}, bf16[512,1024]{1,0:T(8,128)(2,1)S(1)}, u32[]{:S(2)}, u32[]{:S(2)}) collective-permute-start(bf16[512,1024]{1,0:T(8,128)(2,1)} %param.14), channel_id=1, source_target_pairs={{0,32},{16,48},{32,64},{48,80},{64,96},{80,112},{96,0},{112,16},{1... | collective-permute-start | bytes 3145736 | tf_op jit(solution)/shard_map/ppermute | solution.py:23
  24.5 26.7 %collective-permute-start.8 = (bf16[512,1024]{1,0:T(8,128)(2,1)}, bf16[512,1024]{1,0:T(8,128)(2,1)S(1)}, u32[]{:S(2)}, u32[]{:S(2)}) collective-permute-start(bf16[512,1024]{1,0:T(8,128)(2,1)} %param.14), channel_id=1, source_target_pairs={{0,96},{16,112},{32,0},{48,16},{64,32},{80,48},{96,64},{112,80},{1... | collective-permute-start | bytes 3145736 | tf_op jit(solution)/shard_map/ppermute | solution.py:24
  29.7 23.0 %collective-permute-start.6 = (bf16[512,1024]{1,0:T(8,128)(2,1)}, bf16[512,1024]{1,0:T(8,128)(2,1)S(1)}, u32[]{:S(2)}, u32[]{:S(2)}) collective-permute-start(bf16[512,1024]{1,0:T(8,128)(2,1)} %param.14), channel_id=1, source_target_pairs={{0,16},{16,0},{32,48},{48,32},{64,80},{80,64},{96,112},{112,96},{1... | collective-permute-start | bytes 3145736 | tf_op jit(solution)/shard_map/ppermute | solution.py:25
  37.5 43.2 %collective-permute-start.3 = (bf16[512,1024]{1,0:T(8,128)(2,1)}, bf16[512,1024]{1,0:T(8,128)(2,1)}, u32[]{:S(2)}, u32[]{:S(2)}) collective-permute-start(bf16[512,1024]{1,0:T(8,128)(2,1)} %get-tuple-element.8), channel_id=1, source_target_pairs={{0,32},{16,112},{32,64},{48,16},{64,96},{80,48},{96,0},{112,80},{1... | collective-permute-start | bytes 3145736 | tf_op jit(solution)/shard_map/ppermute | solution.py:29
  40.3 20.8 %copy-start.8 = (bf16[128,256]{1,0:T(8,128)(2,1)S(1)}, bf16[128,256]{1,0:T(8,128)(2,1)}, u32[]{:S(2)}) copy-start(bf16[128,256]{1,0:T(8,128)(2,1)} %param.12) | copy-start | bytes 196612
  40.3 52.6 %collective-permute-start.4 = (bf16[2,512,1024]{2,1,0:T(8,128)(2,1)}, bf16[2,512,1024]{2,1,0:T(8,128)(2,1)}, u32[]{:S(2)}, u32[]{:S(2)}) collective-permute-start(bf16[2,512,1024]{2,1,0:T(8,128)(2,1)} %pad_maximum_fusion.1), channel_id=1, source_target_pairs={{0,16},{16,0},{32,48},{48,32},{64,80},{80,64},{96,112},{112,96},{1... | collective-permute-start | bytes 6291464 | tf_op jit(solution)/shard_map/ppermute | solution.py:30
  52.8 44.6 %collective-permute-start.10 = (bf16[2,512,1024]{2,1,0:T(8,128)(2,1)}, bf16[2,512,1024]{2,1,0:T(8,128)(2,1)}, u32[]{:S(2)}, u32[]{:S(2)}) collective-permute-start(bf16[2,512,1024]{2,1,0:T(8,128)(2,1)} %pad_maximum_fusion.2), channel_id=1, source_target_pairs={{0,16},{16,0},{32,48},{48,32},{64,80},{80,64},{96,112},{112,96},{1... | collective-permute-start | bytes 6291464 | tf_op jit(solution)/shard_map/ppermute | solution.py:30
  57.6 24.4 %collective-permute-start.9 = (bf16[512,1024]{1,0:T(8,128)(2,1)}, bf16[512,1024]{1,0:T(8,128)(2,1)}, u32[]{:S(2)}, u32[]{:S(2)}) collective-permute-start(bf16[512,1024]{1,0:T(8,128)(2,1)} %get-tuple-element.10), channel_id=1, source_target_pairs={{0,32},{16,112},{32,64},{48,16},{64,96},{80,48},{96,0},{112,80},{1... | collective-permute-start | bytes 3145736 | tf_op jit(solution)/shard_map/ppermute | solution.py:29
  62.3 28.7 %all-to-all-start.1 = ((bf16[16,128,256]{2,1,0:T(8,128)(2,1)}), bf16[16,128,256]{2,1,0:T(8,128)(2,1)}, u32[]{:S(2)}, u32[]{:S(2)}) async-start(bf16[16,128,256]{2,1,0:T(8,128)(2,1)} %broadcast_in_dim.15), calls=%async_computation.1 | async-start | bytes 2097152 | tf_op jit(solution)/shard_map/all_to_all | solution.py:48
  80.7 19.0 %collective-permute-start.5 = (bf16[512,1024]{1,0:T(8,128)(2,1)}, bf16[512,1024]{1,0:T(8,128)(2,1)S(1)}, u32[]{:S(2)}, u32[]{:S(2)}) collective-permute-start(bf16[512,1024]{1,0:T(8,128)(2,1)} %collective-permute-done.3), channel_id=1, source_target_pairs={{0,16},{16,0},{32,48},{48,32},{64,80},{80,64},{96,112},{112,96},{1... | collective-permute-start | bytes 3145736 | tf_op jit(solution)/shard_map/ppermute | solution.py:31
  82.0 25.8 %collective-permute-start.11 = (bf16[512,1024]{1,0:T(8,128)(2,1)}, bf16[512,1024]{1,0:T(8,128)(2,1)S(1)}, u32[]{:S(2)}, u32[]{:S(2)}) collective-permute-start(bf16[512,1024]{1,0:T(8,128)(2,1)} %collective-permute-done.9), channel_id=1, source_target_pairs={{0,16},{16,0},{32,48},{48,32},{64,80},{80,64},{96,112},{112,96},{1... | collective-permute-start | bytes 3145736 | tf_op jit(solution)/shard_map/ppermute | solution.py:31
  204.0 68.9 %copy-start.4 = (f32[128,1024]{1,0:T(8,128)S(1)}, f32[128,1024]{1,0:T(8,128)}, u32[]{:S(2)}) copy-start(f32[128,1024]{1,0:T(8,128)} %copy-done.3) | copy-start | bytes 1572868
  206.8 66.1 %all-to-all-start.3 = ((bf16[16,4,128,256]{3,2,1,0:T(8,128)(2,1)}), bf16[16,4,128,256]{3,2,1,0:T(8,128)(2,1)}, u32[]{:S(2)}, u32[]{:S(2)}) async-start(bf16[16,4,128,256]{3,2,1,0:T(8,128)(2,1)} %broadcast_in_dim.18), calls=%async_computation.3 | async-start | bytes 8388608 | tf_op jit(solution)/shard_map/all_to_all | solution.py:48
  272.9 28.9 %copy-start.1 = (bf16[128,4096]{1,0:T(8,128)(2,1)S(1)}, bf16[128,4096]{1,0:T(8,128)(2,1)}, u32[]{:S(2)}) copy-start(bf16[128,4096]{1,0:T(8,128)(2,1)} %param.9) | copy-start | bytes 3145732
  285.9 4.8 %collective-permute-start.12 = (f32[128]{0:T(128)S(1)}, f32[128]{0:T(128)S(1)}, u32[]{:S(2)}, u32[]{:S(2)}) collective-permute-start(f32[128]{0:T(128)S(1)} %multiply_add_fusion), channel_id=1, source_target_pairs={{0,1},{1,0},{2,3},{3,2},{4,5},{5,4},{6,7},{7,6},{8,9},{9,8},{10,11... | collective-permute-start | bytes 1544 | tf_op jit(solution)/shard_map/ppermute | solution.py:55
  286.0 5.2 %collective-permute-start.13 = (f32[128]{0:T(128)S(1)}, f32[128]{0:T(128)S(1)}, u32[]{:S(2)}, u32[]{:S(2)}) collective-permute-start(f32[128]{0:T(128)S(1)} %multiply_add_fusion), channel_id=1, source_target_pairs={{0,2},{1,3},{2,0},{3,1},{4,6},{5,7},{6,4},{7,5},{8,10},{9,11},{10,... | collective-permute-start | bytes 1544 | tf_op jit(solution)/shard_map/ppermute | solution.py:55
  288.6 4.8 %collective-permute-start.14 = (f32[128]{0:T(128)S(1)}, f32[128]{0:T(128)S(1)}, u32[]{:S(2)}, u32[]{:S(2)}) collective-permute-start(f32[128]{0:T(128)S(1)} %multiply_add_fusion), channel_id=1, source_target_pairs={{0,3},{1,2},{2,1},{3,0},{4,7},{5,6},{6,5},{7,4},{8,11},{9,10},{10,... | collective-permute-start | bytes 1544 | tf_op jit(solution)/shard_map/ppermute | solution.py:55
  293.4 5.4 %collective-permute-start.15 = (f32[128]{0:T(128)S(1)}, f32[128]{0:T(128)S(1)}, u32[]{:S(2)}, u32[]{:S(2)}) collective-permute-start(f32[128]{0:T(128)S(1)} %add_add_fusion), channel_id=1, source_target_pairs={{0,4},{1,5},{2,6},{3,7},{4,0},{5,1},{6,2},{7,3},{8,12},{9,13},{10,... | collective-permute-start | bytes 1544 | tf_op jit(solution)/shard_map/ppermute | solution.py:55
  293.4 5.4 %collective-permute-start.16 = (f32[128]{0:T(128)S(1)}, f32[128]{0:T(128)S(1)}, u32[]{:S(2)}, u32[]{:S(2)}) collective-permute-start(f32[128]{0:T(128)S(1)} %add_add_fusion), channel_id=1, source_target_pairs={{0,8},{1,9},{2,10},{3,11},{4,12},{5,13},{6,14},{7,15},{8,0},{9,1},... | collective-permute-start | bytes 1544 | tf_op jit(solution)/shard_map/ppermute | solution.py:55
  296.5 4.8 %collective-permute-start.17 = (f32[128]{0:T(128)S(1)}, f32[128]{0:T(128)S(1)}, u32[]{:S(2)}, u32[]{:S(2)}) collective-permute-start(f32[128]{0:T(128)S(1)} %add_add_fusion), channel_id=1, source_target_pairs={{0,12},{1,13},{2,14},{3,15},{4,8},{5,9},{6,10},{7,11},{8,4},{9,5},... | collective-permute-start | bytes 1544 | tf_op jit(solution)/shard_map/ppermute | solution.py:55
  (8 other events, 85.4 us)

commit v2 on v1

--- a/solution.py
+++ b/solution.py
@@ -58,12 +58,15 @@
     return value
 
 
-def series(start_p, w_in_p, w_out_p, slope, side):
+def series(start_p, order, w_in_p, w_out_p, slope, side):
     t = lax.axis_index("tensor")
+    back = jnp.argsort(order)
+    start_in = jnp.take(start_p, order, axis=2, mode="clip")
     pulled = jnp.einsum("pbsc,sch->pbh", start_p, w_out_p, preferred_element_type=jnp.float32)
     scaled = (pulled * slope[None]).astype(jnp.bfloat16)
     part_u = jnp.einsum("pbh,sch->spbc", scaled, w_in_p, preferred_element_type=jnp.float32)
-    pushed = jnp.einsum("pbsc,sch->pbh", start_p, w_in_p, preferred_element_type=jnp.float32)
+    part_u = jnp.take(part_u, back, axis=0, mode="clip")
+    pushed = jnp.einsum("pbsc,sch->pbh", start_in, w_in_p, preferred_element_type=jnp.float32)
     scaled_t = (pushed * slope[None]).astype(jnp.bfloat16)
     part_v = jnp.einsum("pbh,sch->spbc", scaled_t, w_out_p, preferred_element_type=jnp.float32)
     summed = reduce_scatter_pieces(jnp.concatenate([part_u, part_v, side[:, None]], axis=1))
@@ -81,7 +84,8 @@
     )
     scaled3 = (pulled3 * slope[None]).astype(jnp.bfloat16)
     part3 = jnp.einsum("pbh,sch->spbc", scaled3, w_in_p, preferred_element_type=jnp.float32)
-    third = jnp.sum(uv_pieces[:, probes_n:].astype(jnp.float32) * part3, axis=(0, 1, 3))
+    v_in = jnp.take(uv_pieces[:, probes_n:], order, axis=0, mode="clip")
+    third = jnp.sum(v_in.astype(jnp.float32) * part3, axis=(0, 1, 3))
     coeffs = [(-1.0) ** k / (k + 1) for k in range(TERMS)]
     local_sum = coeffs[0] * first + coeffs[1] * second + coeffs[2] * third
     return psum_groups(local_sum), side
@@ -90,12 +94,10 @@
 def local(features, enc_in, enc_out, noise, in_weight, out_weight, probes):
     n = lax.axis_size("tensor")
     w_in, block_ids = gather_dp(in_weight)
-    w_out, _ = gather_dp(out_weight)
     w_in = w_in.reshape(n, -1, in_weight.shape[-1])
-    w_out = w_out.reshape(n, -1, out_weight.shape[-1])
+    w_out = lax.all_gather(out_weight, "dp", axis=0, tiled=True).reshape(n, -1, out_weight.shape[-1])
     halves = n // block_ids.shape[0]
     order = (halves * block_ids[:, None] + jnp.arange(halves)[None, :]).reshape(-1)
-    back = jnp.argsort(order)
     hidden = jax.nn.silu(jnp.dot(features, enc_in, preferred_element_type=jnp.float32)).astype(
         jnp.bfloat16
     )
@@ -111,10 +113,8 @@
     squash = tanh_val.astype(jnp.bfloat16)
     slope = 1.0 - tanh_val * tanh_val
     branch_part = jnp.einsum("bh,sch->sbc", squash, w_out, preferred_element_type=jnp.float32)
-    branch_part = jnp.take(branch_part, back, axis=0, mode="clip")
     start_p = probes.reshape(probes.shape[0], probes.shape[1], n, -1)
-    start_p = jnp.take(start_p, order, axis=2, mode="clip")
-    running, branch = series(start_p, w_in, w_out, slope, branch_part)
+    running, branch = series(start_p, order, w_in, w_out, slope, branch_part)
     flowed = u_slice.astype(jnp.float32) + branch
     logdet = running / PROBES
     return (flowed, logdet)

time: 303 us -> 331 us (1.092)
  waiting for transfers between devices: 79.9 us -> 99.9 us
  between operations: 0.95 us -> 14.4 us
  matrix products: 46.4 us -> 59.7 us
  starting transfers between devices: 40.6 us -> 29.9 us
  other arithmetic: 17.7 us -> 9.42 us
  blocking collectives: 65.9 us -> 70.7 us
  local copies, waits for them, and re-layouts: 50.3 us -> 45.8 us
    unnamed x36 -> x33, local copies, waits for them, and re-layouts: 33.4 us -> 18.9 us
    ppermute x2 -> x1, waiting for transfers between devices: 0.01 us -> 9.88 us  [gather_dp(): far = lax.ppermute(relay, 'dp', fwd)]
    all_to_all x1, waiting for transfers between devices: 0.01 us -> 9.42 us  [reduce_scatter_pieces(): received = lax.all_to_all(pieces.astype(jnp.bfloat16), 'tensor', 0, 0)]
    gather x2 -> x4, local copies, waits for them, and re-layouts: 4.02 us -> 10.6 us  [the longest x2 4.74 us: series(): v_in = jnp.take(uv_pieces[:, probes_n:], order, axis=0, mode='clip')]
    all_to_all x1, blocking collectives: 65.9 us -> 70.7 us  [reduce_scatter_pieces(): received = lax.all_to_all(pieces.astype(jnp.bfloat16), 'tensor', 0, 0)]
    dot_general x1, matrix products: 3.64 us -> 8.32 us  [series(): jnp.einsum('pbh,sch->spbc', scaled_t, w_out_p, preferred_element_type=jnp...]
    all_to_all x2, starting transfers between devices: 12.5 us -> 8.87 us  [all_gather_pieces(): lax.all_to_all(jnp.broadcast_to(piece[None], (n,) + piece.shape), 'tensor...]
    dot_general x1, matrix products: 2.41 us -> 5.79 us  [series(): jnp.einsum('pbsc,sch->pbh', start_p, w_out_p, preferred_element_type=jnp....]
  transfers between devices with their start and end apart: 21 -> 16, of which waited for: 7 -> 9; matrix products, arithmetic and copies ran while one was open for 21% -> 16% of each run, Pallas kernels for 0% -> 0%
where the time goes in v2:
time: 331 us; the launch traced here: 330 us
  waiting for transfers between devices  99.9 us (30%)
  blocking collectives  70.7 us (21%)
  matrix products  59.7 us (18%)
  local copies, waits for them, and re-layouts  45.8 us (14%)
  starting transfers between devices  29.9 us (9%)
  between operations  14.4 us (4%)
  other arithmetic  9.42 us (3%)
    all_to_all x1, blocking collectives, reduce_scatter_pieces(): received = lax.all_to_all(pieces.astype(jnp.bfloat16), 'tensor', 0, 0)  70.7 us
    all_to_all x2, waiting for transfers between devices, all_gather_pieces(): lax.all_to_all(jnp.broadcast_to(piece[None], (n,) + piece.shape), 'tensor...  61.4 us
    unnamed x33, local copies, waits for them, and re-layouts  18.9 us
    ppermute x1, waiting for transfers between devices, gather_dp(): from_below = lax.ppermute(block, 'dp', up)  10.6 us
    ppermute x1, waiting for transfers between devices, gather_dp(): far = lax.ppermute(relay, 'dp', fwd)  9.88 us
    all_to_all x1, waiting for transfers between devices, reduce_scatter_pieces(): received = lax.all_to_all(pieces.astype(jnp.bfloat16), 'tensor', 0, 0)  9.42 us
    dot_general x1, matrix products, series(): jnp.einsum('pbh,sch->spbc', scaled, w_in_p, preferred_element_type=jnp.fl...  9.16 us
    all_to_all x2, starting transfers between devices, all_gather_pieces(): lax.all_to_all(jnp.broadcast_to(piece[None], (n,) + piece.shape), 'tensor...  8.87 us
  transfers between devices with their start and end apart: 16, of which 9 were waited for; matrix products, arithmetic and copies ran while one was open for 16% of the time, Pallas kernels for 0%

profile of v2, /device:TPU:0, one launch (start us, length us, event | category | flops | bytes accessed | tf_op | source)
XLA Modules:
  0.0 329.8 jit_solution(557372824698049610)
XLA Ops:
  11.2 3.5 %copy.58 = bf16[16,8,32,256]{3,2,1,0:T(8,128)(2,1)} copy(bf16[16,8,32,256]{3,1,2,0:T(8,128)(2,1)} %bitcast.133) | data formatting | bytes 4194304
  14.7 5.3 %convert_bitcast_fusion.1 = bf16[16,128,2,256]{3,1,0,2:T(8,128)(2,1)} fusion(bf16[128,2,16,256]{3,2,1,0:T(8,128)(2,1)} %bitcast.131, bf16[128,4096]{1,0:T(8,128)(2,1)S(1)} %copy-done, bf16[4096,128]{1,0:T(8,128)(2,1)} %param.10), kind=kOutput, calls=%fused_computation.16 | convolution fusion | flops 403783680 | bytes 6291456 | tf_op jit(solution)/shard_map/bk,kmsc->sbmc/dot_general | solution.py:105
  20.1 3.4 %copy.34 = bf16[16,128,2,256]{3,1,2,0:T(8,128)(2,1)} copy(bf16[16,128,2,256]{3,1,0,2:T(8,128)(2,1)} %convert_bitcast_fusion.1) | data formatting | bytes 4194304 | tf_op jit(solution)/shard_map/convert_element_type | solution.py:42
  23.5 8.1 %all-to-all-start = ((bf16[16,128,2,256]{3,1,2,0:T(8,128)(2,1)}), bf16[16,128,2,256]{3,1,2,0:T(8,128)(2,1)}, u32[]{:S(2)}, u32[]{:S(2)}) async-start(bf16[16,128,2,256]{3,1,2,0:T(8,128)(2,1)} %copy.34), calls=%async_computation | async-start | bytes 4194304 | tf_op jit(solution)/shard_map/all_to_all | solution.py:42
  32.8 10.6 %collective-permute-done.1 = bf16[512,1024]{1,0:T(8,128)(2,1)S(1)} collective-permute-done((bf16[512,1024]{1,0:T(8,128)(2,1)}, bf16[512,1024]{1,0:T(8,128)(2,1)S(1)}, u32[]{:S(2)}, u32[]{:S(2)}) %collective-permute-start.1) | collective-permute-done | bytes 1048608 | tf_op jit(solution)/shard_map/ppermute | solution.py:23
  52.7 9.4 %all-to-all-done = bf16[16,128,2,256]{3,1,2,0:T(8,128)(2,1)} async-done(((bf16[16,128,2,256]{3,1,2,0:T(8,128)(2,1)}), bf16[16,128,2,256]{3,1,2,0:T(8,128)(2,1)}, u32[]{:S(2)}, u32[]{:S(2)}) %all-to-all-start) | async-done | bytes 2097184 | tf_op jit(solution)/shard_map/all_to_all | solution.py:42
  65.3 4.3 %all-to-all-start.1 = ((bf16[16,128,256]{2,1,0:T(8,128)(2,1)}), bf16[16,128,256]{2,1,0:T(8,128)(2,1)}, u32[]{:S(2)}, u32[]{:S(2)}) async-start(bf16[16,128,256]{2,1,0:T(8,128)(2,1)} %broadcast_in_dim.16), calls=%async_computation.1 | async-start | bytes 2097152 | tf_op jit(solution)/shard_map/all_to_all | solution.py:48
  69.6 9.9 %collective-permute-done.3 = bf16[512,1024]{1,0:T(8,128)(2,1)} collective-permute-done((bf16[512,1024]{1,0:T(8,128)(2,1)S(1)}, bf16[512,1024]{1,0:T(8,128)(2,1)}, u32[]{:S(2)}, u32[]{:S(2)}) %collective-permute-start.3) | collective-permute-done | bytes 1048608 | tf_op jit(solution)/shard_map/ppermute | solution.py:29
  79.8 3.1 copy.36
  97.4 4.8 %multiply_subtract_fusion = (f32[128,1024]{1,0:T(8,128)S(1)}, bf16[128,1024]{1,0:T(8,128)(2,1)S(1)}) fusion(bf16[16,128,256]{2,1,0:T(8,128)(2,1)S(1)} %gather_fusion, bf16[16,256,1024]{2,1,0:T(8,128)(2,1)} %bitcast.9), kind=kOutput, calls=%fused_computation.38 | convolution fusion | flops 1074135040 | bytes 10223616 | tf_op jit(solution)/shard_map/sbc,sch->bh/dot_general | solution.py:111
  103.0 5.8 %fusion.24 = bf16[2,128,1024,1]{2,1,0,3:T(8,128)(2,1)S(1)} fusion(bf16[16,256,1024,1]{2,1,3,0:T(8,128)(2,1)} %bitcast.11, bf16[16,2,128,256]{2,3,1,0:T(8,128)(2,1)S(1)} %copy-done.2, f32[128,1024]{1,0:T(8,128)S(1)} %get-tuple-element.10), kind=kOutput, calls=%fused_computation.32 | convolution fusion | flops 2148007936 | bytes 11534336 | tf_op jit(solution)/shard_map/pbsc,sch->pbh/dot_general | solution.py:69
  108.8 5.8 %fusion.23 = bf16[2,128,1024,1]{2,1,0,3:T(8,128)(2,1)S(1)} fusion(bf16[2,128,16,256]{1,3,2,0:T(8,128)(2,1)S(1)} %bitcast.128, bf16[16,256,1024,1]{2,1,0,3:T(8,128)(2,1)} %bitcast.123, f32[128,1024]{1,0:T(8,128)} %copy-done.4), kind=kOutput, calls=%fused_computation.31 | convolution fusion | flops 2148007936 | bytes 11534336 | tf_op jit(solution)/shard_map/pbsc,sch->pbh/dot_general | solution.py:65
  114.6 9.2 %convolution_bitcast_fusion = bf16[16,2,128,256]{2,3,1,0:T(8,128)(2,1)} fusion(bf16[16,256,1024,1]{2,1,3,0:T(8,128)(2,1)} %bitcast.11, bf16[2,128,1024,1]{2,1,0,3:T(8,128)(2,1)S(1)} %fusion.23), kind=kOutput, calls=%fused_computation.9 | convolution fusion | flops 2147483648 | bytes 11010048 | tf_op jit(solution)/shard_map/pbh,sch->spbc/dot_general | solution.py:67
  123.7 3.7 %gather_fusion.1 = bf16[16,2,128,256]{2,3,1,0:T(8,128)(2,1)} fusion(bf16[16,2,128,256]{2,3,1,0:T(8,128)(2,1)} %convolution_bitcast_fusion, s32[1024]{0:T(1024)S(1)} %pad_clamp_fusion), kind=kCustom, calls=%fused_computation.1 | custom fusion | bytes 4194368 | tf_op jit(solution)/shard_map/jit(_take)/gather | solution.py:68
  127.5 8.3 %convert_bitcast_fusion = bf16[16,2,128,256]{2,3,1,0:T(8,128)(2,1)S(1)} fusion(bf16[2,128,1024,1]{2,1,0,3:T(8,128)(2,1)S(1)} %fusion.24, bf16[16,256,1024,1]{2,1,3,0:T(8,128)(2,1)} %bitcast.124), kind=kOutput, calls=%fused_computation.15 | convolution fusion | flops 2148532224 | bytes 11010048 | tf_op jit(solution)/shard_map/pbh,sch->spbc/dot_general | solution.py:71
  135.8 5.9 %fusion.7 = bf16[16,1,128,256]{2,3,1,0:T(8,128)(2,1)S(1)} fusion(bf16[16,256,1024]{2,1,0:T(8,128)(2,1)} %bitcast.125, bf16[128,1024]{1,0:T(8,128)(2,1)S(1)} %get-tuple-element.11), kind=kOutput, calls=%fused_computation.18 | convolution fusion | flops 1074266112 | bytes 9699328 | tf_op jit(solution)/shard_map/bh,sch->sbc/dot_general | solution.py:115
  142.4 70.7 %all_to_all.20 = bf16[16,5,128,256]{2,3,1,0:T(8,128)(2,1)S(1)} all-to-all(bf16[16,5,128,256]{2,3,1,0:T(8,128)(2,1)S(1)} %pad_maximum_fusion), channel_id=1, replica_groups=mesh['dp'=8,'tensor'=16] {'tensor'}, dimensions={0} | all-to-all | bytes 10485760 | tf_op jit(solution)/shard_map/all_to_all | solution.py:42
  218.6 4.5 %all-to-all-start.3 = ((bf16[16,4,128,256]{3,2,1,0:T(8,128)(2,1)}), bf16[16,4,128,256]{3,2,1,0:T(8,128)(2,1)}, u32[]{:S(2)}, u32[]{:S(2)}) async-start(bf16[16,4,128,256]{3,2,1,0:T(8,128)(2,1)} %broadcast_in_dim.19), calls=%async_computation.3 | async-start | bytes 8388608 | tf_op jit(solution)/shard_map/all_to_all | solution.py:48
  223.2 61.4 %all-to-all-done.3 = bf16[16,4,128,256]{3,2,1,0:T(8,128)(2,1)} async-done(((bf16[16,4,128,256]{3,2,1,0:T(8,128)(2,1)}), bf16[16,4,128,256]{3,2,1,0:T(8,128)(2,1)}, u32[]{:S(2)}, u32[]{:S(2)}) %all-to-all-start.3) | async-done | bytes 4194336 | tf_op jit(solution)/shard_map/all_to_all | solution.py:48
  284.6 3.2 slice.59
  292.5 6.5 %fusion.22 = bf16[2,128,1024,1]{2,1,0,3:T(8,128)(2,1)S(1)} fusion(bf16[16,4,128,256]{3,2,1,0:T(8,128)(2,1)} %all-to-all-done.3, bf16[16,256,1024,1]{2,1,3,0:T(8,128)(2,1)} %bitcast.126, f32[128,1024]{1,0:T(8,128)S(1)} %copy-done.5), kind=kOutput, calls=%fused_computation.30 | convolution fusion | flops 2148007936 | bytes 13631488 | tf_op jit(solution)/shard_map/spbc,sch->pbh/dot_general | solution.py:82
  299.0 8.2 %fusion = f32[128]{0:T(128)S(1)} fusion(bf16[16,2,128,256]{2,3,1,0:T(8,128)(2,1)S(1)} %copy-done.7, bf16[16,256,1024,1]{2,1,3,0:T(8,128)(2,1)} %bitcast.11, bf16[2,128,1024,1]{2,1,0,3:T(8,128)(2,1)S(1)} %fusion.22), kind=kOutput, calls=%fused_computation.7 | convolution fusion | flops 2150629376 | bytes 11010560 | tf_op jit(solution)/shard_map/pbh,sch->spbc/dot_general | solution.py:86
  314.7 3.0 collective-permute-start.10
  319.7 2.7 collective-permute-done.11
  (85 shorter events, 54.1 us)
Async XLA Ops:
  7.2 7.6 %copy-start = (bf16[128,4096]{1,0:T(8,128)(2,1)S(1)}, bf16[128,4096]{1,0:T(8,128)(2,1)}, u32[]{:S(2)}) copy-start(bf16[128,4096]{1,0:T(8,128)(2,1)} %param.9) | copy-start | bytes 3145732
  7.2 101.6 %all-gather.2.cloned.1.call-start = ((), (), s32[]{:S(2)}) async-start(), calls=%async_computation.4 | async-start | bytes 9437184 | tf_op jit(solution)/shard_map/all_gather | solution.py:98
  7.9 35.6 %collective-permute-start.1 = (bf16[512,1024]{1,0:T(8,128)(2,1)}, bf16[512,1024]{1,0:T(8,128)(2,1)S(1)}, u32[]{:S(2)}, u32[]{:S(2)}) collective-permute-start(bf16[512,1024]{1,0:T(8,128)(2,1)} %param.13), channel_id=1, source_target_pairs={{0,32},{16,48},{32,64},{48,80},{64,96},{80,112},{96,0},{112,16},{1... | collective-permute-start | bytes 3145736 | tf_op jit(solution)/shard_map/ppermute | solution.py:23
  9.7 35.5 %collective-permute-start.2 = (bf16[512,1024]{1,0:T(8,128)(2,1)}, bf16[512,1024]{1,0:T(8,128)(2,1)S(1)}, u32[]{:S(2)}, u32[]{:S(2)}) collective-permute-start(bf16[512,1024]{1,0:T(8,128)(2,1)} %param.13), channel_id=1, source_target_pairs={{0,96},{16,112},{32,0},{48,16},{64,32},{80,48},{96,64},{112,80},{1... | collective-permute-start | bytes 3145736 | tf_op jit(solution)/shard_map/ppermute | solution.py:24
  20.1 11.5 %copy-start.8 = (bf16[512,1024]{1,0:T(8,128)(2,1)S(1)}, bf16[512,1024]{1,0:T(8,128)(2,1)}, u32[]{:S(2)}) copy-start(bf16[512,1024]{1,0:T(8,128)(2,1)} %param.13) | copy-start | bytes 3145732
  23.5 38.6 %all-to-all-start = ((bf16[16,128,2,256]{3,1,2,0:T(8,128)(2,1)}), bf16[16,128,2,256]{3,1,2,0:T(8,128)(2,1)}, u32[]{:S(2)}, u32[]{:S(2)}) async-start(bf16[16,128,2,256]{3,1,2,0:T(8,128)(2,1)} %copy.34), calls=%async_computation | async-start | bytes 4194304 | tf_op jit(solution)/shard_map/all_to_all | solution.py:42
  31.6 15.1 %collective-permute-start = (bf16[512,1024]{1,0:T(8,128)(2,1)S(1)}, bf16[512,1024]{1,0:T(8,128)(2,1)}, u32[]{:S(2)}, u32[]{:S(2)}) collective-permute-start(bf16[512,1024]{1,0:T(8,128)(2,1)S(1)} %copy-done.8), channel_id=1, source_target_pairs={{0,16},{16,0},{32,48},{48,32},{64,80},{80,64},{96,112},{112,96},{1... | collective-permute-start | bytes 3145736 | tf_op jit(solution)/shard_map/ppermute | solution.py:25
  46.7 43.9 %collective-permute-start.4 = (bf16[2,512,1024]{2,1,0:T(8,128)(2,1)}, bf16[2,512,1024]{2,1,0:T(8,128)(2,1)}, u32[]{:S(2)}, u32[]{:S(2)}) collective-permute-start(bf16[2,512,1024]{2,1,0:T(8,128)(2,1)} %pad_maximum_fusion.1), channel_id=1, source_target_pairs={{0,16},{16,0},{32,48},{48,32},{64,80},{80,64},{96,112},{112,96},{1... | collective-permute-start | bytes 6291464 | tf_op jit(solution)/shard_map/ppermute | solution.py:30
  49.0 15.1 %copy-start.9 = (bf16[128,256]{1,0:T(8,128)(2,1)S(1)}, bf16[128,256]{1,0:T(8,128)(2,1)}, u32[]{:S(2)}) copy-start(bf16[128,256]{1,0:T(8,128)(2,1)} %param.12) | copy-start | bytes 196612
  50.0 19.6 %copy-start.10 = (s32[8]{0:T(128)S(1)}, s32[8]{0:T(128)}, u32[]{:S(2)}) copy-start(s32[8]{0:T(128)} %constant.74.clone) | copy-start | bytes 100
  50.0 19.6 %copy-start.11 = (s32[8]{0:T(128)S(1)}, s32[8]{0:T(128)}, u32[]{:S(2)}) copy-start(s32[8]{0:T(128)} %constant.75.clone) | copy-start | bytes 100
  51.6 27.9 %collective-permute-start.3 = (bf16[512,1024]{1,0:T(8,128)(2,1)S(1)}, bf16[512,1024]{1,0:T(8,128)(2,1)}, u32[]{:S(2)}, u32[]{:S(2)}) collective-permute-start(bf16[512,1024]{1,0:T(8,128)(2,1)S(1)} %get-tuple-element.8), channel_id=1, source_target_pairs={{0,32},{16,112},{32,64},{48,16},{64,96},{80,48},{96,0},{112,80},{1... | collective-permute-start | bytes 3145736 | tf_op jit(solution)/shard_map/ppermute | solution.py:29
  65.3 23.5 %all-to-all-start.1 = ((bf16[16,128,256]{2,1,0:T(8,128)(2,1)}), bf16[16,128,256]{2,1,0:T(8,128)(2,1)}, u32[]{:S(2)}, u32[]{:S(2)}) async-start(bf16[16,128,256]{2,1,0:T(8,128)(2,1)} %broadcast_in_dim.16), calls=%async_computation.1 | async-start | bytes 2097152 | tf_op jit(solution)/shard_map/all_to_all | solution.py:48
  79.5 15.6 %collective-permute-start.5 = (bf16[512,1024]{1,0:T(8,128)(2,1)}, bf16[512,1024]{1,0:T(8,128)(2,1)}, u32[]{:S(2)}, u32[]{:S(2)}) collective-permute-start(bf16[512,1024]{1,0:T(8,128)(2,1)} %collective-permute-done.3), channel_id=1, source_target_pairs={{0,16},{16,0},{32,48},{48,32},{64,80},{80,64},{96,112},{112,96},{1... | collective-permute-start | bytes 3145736 | tf_op jit(solution)/shard_map/ppermute | solution.py:31
  218.6 66.0 %all-to-all-start.3 = ((bf16[16,4,128,256]{3,2,1,0:T(8,128)(2,1)}), bf16[16,4,128,256]{3,2,1,0:T(8,128)(2,1)}, u32[]{:S(2)}, u32[]{:S(2)}) async-start(bf16[16,4,128,256]{3,2,1,0:T(8,128)(2,1)} %broadcast_in_dim.19), calls=%async_computation.3 | async-start | bytes 8388608 | tf_op jit(solution)/shard_map/all_to_all | solution.py:48
  292.5 6.5 %copy-start.7 = (bf16[16,2,128,256]{2,3,1,0:T(8,128)(2,1)S(1)}, bf16[16,2,128,256]{2,3,1,0:T(8,128)(2,1)}, u32[]{:S(2)}) copy-start(bf16[16,2,128,256]{2,3,1,0:T(8,128)(2,1)} %copy.44) | copy-start | bytes 6291460
  299.0 13.0 %slice-start = ((f32[5,128,256]{1,2,0:T(8,128)}), f32[1,128,256]{1,2,0:T(8,128)S(1)}, s32[]{:S(2)}) async-start(f32[5,128,256]{1,2,0:T(8,128)} %copy-done.6), calls=%async_computation.5 | async-start | bytes 262144 | tf_op jit(solution)/shard_map/slice | solution.py:75
  299.0 24.0 %copy-start.1 = (bf16[128,4096]{1,0:T(8,128)(2,1)S(1)}, bf16[128,4096]{1,0:T(8,128)(2,1)}, u32[]{:S(2)}) copy-start(bf16[128,4096]{1,0:T(8,128)(2,1)} %param.9) | copy-start | bytes 3145732
  307.2 4.9 %collective-permute-start.6 = (f32[128]{0:T(128)S(1)}, f32[128]{0:T(128)S(1)}, u32[]{:S(2)}, u32[]{:S(2)}) collective-permute-start(f32[128]{0:T(128)S(1)} %multiply_add_fusion), channel_id=1, source_target_pairs={{0,1},{1,0},{2,3},{3,2},{4,5},{5,4},{6,7},{7,6},{8,9},{9,8},{10,11... | collective-permute-start | bytes 1544 | tf_op jit(solution)/shard_map/ppermute | solution.py:55
  307.3 5.2 %collective-permute-start.7 = (f32[128]{0:T(128)S(1)}, f32[128]{0:T(128)S(1)}, u32[]{:S(2)}, u32[]{:S(2)}) collective-permute-start(f32[128]{0:T(128)S(1)} %multiply_add_fusion), channel_id=1, source_target_pairs={{0,2},{1,3},{2,0},{3,1},{4,6},{5,7},{6,4},{7,5},{8,10},{9,11},{10,... | collective-permute-start | bytes 1544 | tf_op jit(solution)/shard_map/ppermute | solution.py:55
  309.9 4.8 %collective-permute-start.8 = (f32[128]{0:T(128)S(1)}, f32[128]{0:T(128)S(1)}, u32[]{:S(2)}, u32[]{:S(2)}) collective-permute-start(f32[128]{0:T(128)S(1)} %multiply_add_fusion), channel_id=1, source_target_pairs={{0,3},{1,2},{2,1},{3,0},{4,7},{5,6},{6,5},{7,4},{8,11},{9,10},{10,... | collective-permute-start | bytes 1544 | tf_op jit(solution)/shard_map/ppermute | solution.py:55
  314.7 5.1 %collective-permute-start.10 = (f32[128]{0:T(128)S(1)}, f32[128]{0:T(128)S(1)}, u32[]{:S(2)}, u32[]{:S(2)}) collective-permute-start(f32[128]{0:T(128)S(1)} %add_add_fusion), channel_id=1, source_target_pairs={{0,8},{1,9},{2,10},{3,11},{4,12},{5,13},{6,14},{7,15},{8,0},{9,1},... | collective-permute-start | bytes 1544 | tf_op jit(solution)/shard_map/ppermute | solution.py:55
  317.7 4.8 %collective-permute-start.11 = (f32[128]{0:T(128)S(1)}, f32[128]{0:T(128)S(1)}, u32[]{:S(2)}, u32[]{:S(2)}) collective-permute-start(f32[128]{0:T(128)S(1)} %add_add_fusion), channel_id=1, source_target_pairs={{0,12},{1,13},{2,14},{3,15},{4,8},{5,9},{6,10},{7,11},{8,4},{9,5},... | collective-permute-start | bytes 1544 | tf_op jit(solution)/shard_map/ppermute | solution.py:55
  317.7 4.8 %collective-permute-start.9 = (f32[128]{0:T(128)S(1)}, f32[128]{0:T(128)S(1)}, u32[]{:S(2)}, u32[]{:S(2)}) collective-permute-start(f32[128]{0:T(128)S(1)} %add_add_fusion), channel_id=1, source_target_pairs={{0,4},{1,5},{2,6},{3,7},{4,0},{5,1},{6,2},{7,3},{8,12},{9,13},{10,... | collective-permute-start | bytes 1544 | tf_op jit(solution)/shard_map/ppermute | solution.py:55
  (5 other events, 21.5 us)
Sparse Core Ops, SparseCore 0:
  9.7 66.7 all-gather.1

commit v3 on v1

--- a/solution.py
+++ b/solution.py
@@ -8,9 +8,11 @@
 TERMS = 3
 
 
-def gather_dp(block):
+def gather_dp(block, after=None):
     n = lax.axis_size("dp")
     ny = n // 2
+    if after is not None:
+        block, _ = lax.optimization_barrier((block, after))
 
     def perm(fn):
         return [(d, fn(d // 2, d % 2)) for d in range(n)]
@@ -35,7 +37,7 @@
     rel_y = jnp.array([0, 0, -1, 1, 2, -1, 1, 2], jnp.int32)
     flip = jnp.array([0, 1, 0, 0, 0, 1, 1, 1], jnp.int32)
     block_ids = 2 * ((y + rel_y) % ny) + (c ^ flip)
-    return joined, block_ids
+    return joined, block_ids, (from_below, from_above, far)
 
 
 def reduce_scatter_pieces(pieces):
@@ -89,8 +91,8 @@
 
 def local(features, enc_in, enc_out, noise, in_weight, out_weight, probes):
     n = lax.axis_size("tensor")
-    w_in, block_ids = gather_dp(in_weight)
-    w_out, _ = gather_dp(out_weight)
+    w_in, block_ids, first_round = gather_dp(in_weight)
+    w_out, _, _ = gather_dp(out_weight, after=first_round)
     w_in = w_in.reshape(n, -1, in_weight.shape[-1])
     w_out = w_out.reshape(n, -1, out_weight.shape[-1])
     halves = n // block_ids.shape[0]

time: 303 us -> 309 us (1.020)
  waiting for transfers between devices: 79.9 us -> 97 us
  local copies, waits for them, and re-layouts: 50.3 us -> 41.8 us
  starting transfers between devices: 40.6 us -> 35.4 us
  blocking collectives: 65.9 us -> 69.7 us
    all_to_all x1, waiting for transfers between devices: 0.01 us -> 23.1 us  [reduce_scatter_pieces(): received = lax.all_to_all(pieces.astype(jnp.bfloat16), 'tensor', 0, 0)]
    unnamed x36 -> x38, local copies, waits for them, and re-layouts: 33.4 us -> 24.8 us
    ppermute x2, waiting for transfers between devices: 9.28 us -> 3.6 us  [gather_dp(): from_below = lax.ppermute(block, 'dp', up)]
    all_to_all x1, blocking collectives: 65.9 us -> 69.7 us  [reduce_scatter_pieces(): received = lax.all_to_all(pieces.astype(jnp.bfloat16), 'tensor', 0, 0)]
    all_to_all x2, starting transfers between devices: 12.5 us -> 8.87 us  [all_gather_pieces(): lax.all_to_all(jnp.broadcast_to(piece[None], (n,) + piece.shape), 'tensor...]
    ppermute x2, waiting for transfers between devices: 0.01 us -> 3.16 us  [gather_dp(): far = lax.ppermute(relay, 'dp', fwd)]
  transfers between devices with their start and end apart: 21 -> 21, of which waited for: 7 -> 9; matrix products, arithmetic and copies ran while one was open for 21% -> 21% of each run, Pallas kernels for 0% -> 0%
where the time goes in v3:
time: 309 us; the launch traced here: 308 us
  waiting for transfers between devices  97 us (31%)
  blocking collectives  69.7 us (23%)
  matrix products  46.8 us (15%)
  local copies, waits for them, and re-layouts  41.8 us (14%)
  starting transfers between devices  35.4 us (11%)
  other arithmetic  16 us (5%)
    all_to_all x1, blocking collectives, reduce_scatter_pieces(): received = lax.all_to_all(pieces.astype(jnp.bfloat16), 'tensor', 0, 0)  69.7 us
    all_to_all x2, waiting for transfers between devices, all_gather_pieces(): lax.all_to_all(jnp.broadcast_to(piece[None], (n,) + piece.shape), 'tensor...  62 us
    unnamed x38, local copies, waits for them, and re-layouts  24.8 us
    all_to_all x1, waiting for transfers between devices, reduce_scatter_pieces(): received = lax.all_to_all(pieces.astype(jnp.bfloat16), 'tensor', 0, 0)  23.1 us
    ppermute x6, starting transfers between devices, psum_groups(): lax.ppermute(value, 'tensor', [(t, t ^ k * step) for t in range(n)])  9.47 us
    all_to_all x2, starting transfers between devices, all_gather_pieces(): lax.all_to_all(jnp.broadcast_to(piece[None], (n,) + piece.shape), 'tensor...  8.87 us
    dot_general x1, matrix products, series(): jnp.einsum('pbh,sch->spbc', scaled, w_in_p, preferred_element_type=jnp.fl...  8.56 us
    all_to_all x1, starting transfers between devices, reduce_scatter_pieces(): received = lax.all_to_all(pieces.astype(jnp.bfloat16), 'tensor', 0, 0)  8.04 us
  transfers between devices with their start and end apart: 21, of which 9 were waited for; matrix products, arithmetic and copies ran while one was open for 21% of the time, Pallas kernels for 0%

profile of v3, /device:TPU:0, one launch (start us, length us, event | category | flops | bytes accessed | tf_op | source)
XLA Modules:
  0.0 307.7 jit_solution(12419846900894584571)
XLA Ops:
  4.0 3.5 %copy.39 = bf16[16,8,32,256]{3,2,1,0:T(8,128)(2,1)} copy(bf16[16,8,32,256]{3,1,2,0:T(8,128)(2,1)} %bitcast.148) | data formatting | bytes 4194304
  7.6 5.3 %convert_bitcast_fusion.2 = bf16[16,128,2,256]{3,1,0,2:T(8,128)(2,1)} fusion(bf16[128,2,16,256]{3,2,1,0:T(8,128)(2,1)} %bitcast.144, bf16[128,4096]{1,0:T(8,128)(2,1)S(1)} %copy-done, bf16[4096,128]{1,0:T(8,128)(2,1)} %param.10), kind=kOutput, calls=%fused_computation.18 | convolution fusion | flops 403783680 | bytes 6291456 | tf_op jit(solution)/shard_map/bk,kmsc->sbmc/dot_general | solution.py:105
  12.8 3.2 %copy.29 = bf16[16,128,2,256]{3,1,2,0:T(8,128)(2,1)} copy(bf16[16,128,2,256]{3,1,0,2:T(8,128)(2,1)} %convert_bitcast_fusion.2) | data formatting | bytes 4194304 | tf_op jit(solution)/shard_map/convert_element_type | solution.py:44
  16.1 8.0 %all-to-all-start = ((bf16[16,128,2,256]{3,1,2,0:T(8,128)(2,1)}), bf16[16,128,2,256]{3,1,2,0:T(8,128)(2,1)}, u32[]{:S(2)}, u32[]{:S(2)}) async-start(bf16[16,128,2,256]{3,1,2,0:T(8,128)(2,1)} %copy.29), calls=%async_computation | async-start | bytes 4194304 | tf_op jit(solution)/shard_map/all_to_all | solution.py:44
  33.1 23.1 %all-to-all-done = bf16[16,128,2,256]{3,1,2,0:T(8,128)(2,1)} async-done(((bf16[16,128,2,256]{3,1,2,0:T(8,128)(2,1)}), bf16[16,128,2,256]{3,1,2,0:T(8,128)(2,1)}, u32[]{:S(2)}, u32[]{:S(2)}) %all-to-all-start) | async-done | bytes 2097184 | tf_op jit(solution)/shard_map/all_to_all | solution.py:44
  59.4 4.3 %all-to-all-start.1 = ((bf16[16,128,256]{2,1,0:T(8,128)(2,1)}), bf16[16,128,256]{2,1,0:T(8,128)(2,1)}, u32[]{:S(2)}, u32[]{:S(2)}) async-start(bf16[16,128,256]{2,1,0:T(8,128)(2,1)} %broadcast_in_dim.15), calls=%async_computation.1 | async-start | bytes 2097152 | tf_op jit(solution)/shard_map/all_to_all | solution.py:50
  64.1 3.0 collective-permute-start.8
  67.3 4.1 %copy.30 = bf16[2,128,4096]{1,2,0:T(8,128)(2,1)} copy(bf16[2,128,4096]{2,1,0:T(8,128)(2,1)} %param.15) | data formatting | bytes 4194304 | tf_op args[6]
  71.4 2.9 copy.31
  87.5 3.3 %collective-permute-done.7 = bf16[512,1024]{1,0:T(8,128)(2,1)S(1)} collective-permute-done((bf16[512,1024]{1,0:T(8,128)(2,1)}, bf16[512,1024]{1,0:T(8,128)(2,1)S(1)}, u32[]{:S(2)}, u32[]{:S(2)}) %collective-permute-start.7) | collective-permute-done | bytes 1048608 | tf_op jit(solution)/shard_map/ppermute | solution.py:25
  91.9 2.7 broadcast_select_fusion
  102.7 4.7 %multiply_subtract_fusion = (f32[128,1024]{1,0:T(8,128)S(1)}, bf16[128,1024]{1,0:T(8,128)(2,1)S(1)}) fusion(bf16[16,128,256]{2,1,0:T(8,128)(2,1)S(1)} %gather_fusion.1, bf16[16,256,1024]{2,1,0:T(8,128)(2,1)} %bitcast.9), kind=kOutput, calls=%fused_computation.45 | convolution fusion | flops 1074135040 | bytes 10223616 | tf_op jit(solution)/shard_map/sbc,sch->bh/dot_general | solution.py:111
  107.4 3.2 %collective-permute-done.9 = bf16[512,1024]{1,0:T(8,128)(2,1)S(1)} collective-permute-done((bf16[512,1024]{1,0:T(8,128)(2,1)S(1)}, bf16[512,1024]{1,0:T(8,128)(2,1)S(1)}, u32[]{:S(2)}, u32[]{:S(2)}) %collective-permute-start.9) | collective-permute-done | bytes 1048608 | tf_op jit(solution)/shard_map/ppermute | solution.py:31
  110.6 5.9 %fusion.34 = bf16[2,128,1024,1]{2,1,0,3:T(8,128)(2,1)S(1)} fusion(bf16[16,256,1024,1]{2,1,3,0:T(8,128)(2,1)} %bitcast.11, bf16[16,2,128,256]{3,2,1,0:T(8,128)(2,1)S(1)} %copy-done.2, f32[128,1024]{1,0:T(8,128)S(1)} %get-tuple-element.14), kind=kOutput, calls=%fused_computation.33 | convolution fusion | flops 2148007936 | bytes 11534336 | tf_op jit(solution)/shard_map/pbsc,sch->pbh/dot_general | solution.py:68
  119.3 8.6 %convert_bitcast_fusion.1 = bf16[16,2,128,256]{2,3,1,0:T(8,128)(2,1)S(1)} fusion(bf16[16,256,1024,1]{2,1,3,0:T(8,128)(2,1)} %bitcast.11, bf16[2,128,1024,1]{2,1,0,3:T(8,128)(2,1)S(1)} %fusion.31), kind=kOutput, calls=%fused_computation.17 | convolution fusion | flops 2148532224 | bytes 11010048 | tf_op jit(solution)/shard_map/pbh,sch->spbc/dot_general | solution.py:67
  127.8 3.6 %convert_bitcast_fusion = bf16[16,2,128,256]{2,3,1,0:T(8,128)(2,1)} fusion(bf16[16,256,1024,1]{2,1,3,0:T(8,128)(2,1)S(1)} %bitcast.152, bf16[2,128,1024,1]{2,1,0,3:T(8,128)(2,1)S(1)} %fusion.34), kind=kOutput, calls=%fused_computation.16 | convolution fusion | flops 2148532224 | bytes 11010048 | tf_op jit(solution)/shard_map/pbh,sch->spbc/dot_general | solution.py:70
  131.4 3.4 %convolution_bitcast_fusion = bf16[16,128,256]{1,2,0:T(8,128)(2,1)} fusion(bf16[16,256,1024]{2,1,0:T(8,128)(2,1)S(1)} %bitcast.153, bf16[128,1024]{1,0:T(8,128)(2,1)S(1)} %get-tuple-element.15), kind=kOutput, calls=%fused_computation.19 | convolution fusion | flops 1073741824 | bytes 9699328 | tf_op jit(solution)/shard_map/bh,sch->sbc/dot_general | solution.py:115
  139.0 69.7 %all_to_all.20 = bf16[16,5,128,256]{2,3,1,0:T(8,128)(2,1)S(1)} all-to-all(bf16[16,5,128,256]{2,3,1,0:T(8,128)(2,1)S(1)} %pad_maximum_fusion), channel_id=1, replica_groups=mesh['dp'=8,'tensor'=16] {'tensor'}, dimensions={0} | all-to-all | bytes 10485760 | tf_op jit(solution)/shard_map/all_to_all | solution.py:44
  212.5 4.5 %all-to-all-start.3 = ((bf16[16,4,128,256]{3,2,1,0:T(8,128)(2,1)}), bf16[16,4,128,256]{3,2,1,0:T(8,128)(2,1)}, u32[]{:S(2)}, u32[]{:S(2)}) async-start(bf16[16,4,128,256]{3,2,1,0:T(8,128)(2,1)} %broadcast_in_dim.18), calls=%async_computation.3 | async-start | bytes 8388608 | tf_op jit(solution)/shard_map/all_to_all | solution.py:50
  218.1 60.8 %all-to-all-done.3 = bf16[16,4,128,256]{3,2,1,0:T(8,128)(2,1)} async-done(((bf16[16,4,128,256]{3,2,1,0:T(8,128)(2,1)}), bf16[16,4,128,256]{3,2,1,0:T(8,128)(2,1)}, u32[]{:S(2)}, u32[]{:S(2)}) %all-to-all-start.3) | async-done | bytes 4194336 | tf_op jit(solution)/shard_map/all_to_all | solution.py:50
  278.9 6.4 %fusion.30 = bf16[2,128,1024,1]{2,1,0,3:T(8,128)(2,1)S(1)} fusion(bf16[16,4,128,256]{3,2,1,0:T(8,128)(2,1)} %all-to-all-done.3, bf16[16,256,1024,1]{2,1,3,0:T(8,128)(2,1)} %bitcast.154, f32[128,1024]{1,0:T(8,128)S(1)} %copy-done.5), kind=kOutput, calls=%fused_computation.31 | convolution fusion | flops 2148007936 | bytes 13631488 | tf_op jit(solution)/shard_map/spbc,sch->pbh/dot_general | solution.py:81
  285.4 6.6 %fusion = f32[128]{0:T(128)S(1)} fusion(bf16[16,256,1024,1]{2,1,3,0:T(8,128)(2,1)} %bitcast.11, bf16[2,128,1024,1]{2,1,0,3:T(8,128)(2,1)S(1)} %fusion.30, bf16[16,4,128,256]{3,2,1,0:T(8,128)(2,1)} %all-to-all-done.3), kind=kOutput, calls=%fused_computation.6 | convolution fusion | flops 2150629376 | bytes 11010560 | tf_op jit(solution)/shard_map/pbh,sch->spbc/dot_general | solution.py:85
  292.0 2.6 collective-permute-start.13
  299.4 3.0 collective-permute-start.16
  (99 shorter events, 60.2 us)
Async XLA Ops:
  0.6 24.7 %collective-permute-start = (bf16[512,1024]{1,0:T(8,128)(2,1)}, bf16[512,1024]{1,0:T(8,128)(2,1)}, u32[]{:S(2)}, u32[]{:S(2)}) collective-permute-start(bf16[512,1024]{1,0:T(8,128)(2,1)} %param.13), channel_id=1, source_target_pairs={{0,16},{16,0},{32,48},{48,32},{64,80},{80,64},{96,112},{112,96},{1... | collective-permute-start | bytes 3145736 | tf_op jit(solution)/shard_map/ppermute | solution.py:27
  0.7 27.2 %collective-permute-start.1 = (bf16[512,1024]{1,0:T(8,128)(2,1)}, bf16[512,1024]{1,0:T(8,128)(2,1)S(1)}, u32[]{:S(2)}, u32[]{:S(2)}) collective-permute-start(bf16[512,1024]{1,0:T(8,128)(2,1)} %param.13), channel_id=1, source_target_pairs={{0,32},{16,48},{32,64},{48,80},{64,96},{80,112},{96,0},{112,16},{1... | collective-permute-start | bytes 3145736 | tf_op jit(solution)/shard_map/ppermute | solution.py:25
  2.5 26.4 %collective-permute-start.2 = (bf16[512,1024]{1,0:T(8,128)(2,1)}, bf16[512,1024]{1,0:T(8,128)(2,1)S(1)}, u32[]{:S(2)}, u32[]{:S(2)}) collective-permute-start(bf16[512,1024]{1,0:T(8,128)(2,1)} %param.13), channel_id=1, source_target_pairs={{0,96},{16,112},{32,0},{48,16},{64,32},{80,48},{96,64},{112,80},{1... | collective-permute-start | bytes 3145736 | tf_op jit(solution)/shard_map/ppermute | solution.py:26
  16.1 40.1 %all-to-all-start = ((bf16[16,128,2,256]{3,1,2,0:T(8,128)(2,1)}), bf16[16,128,2,256]{3,1,2,0:T(8,128)(2,1)}, u32[]{:S(2)}, u32[]{:S(2)}) async-start(bf16[16,128,2,256]{3,1,2,0:T(8,128)(2,1)} %copy.29), calls=%async_computation | async-start | bytes 4194304 | tf_op jit(solution)/shard_map/all_to_all | solution.py:44
  27.6 39.5 %copy-start.8 = (s32[8]{0:T(128)S(1)}, s32[8]{0:T(128)}, u32[]{:S(2)}) copy-start(s32[8]{0:T(128)} %constant.76.clone) | copy-start | bytes 100
  27.6 39.5 %copy-start.9 = (s32[8]{0:T(128)S(1)}, s32[8]{0:T(128)}, u32[]{:S(2)}) copy-start(s32[8]{0:T(128)} %constant.77.clone) | copy-start | bytes 100
  30.5 27.6 %collective-permute-start.3 = (bf16[512,1024]{1,0:T(8,128)(2,1)S(1)}, bf16[512,1024]{1,0:T(8,128)(2,1)}, u32[]{:S(2)}, u32[]{:S(2)}) collective-permute-start(bf16[512,1024]{1,0:T(8,128)(2,1)S(1)} %get-tuple-element.11), channel_id=1, source_target_pairs={{0,32},{16,112},{32,64},{48,16},{64,96},{80,48},{96,0},{112,80},{1... | collective-permute-start | bytes 3145736 | tf_op jit(solution)/shard_map/ppermute | solution.py:31
  32.6 64.6 %collective-permute-start.4 = (bf16[2,512,1024]{2,1,0:T(8,128)(2,1)}, bf16[2,512,1024]{2,1,0:T(8,128)(2,1)}, u32[]{:S(2)}, u32[]{:S(2)}) collective-permute-start(bf16[2,512,1024]{2,1,0:T(8,128)(2,1)} %pad_maximum_fusion.1), channel_id=1, source_target_pairs={{0,16},{16,0},{32,48},{48,32},{64,80},{80,64},{96,112},{112,96},{1... | collective-permute-start | bytes 6291464 | tf_op jit(solution)/shard_map/ppermute | solution.py:32
  58.2 27.1 %collective-permute-start.6 = (bf16[512,1024]{1,0:T(8,128)(2,1)}, bf16[512,1024]{1,0:T(8,128)(2,1)}, u32[]{:S(2)}, u32[]{:S(2)}) collective-permute-start(bf16[512,1024]{1,0:T(8,128)(2,1)} %param.14), channel_id=1, source_target_pairs={{0,16},{16,0},{32,48},{48,32},{64,80},{80,64},{96,112},{112,96},{1... | collective-permute-start | bytes 3145736 | tf_op jit(solution)/shard_map/ppermute | solution.py:27
  59.4 24.0 %all-to-all-start.1 = ((bf16[16,128,256]{2,1,0:T(8,128)(2,1)}), bf16[16,128,256]{2,1,0:T(8,128)(2,1)}, u32[]{:S(2)}, u32[]{:S(2)}) async-start(bf16[16,128,256]{2,1,0:T(8,128)(2,1)} %broadcast_in_dim.15), calls=%async_computation.1 | async-start | bytes 2097152 | tf_op jit(solution)/shard_map/all_to_all | solution.py:50
  63.8 27.0 %collective-permute-start.7 = (bf16[512,1024]{1,0:T(8,128)(2,1)}, bf16[512,1024]{1,0:T(8,128)(2,1)S(1)}, u32[]{:S(2)}, u32[]{:S(2)}) collective-permute-start(bf16[512,1024]{1,0:T(8,128)(2,1)} %param.14), channel_id=1, source_target_pairs={{0,32},{16,48},{32,64},{48,80},{64,96},{80,112},{96,0},{112,16},{1... | collective-permute-start | bytes 3145736 | tf_op jit(solution)/shard_map/ppermute | solution.py:25
  64.1 27.8 %collective-permute-start.8 = (bf16[512,1024]{1,0:T(8,128)(2,1)}, bf16[512,1024]{1,0:T(8,128)(2,1)}, u32[]{:S(2)}, u32[]{:S(2)}) collective-permute-start(bf16[512,1024]{1,0:T(8,128)(2,1)} %param.14), channel_id=1, source_target_pairs={{0,96},{16,112},{32,0},{48,16},{64,32},{80,48},{96,64},{112,80},{1... | collective-permute-start | bytes 3145736 | tf_op jit(solution)/shard_map/ppermute | solution.py:26
  77.6 24.1 %collective-permute-start.5 = (bf16[512,1024]{1,0:T(8,128)(2,1)}, bf16[512,1024]{1,0:T(8,128)(2,1)S(1)}, u32[]{:S(2)}, u32[]{:S(2)}) collective-permute-start(bf16[512,1024]{1,0:T(8,128)(2,1)} %collective-permute-done.3), channel_id=1, source_target_pairs={{0,16},{16,0},{32,48},{48,32},{64,80},{80,64},{96,112},{112,96},{1... | collective-permute-start | bytes 3145736 | tf_op jit(solution)/shard_map/ppermute | solution.py:33
  94.6 16.0 %collective-permute-start.9 = (bf16[512,1024]{1,0:T(8,128)(2,1)S(1)}, bf16[512,1024]{1,0:T(8,128)(2,1)S(1)}, u32[]{:S(2)}, u32[]{:S(2)}) collective-permute-start(bf16[512,1024]{1,0:T(8,128)(2,1)S(1)} %get-tuple-element.12), channel_id=1, source_target_pairs={{0,32},{16,112},{32,64},{48,16},{64,96},{80,48},{96,0},{112,80},{1... | collective-permute-start | bytes 3145736 | tf_op jit(solution)/shard_map/ppermute | solution.py:31
  96.0 20.7 %collective-permute-start.10 = (bf16[2,512,1024]{2,1,0:T(8,128)(2,1)S(1)}, bf16[2,512,1024]{2,1,0:T(8,128)(2,1)S(1)}, u32[]{:S(2)}, u32[]{:S(2)}) collective-permute-start(bf16[2,512,1024]{2,1,0:T(8,128)(2,1)S(1)} %pad_maximum_fusion.2), channel_id=1, source_target_pairs={{0,16},{16,0},{32,48},{48,32},{64,80},{80,64},{96,112},{112,96},{1... | collective-permute-start | bytes 6291464 | tf_op jit(solution)/shard_map/ppermute | solution.py:32
  110.6 6.2 %collective-permute-start.11 = (bf16[512,1024]{1,0:T(8,128)(2,1)S(1)}, bf16[512,1024]{1,0:T(8,128)(2,1)S(1)}, u32[]{:S(2)}, u32[]{:S(2)}) collective-permute-start(bf16[512,1024]{1,0:T(8,128)(2,1)S(1)} %collective-permute-done.9), channel_id=1, source_target_pairs={{0,16},{16,0},{32,48},{48,32},{64,80},{80,64},{96,112},{112,96},{1... | collective-permute-start | bytes 3145736 | tf_op jit(solution)/shard_map/ppermute | solution.py:33
  209.7 69.2 %copy-start.5 = (f32[128,1024]{1,0:T(8,128)S(1)}, f32[128,1024]{1,0:T(8,128)}, u32[]{:S(2)}) copy-start(f32[128,1024]{1,0:T(8,128)} %copy-done.4) | copy-start | bytes 1572868
  212.5 66.4 %all-to-all-start.3 = ((bf16[16,4,128,256]{3,2,1,0:T(8,128)(2,1)}), bf16[16,4,128,256]{3,2,1,0:T(8,128)(2,1)}, u32[]{:S(2)}, u32[]{:S(2)}) async-start(bf16[16,4,128,256]{3,2,1,0:T(8,128)(2,1)} %broadcast_in_dim.18), calls=%async_computation.3 | async-start | bytes 8388608 | tf_op jit(solution)/shard_map/all_to_all | solution.py:50
  291.9 4.8 %collective-permute-start.12 = (f32[128]{0:T(128)S(1)}, f32[128]{0:T(128)S(1)}, u32[]{:S(2)}, u32[]{:S(2)}) collective-permute-start(f32[128]{0:T(128)S(1)} %multiply_add_fusion), channel_id=1, source_target_pairs={{0,1},{1,0},{2,3},{3,2},{4,5},{5,4},{6,7},{7,6},{8,9},{9,8},{10,11... | collective-permute-start | bytes 1544 | tf_op jit(solution)/shard_map/ppermute | solution.py:57
  292.0 5.2 %collective-permute-start.13 = (f32[128]{0:T(128)S(1)}, f32[128]{0:T(128)S(1)}, u32[]{:S(2)}, u32[]{:S(2)}) collective-permute-start(f32[128]{0:T(128)S(1)} %multiply_add_fusion), channel_id=1, source_target_pairs={{0,2},{1,3},{2,0},{3,1},{4,6},{5,7},{6,4},{7,5},{8,10},{9,11},{10,... | collective-permute-start | bytes 1544 | tf_op jit(solution)/shard_map/ppermute | solution.py:57
  294.6 4.8 %collective-permute-start.14 = (f32[128]{0:T(128)S(1)}, f32[128]{0:T(128)S(1)}, u32[]{:S(2)}, u32[]{:S(2)}) collective-permute-start(f32[128]{0:T(128)S(1)} %multiply_add_fusion), channel_id=1, source_target_pairs={{0,3},{1,2},{2,1},{3,0},{4,7},{5,6},{6,5},{7,4},{8,11},{9,10},{10,... | collective-permute-start | bytes 1544 | tf_op jit(solution)/shard_map/ppermute | solution.py:57
  299.4 5.4 %collective-permute-start.15 = (f32[128]{0:T(128)S(1)}, f32[128]{0:T(128)S(1)}, u32[]{:S(2)}, u32[]{:S(2)}) collective-permute-start(f32[128]{0:T(128)S(1)} %add_add_fusion), channel_id=1, source_target_pairs={{0,4},{1,5},{2,6},{3,7},{4,0},{5,1},{6,2},{7,3},{8,12},{9,13},{10,... | collective-permute-start | bytes 1544 | tf_op jit(solution)/shard_map/ppermute | solution.py:57
  299.4 5.4 %collective-permute-start.16 = (f32[128]{0:T(128)S(1)}, f32[128]{0:T(128)S(1)}, u32[]{:S(2)}, u32[]{:S(2)}) collective-permute-start(f32[128]{0:T(128)S(1)} %add_add_fusion), channel_id=1, source_target_pairs={{0,8},{1,9},{2,10},{3,11},{4,12},{5,13},{6,14},{7,15},{8,0},{9,1},... | collective-permute-start | bytes 1544 | tf_op jit(solution)/shard_map/ppermute | solution.py:57
  302.4 4.8 %collective-permute-start.17 = (f32[128]{0:T(128)S(1)}, f32[128]{0:T(128)S(1)}, u32[]{:S(2)}, u32[]{:S(2)}) collective-permute-start(f32[128]{0:T(128)S(1)} %add_add_fusion), channel_id=1, source_target_pairs={{0,12},{1,13},{2,14},{3,15},{4,8},{5,9},{6,10},{7,11},{8,4},{9,5},... | collective-permute-start | bytes 1544 | tf_op jit(solution)/shard_map/ppermute | solution.py:57
  (9 other events, 129.2 us)

commit v4 on v1

--- a/solution.py
+++ b/solution.py
@@ -72,16 +72,17 @@
     side = summed[2 * probes_n]
     u_here = uv_here[:probes_n].astype(jnp.float32)
     v_here = uv_here[probes_n:].astype(jnp.float32)
-    uv_pieces = all_gather_pieces(uv_here)
+    u_pieces = all_gather_pieces(uv_here[:probes_n])
+    v_pieces = lax.all_gather(uv_here[probes_n:], "tensor", axis=0, tiled=False)
     start_here = lax.dynamic_index_in_dim(start_p, t, axis=2, keepdims=False).astype(jnp.float32)
     first = jnp.sum(start_here * u_here, axis=(0, 2))
     second = jnp.sum(v_here * u_here, axis=(0, 2))
     pulled3 = jnp.einsum(
-        "spbc,sch->pbh", uv_pieces[:, :probes_n], w_out_p, preferred_element_type=jnp.float32
+        "spbc,sch->pbh", u_pieces, w_out_p, preferred_element_type=jnp.float32
     )
     scaled3 = (pulled3 * slope[None]).astype(jnp.bfloat16)
     part3 = jnp.einsum("pbh,sch->spbc", scaled3, w_in_p, preferred_element_type=jnp.float32)
-    third = jnp.sum(uv_pieces[:, probes_n:].astype(jnp.float32) * part3, axis=(0, 1, 3))
+    third = jnp.sum(v_pieces.astype(jnp.float32) * part3, axis=(0, 1, 3))
     coeffs = [(-1.0) ** k / (k + 1) for k in range(TERMS)]
     local_sum = coeffs[0] * first + coeffs[1] * second + coeffs[2] * third
     return psum_groups(local_sum), side

time: 303 us -> 305 us (level)
  waiting for transfers between devices: 79.9 us -> 62.3 us
  between operations: 0.95 us -> 14.3 us
  local copies, waits for them, and re-layouts: 50.3 us -> 54.3 us
    all_to_all x2, waiting for transfers between devices: 64.5 us -> 36.5 us  [all_gather_pieces(): lax.all_to_all(jnp.broadcast_to(piece[None], (n,) + piece.shape), 'tensor...]
    all_gather x0 -> x1, waiting for transfers between devices: none -> 10 us  [series(): v_pieces = lax.all_gather(uv_here[probes_n:], 'tensor', axis=0, tiled=False)]
    convert_element_type x0 -> x1, local copies, waits for them, and re-layouts: none -> 4.3 us  [series(): third = jnp.sum(v_pieces.astype(jnp.float32) * part3, axis=(0, 1, 3))]
  transfers between devices with their start and end apart: 21 -> 22, of which waited for: 7 -> 8; matrix products, arithmetic and copies ran while one was open for 21% -> 24% of each run, Pallas kernels for 0% -> 0%
where the time goes in v4:
time: 305 us; the launch traced here: 304 us
  blocking collectives  65.9 us (22%)
  waiting for transfers between devices  62.3 us (20%)
  local copies, waits for them, and re-layouts  54.3 us (18%)
  matrix products  48.8 us (16%)
  starting transfers between devices  40.6 us (13%)
  other arithmetic  17.8 us (6%)
  between operations  14.3 us (5%)
    all_to_all x1, blocking collectives, reduce_scatter_pieces(): received = lax.all_to_all(pieces.astype(jnp.bfloat16), 'tensor', 0, 0)  65.9 us
    all_to_all x2, waiting for transfers between devices, all_gather_pieces(): lax.all_to_all(jnp.broadcast_to(piece[None], (n,) + piece.shape), 'tensor...  36.5 us
    unnamed x36, local copies, waits for them, and re-layouts  33.4 us
    all_to_all x2, starting transfers between devices, all_gather_pieces(): lax.all_to_all(jnp.broadcast_to(piece[None], (n,) + piece.shape), 'tensor...  12.4 us
    all_gather x1, waiting for transfers between devices, series(): v_pieces = lax.all_gather(uv_here[probes_n:], 'tensor', axis=0, tiled=False)  10 us
    ppermute x6, starting transfers between devices, psum_groups(): lax.ppermute(value, 'tensor', [(t, t ^ k * step) for t in range(n)])  9.47 us
    ppermute x2, waiting for transfers between devices, gather_dp(): from_below = lax.ppermute(block, 'dp', up)  9.26 us
    dot_general x1, matrix products, series(): jnp.einsum('pbh,sch->spbc', scaled3, w_in_p, preferred_element_type=jnp.f...  8.84 us
  transfers between devices with their start and end apart: 22, of which 8 were waited for; matrix products, arithmetic and copies ran while one was open for 24% of the time, Pallas kernels for 0%

profile of v4, /device:TPU:0, one launch (start us, length us, event | category | flops | bytes accessed | tf_op | source)
XLA Modules:
  0.0 304.0 jit_solution(9629184102579019800)
XLA Ops:
  10.6 3.5 %copy.38 = bf16[16,8,32,256]{3,2,1,0:T(8,128)(2,1)} copy(bf16[16,8,32,256]{3,1,2,0:T(8,128)(2,1)} %bitcast.150) | data formatting | bytes 4194304
  14.1 5.3 %convert_bitcast_fusion.2 = bf16[16,128,2,256]{3,1,0,2:T(8,128)(2,1)} fusion(bf16[128,2,16,256]{3,2,1,0:T(8,128)(2,1)} %bitcast.145, bf16[128,4096]{1,0:T(8,128)(2,1)S(1)} %copy-done, bf16[4096,128]{1,0:T(8,128)(2,1)} %param.10), kind=kOutput, calls=%fused_computation.18 | convolution fusion | flops 403783680 | bytes 6291456 | tf_op jit(solution)/shard_map/bk,kmsc->sbmc/dot_general | solution.py:104
  19.4 3.1 %copy.29 = bf16[16,128,2,256]{3,1,2,0:T(8,128)(2,1)} copy(bf16[16,128,2,256]{3,1,0,2:T(8,128)(2,1)} %convert_bitcast_fusion.2) | data formatting | bytes 4194304 | tf_op jit(solution)/shard_map/convert_element_type | solution.py:42
  22.5 8.0 %all-to-all-start = ((bf16[16,128,2,256]{3,1,2,0:T(8,128)(2,1)}), bf16[16,128,2,256]{3,1,2,0:T(8,128)(2,1)}, u32[]{:S(2)}, u32[]{:S(2)}) async-start(bf16[16,128,2,256]{3,1,2,0:T(8,128)(2,1)} %copy.29), calls=%async_computation | async-start | bytes 4194304 | tf_op jit(solution)/shard_map/all_to_all | solution.py:42
  31.0 2.9 collective-permute-start.8
  40.9 3.1 %broadcast_select_fusion.1 = (bf16[512,1024]{1,0:T(8,128)(2,1)}, bf16[4096,1024]{1,0:T(8,128)(2,1)}) fusion(bf16[512,1024]{1,0:T(8,128)(2,1)S(1)} %collective-permute-done.1, bf16[512,1024]{1,0:T(8,128)(2,1)} %collective-permute-done.2, pred[]{:T(512)S(6)} %eq.9, bf16[4096,1024]{1,0:T(8,128)(2,1)} %constant_dynamic-update-slice_fusion.3), kind=kLoop, calls=%fused_computation.44 | loop fusion | flops 524288 | bytes 4194305 | tf_op jit(solution)/shard_map/jit(_where)/select_n | solution.py:28
  47.6 9.3 %collective-permute-done.7 = bf16[512,1024]{1,0:T(8,128)(2,1)S(1)} collective-permute-done((bf16[512,1024]{1,0:T(8,128)(2,1)}, bf16[512,1024]{1,0:T(8,128)(2,1)S(1)}, u32[]{:S(2)}, u32[]{:S(2)}) %collective-permute-start.7) | collective-permute-done | bytes 1048608 | tf_op jit(solution)/shard_map/ppermute | solution.py:23
  60.9 3.2 %copy-done.5 = bf16[4096,1024]{1,0:T(8,128)(2,1)} copy-done((bf16[4096,1024]{1,0:T(8,128)(2,1)}, bf16[4096,1024]{1,0:T(8,128)(2,1)S(1)}, u32[]{:S(2)}) %copy-start.5) | copy-done | bytes 8388632
  68.9 7.9 %all-to-all-start.1 = ((bf16[16,128,256]{2,1,0:T(8,128)(2,1)}), bf16[16,128,256]{2,1,0:T(8,128)(2,1)}, u32[]{:S(2)}, u32[]{:S(2)}) async-start(bf16[16,128,256]{2,1,0:T(8,128)(2,1)} %broadcast_in_dim.15), calls=%async_computation.1 | async-start | bytes 2097152 | tf_op jit(solution)/shard_map/all_to_all | solution.py:48
  77.1 4.1 %copy.30 = bf16[2,128,4096]{1,2,0:T(8,128)(2,1)} copy(bf16[2,128,4096]{2,1,0:T(8,128)(2,1)} %param.15) | data formatting | bytes 4194304 | tf_op args[6]
  81.1 2.9 copy.31
  93.5 4.1 %all-to-all-done.1 = bf16[16,128,256]{2,1,0:T(8,128)(2,1)} async-done(((bf16[16,128,256]{2,1,0:T(8,128)(2,1)}), bf16[16,128,256]{2,1,0:T(8,128)(2,1)}, u32[]{:S(2)}, u32[]{:S(2)}) %all-to-all-start.1) | async-done | bytes 1048608 | tf_op jit(solution)/shard_map/all_to_all | solution.py:48
  109.6 4.8 %multiply_subtract_fusion = (f32[128,1024]{1,0:T(8,128)S(1)}, bf16[128,1024]{1,0:T(8,128)(2,1)S(1)}) fusion(bf16[16,128,256]{2,1,0:T(8,128)(2,1)S(1)} %gather_fusion.1, bf16[16,256,1024]{2,1,0:T(8,128)(2,1)} %bitcast.9), kind=kOutput, calls=%fused_computation.45 | convolution fusion | flops 1074135040 | bytes 10223616 | tf_op jit(solution)/shard_map/sbc,sch->bh/dot_general | solution.py:110
  118.6 5.8 %fusion.34 = bf16[2,128,1024,1]{2,1,0,3:T(8,128)(2,1)S(1)} fusion(bf16[16,256,1024,1]{2,1,3,0:T(8,128)(2,1)} %bitcast.11, bf16[16,2,128,256]{3,2,1,0:T(8,128)(2,1)S(1)} %copy-done.2, f32[128,1024]{1,0:T(8,128)S(1)} %get-tuple-element.14), kind=kOutput, calls=%fused_computation.33 | convolution fusion | flops 2148007936 | bytes 11534336 | tf_op jit(solution)/shard_map/pbsc,sch->pbh/dot_general | solution.py:66
  124.4 8.1 %convert_bitcast_fusion.1 = bf16[16,2,128,256]{2,3,1,0:T(8,128)(2,1)S(1)} fusion(bf16[16,256,1024,1]{2,1,3,0:T(8,128)(2,1)} %bitcast.11, bf16[2,128,1024,1]{2,1,0,3:T(8,128)(2,1)S(1)} %fusion.31), kind=kOutput, calls=%fused_computation.17 | convolution fusion | flops 2148532224 | bytes 11010048 | tf_op jit(solution)/shard_map/pbh,sch->spbc/dot_general | solution.py:65
  132.5 3.7 %convert_bitcast_fusion = bf16[16,2,128,256]{2,3,1,0:T(8,128)(2,1)} fusion(bf16[16,256,1024,1]{2,1,3,0:T(8,128)(2,1)S(1)} %bitcast.152, bf16[2,128,1024,1]{2,1,0,3:T(8,128)(2,1)S(1)} %fusion.34), kind=kOutput, calls=%fused_computation.16 | convolution fusion | flops 2148532224 | bytes 11010048 | tf_op jit(solution)/shard_map/pbh,sch->spbc/dot_general | solution.py:68
  136.2 3.3 %convolution_bitcast_fusion = bf16[16,128,256]{1,2,0:T(8,128)(2,1)} fusion(bf16[16,256,1024]{2,1,0:T(8,128)(2,1)S(1)} %bitcast.153, bf16[128,1024]{1,0:T(8,128)(2,1)S(1)} %get-tuple-element.15), kind=kOutput, calls=%fused_computation.19 | convolution fusion | flops 1073741824 | bytes 9699328 | tf_op jit(solution)/shard_map/bh,sch->sbc/dot_general | solution.py:114
  143.7 65.9 %all_to_all.20 = bf16[16,5,128,256]{2,3,1,0:T(8,128)(2,1)S(1)} all-to-all(bf16[16,5,128,256]{2,3,1,0:T(8,128)(2,1)S(1)} %pad_maximum_fusion), channel_id=1, replica_groups=mesh['dp'=8,'tensor'=16] {'tensor'}, dimensions={0} | all-to-all | bytes 10485760 | tf_op jit(solution)/shard_map/all_to_all | solution.py:42
  213.2 4.4 %all-to-all-start.3 = ((bf16[16,2,128,256]{3,2,1,0:T(8,128)(2,1)}), bf16[16,2,128,256]{3,2,1,0:T(8,128)(2,1)}, u32[]{:S(2)}, u32[]{:S(2)}) async-start(bf16[16,2,128,256]{3,2,1,0:T(8,128)(2,1)} %broadcast_in_dim.18), calls=%async_computation.3 | async-start | bytes 4194304 | tf_op jit(solution)/shard_map/all_to_all | solution.py:48
  218.7 32.4 %all-to-all-done.3 = bf16[16,2,128,256]{3,2,1,0:T(8,128)(2,1)} async-done(((bf16[16,2,128,256]{3,2,1,0:T(8,128)(2,1)}), bf16[16,2,128,256]{3,2,1,0:T(8,128)(2,1)}, u32[]{:S(2)}, u32[]{:S(2)}) %all-to-all-start.3) | async-done | bytes 2097184 | tf_op jit(solution)/shard_map/all_to_all | solution.py:48
  251.1 6.5 %fusion.30 = bf16[2,128,1024,1]{2,1,0,3:T(8,128)(2,1)S(1)} fusion(bf16[16,2,128,256]{3,2,1,0:T(8,128)(2,1)} %all-to-all-done.3, bf16[16,256,1024,1]{2,1,3,0:T(8,128)(2,1)} %bitcast.154, f32[128,1024]{1,0:T(8,128)S(1)} %copy-done.4), kind=kOutput, calls=%fused_computation.31 | convolution fusion | flops 2148007936 | bytes 11534336 | tf_op jit(solution)/shard_map/spbc,sch->pbh/dot_general | solution.py:80
  257.7 10.0 %all-gather.3.cloned.1.call-done = bf16[32,128,256]{2,1,0:T(8,128)(2,1)} async-done(((bf16[2,128,256]{2,1,0:T(8,128)(2,1)}), bf16[32,128,256]{2,1,0:T(8,128)(2,1)}) %all-gather.3.cloned.1.call-update) | async-done | bytes 2097168 | tf_op jit(solution)/shard_map/all_gather | solution.py:76
  267.7 4.3 %copy.34 = f32[32,128,256]{1,2,0:T(8,128)} copy(bf16[32,128,256]{2,1,0:T(8,128)(2,1)} %all-gather.3.cloned.1.call-done) | data formatting | bytes 6291456 | tf_op jit(solution)/shard_map/convert_element_type | solution.py:85
  272.0 8.8 %fusion = f32[128]{0:T(128)S(1)} fusion(f32[16,2,128,256]{2,3,1,0:T(8,128)} %bitcast.148, bf16[16,256,1024,1]{2,1,3,0:T(8,128)(2,1)} %bitcast.11, bf16[2,128,1024,1]{2,1,0,3:T(8,128)(2,1)S(1)} %fusion.30), kind=kOutput, calls=%fused_computation.6 | convolution fusion | flops 2149580800 | bytes 13107712 | tf_op jit(solution)/shard_map/pbh,sch->spbc/dot_general | solution.py:84
  (100 shorter events, 74.1 us)
Async XLA Ops:
  7.2 29.1 %collective-permute-start = (bf16[512,1024]{1,0:T(8,128)(2,1)}, bf16[512,1024]{1,0:T(8,128)(2,1)}, u32[]{:S(2)}, u32[]{:S(2)}) collective-permute-start(bf16[512,1024]{1,0:T(8,128)(2,1)} %param.13), channel_id=1, source_target_pairs={{0,16},{16,0},{32,48},{48,32},{64,80},{80,64},{96,112},{112,96},{1... | collective-permute-start | bytes 3145736 | tf_op jit(solution)/shard_map/ppermute | solution.py:25
  7.3 32.6 %collective-permute-start.1 = (bf16[512,1024]{1,0:T(8,128)(2,1)}, bf16[512,1024]{1,0:T(8,128)(2,1)S(1)}, u32[]{:S(2)}, u32[]{:S(2)}) collective-permute-start(bf16[512,1024]{1,0:T(8,128)(2,1)} %param.13), channel_id=1, source_target_pairs={{0,32},{16,48},{32,64},{48,80},{64,96},{80,112},{96,0},{112,16},{1... | collective-permute-start | bytes 3145736 | tf_op jit(solution)/shard_map/ppermute | solution.py:23
  9.0 31.9 %collective-permute-start.2 = (bf16[512,1024]{1,0:T(8,128)(2,1)}, bf16[512,1024]{1,0:T(8,128)(2,1)}, u32[]{:S(2)}, u32[]{:S(2)}) collective-permute-start(bf16[512,1024]{1,0:T(8,128)(2,1)} %param.13), channel_id=1, source_target_pairs={{0,96},{16,112},{32,0},{48,16},{64,32},{80,48},{96,64},{112,80},{1... | collective-permute-start | bytes 3145736 | tf_op jit(solution)/shard_map/ppermute | solution.py:24
  22.5 43.2 %all-to-all-start = ((bf16[16,128,2,256]{3,1,2,0:T(8,128)(2,1)}), bf16[16,128,2,256]{3,1,2,0:T(8,128)(2,1)}, u32[]{:S(2)}, u32[]{:S(2)}) async-start(bf16[16,128,2,256]{3,1,2,0:T(8,128)(2,1)} %copy.29), calls=%async_computation | async-start | bytes 4194304 | tf_op jit(solution)/shard_map/all_to_all | solution.py:42
  30.6 26.3 %collective-permute-start.7 = (bf16[512,1024]{1,0:T(8,128)(2,1)}, bf16[512,1024]{1,0:T(8,128)(2,1)S(1)}, u32[]{:S(2)}, u32[]{:S(2)}) collective-permute-start(bf16[512,1024]{1,0:T(8,128)(2,1)} %param.14), channel_id=1, source_target_pairs={{0,32},{16,48},{32,64},{48,80},{64,96},{80,112},{96,0},{112,16},{1... | collective-permute-start | bytes 3145736 | tf_op jit(solution)/shard_map/ppermute | solution.py:23
  31.0 26.7 %collective-permute-start.8 = (bf16[512,1024]{1,0:T(8,128)(2,1)}, bf16[512,1024]{1,0:T(8,128)(2,1)S(1)}, u32[]{:S(2)}, u32[]{:S(2)}) collective-permute-start(bf16[512,1024]{1,0:T(8,128)(2,1)} %param.14), channel_id=1, source_target_pairs={{0,96},{16,112},{32,0},{48,16},{64,32},{80,48},{96,64},{112,80},{1... | collective-permute-start | bytes 3145736 | tf_op jit(solution)/shard_map/ppermute | solution.py:24
  36.2 23.0 %collective-permute-start.6 = (bf16[512,1024]{1,0:T(8,128)(2,1)}, bf16[512,1024]{1,0:T(8,128)(2,1)S(1)}, u32[]{:S(2)}, u32[]{:S(2)}) collective-permute-start(bf16[512,1024]{1,0:T(8,128)(2,1)} %param.14), channel_id=1, source_target_pairs={{0,16},{16,0},{32,48},{48,32},{64,80},{80,64},{96,112},{112,96},{1... | collective-permute-start | bytes 3145736 | tf_op jit(solution)/shard_map/ppermute | solution.py:25
  44.0 43.3 %collective-permute-start.3 = (bf16[512,1024]{1,0:T(8,128)(2,1)}, bf16[512,1024]{1,0:T(8,128)(2,1)}, u32[]{:S(2)}, u32[]{:S(2)}) collective-permute-start(bf16[512,1024]{1,0:T(8,128)(2,1)} %get-tuple-element.8), channel_id=1, source_target_pairs={{0,32},{16,112},{32,64},{48,16},{64,96},{80,48},{96,0},{112,80},{1... | collective-permute-start | bytes 3145736 | tf_op jit(solution)/shard_map/ppermute | solution.py:29
  46.8 52.6 %collective-permute-start.4 = (bf16[2,512,1024]{2,1,0:T(8,128)(2,1)}, bf16[2,512,1024]{2,1,0:T(8,128)(2,1)}, u32[]{:S(2)}, u32[]{:S(2)}) collective-permute-start(bf16[2,512,1024]{2,1,0:T(8,128)(2,1)} %pad_maximum_fusion.1), channel_id=1, source_target_pairs={{0,16},{16,0},{32,48},{48,32},{64,80},{80,64},{96,112},{112,96},{1... | collective-permute-start | bytes 6291464 | tf_op jit(solution)/shard_map/ppermute | solution.py:30
  59.3 44.7 %collective-permute-start.10 = (bf16[2,512,1024]{2,1,0:T(8,128)(2,1)}, bf16[2,512,1024]{2,1,0:T(8,128)(2,1)}, u32[]{:S(2)}, u32[]{:S(2)}) collective-permute-start(bf16[2,512,1024]{2,1,0:T(8,128)(2,1)} %pad_maximum_fusion.2), channel_id=1, source_target_pairs={{0,16},{16,0},{32,48},{48,32},{64,80},{80,64},{96,112},{112,96},{1... | collective-permute-start | bytes 6291464 | tf_op jit(solution)/shard_map/ppermute | solution.py:30
  64.1 24.5 %collective-permute-start.9 = (bf16[512,1024]{1,0:T(8,128)(2,1)}, bf16[512,1024]{1,0:T(8,128)(2,1)}, u32[]{:S(2)}, u32[]{:S(2)}) collective-permute-start(bf16[512,1024]{1,0:T(8,128)(2,1)} %get-tuple-element.10), channel_id=1, source_target_pairs={{0,32},{16,112},{32,64},{48,16},{64,96},{80,48},{96,0},{112,80},{1... | collective-permute-start | bytes 3145736 | tf_op jit(solution)/shard_map/ppermute | solution.py:29
  68.9 28.7 %all-to-all-start.1 = ((bf16[16,128,256]{2,1,0:T(8,128)(2,1)}), bf16[16,128,256]{2,1,0:T(8,128)(2,1)}, u32[]{:S(2)}, u32[]{:S(2)}) async-start(bf16[16,128,256]{2,1,0:T(8,128)(2,1)} %broadcast_in_dim.15), calls=%async_computation.1 | async-start | bytes 2097152 | tf_op jit(solution)/shard_map/all_to_all | solution.py:48
  76.8 190.9 %all-gather.3.cloned.1.call-start = ((), (), s32[]{:S(2)}) async-start(), calls=%async_computation.4 | async-start | bytes 2228224 | tf_op jit(solution)/shard_map/all_gather | solution.py:76
  87.3 19.0 %collective-permute-start.5 = (bf16[512,1024]{1,0:T(8,128)(2,1)}, bf16[512,1024]{1,0:T(8,128)(2,1)S(1)}, u32[]{:S(2)}, u32[]{:S(2)}) collective-permute-start(bf16[512,1024]{1,0:T(8,128)(2,1)} %collective-permute-done.3), channel_id=1, source_target_pairs={{0,16},{16,0},{32,48},{48,32},{64,80},{80,64},{96,112},{112,96},{1... | collective-permute-start | bytes 3145736 | tf_op jit(solution)/shard_map/ppermute | solution.py:31
  88.6 25.8 %collective-permute-start.11 = (bf16[512,1024]{1,0:T(8,128)(2,1)}, bf16[512,1024]{1,0:T(8,128)(2,1)S(1)}, u32[]{:S(2)}, u32[]{:S(2)}) collective-permute-start(bf16[512,1024]{1,0:T(8,128)(2,1)} %collective-permute-done.9), channel_id=1, source_target_pairs={{0,16},{16,0},{32,48},{48,32},{64,80},{80,64},{96,112},{112,96},{1... | collective-permute-start | bytes 3145736 | tf_op jit(solution)/shard_map/ppermute | solution.py:31
  209.6 41.5 %copy-start.4 = (f32[128,1024]{1,0:T(8,128)S(1)}, f32[128,1024]{1,0:T(8,128)}, u32[]{:S(2)}) copy-start(f32[128,1024]{1,0:T(8,128)} %copy-done.3) | copy-start | bytes 1572868
  213.2 37.9 %all-to-all-start.3 = ((bf16[16,2,128,256]{3,2,1,0:T(8,128)(2,1)}), bf16[16,2,128,256]{3,2,1,0:T(8,128)(2,1)}, u32[]{:S(2)}, u32[]{:S(2)}) async-start(bf16[16,2,128,256]{3,2,1,0:T(8,128)(2,1)} %broadcast_in_dim.18), calls=%async_computation.3 | async-start | bytes 4194304 | tf_op jit(solution)/shard_map/all_to_all | solution.py:48
  272.0 25.2 %copy-start.1 = (bf16[128,4096]{1,0:T(8,128)(2,1)S(1)}, bf16[128,4096]{1,0:T(8,128)(2,1)}, u32[]{:S(2)}) copy-start(bf16[128,4096]{1,0:T(8,128)(2,1)} %param.9) | copy-start | bytes 3145732
  280.8 4.8 %collective-permute-start.12 = (f32[128]{0:T(128)S(1)}, f32[128]{0:T(128)S(1)}, u32[]{:S(2)}, u32[]{:S(2)}) collective-permute-start(f32[128]{0:T(128)S(1)} %multiply_add_fusion), channel_id=1, source_target_pairs={{0,1},{1,0},{2,3},{3,2},{4,5},{5,4},{6,7},{7,6},{8,9},{9,8},{10,11... | collective-permute-start | bytes 1544 | tf_op jit(solution)/shard_map/ppermute | solution.py:55
  282.1 5.1 %collective-permute-start.13 = (f32[128]{0:T(128)S(1)}, f32[128]{0:T(128)S(1)}, u32[]{:S(2)}, u32[]{:S(2)}) collective-permute-start(f32[128]{0:T(128)S(1)} %multiply_add_fusion), channel_id=1, source_target_pairs={{0,2},{1,3},{2,0},{3,1},{4,6},{5,7},{6,4},{7,5},{8,10},{9,11},{10,... | collective-permute-start | bytes 1544 | tf_op jit(solution)/shard_map/ppermute | solution.py:55
  284.8 4.8 %collective-permute-start.14 = (f32[128]{0:T(128)S(1)}, f32[128]{0:T(128)S(1)}, u32[]{:S(2)}, u32[]{:S(2)}) collective-permute-start(f32[128]{0:T(128)S(1)} %multiply_add_fusion), channel_id=1, source_target_pairs={{0,3},{1,2},{2,1},{3,0},{4,7},{5,6},{6,5},{7,4},{8,11},{9,10},{10,... | collective-permute-start | bytes 1544 | tf_op jit(solution)/shard_map/ppermute | solution.py:55
  289.6 5.4 %collective-permute-start.15 = (f32[128]{0:T(128)S(1)}, f32[128]{0:T(128)S(1)}, u32[]{:S(2)}, u32[]{:S(2)}) collective-permute-start(f32[128]{0:T(128)S(1)} %add_add_fusion), channel_id=1, source_target_pairs={{0,4},{1,5},{2,6},{3,7},{4,0},{5,1},{6,2},{7,3},{8,12},{9,13},{10,... | collective-permute-start | bytes 1544 | tf_op jit(solution)/shard_map/ppermute | solution.py:55
  289.6 5.4 %collective-permute-start.16 = (f32[128]{0:T(128)S(1)}, f32[128]{0:T(128)S(1)}, u32[]{:S(2)}, u32[]{:S(2)}) collective-permute-start(f32[128]{0:T(128)S(1)} %add_add_fusion), channel_id=1, source_target_pairs={{0,8},{1,9},{2,10},{3,11},{4,12},{5,13},{6,14},{7,15},{8,0},{9,1},... | collective-permute-start | bytes 1544 | tf_op jit(solution)/shard_map/ppermute | solution.py:55
  291.9 4.8 %collective-permute-start.17 = (f32[128]{0:T(128)S(1)}, f32[128]{0:T(128)S(1)}, u32[]{:S(2)}, u32[]{:S(2)}) collective-permute-start(f32[128]{0:T(128)S(1)} %add_add_fusion), channel_id=1, source_target_pairs={{0,12},{1,13},{2,14},{3,15},{4,8},{5,9},{6,10},{7,11},{8,4},{9,5},... | collective-permute-start | bytes 1544 | tf_op jit(solution)/shard_map/ppermute | solution.py:55
  (9 other events, 106.4 us)
Sparse Core Ops, SparseCore 0:
  211.7 55.9 all-gather.2

commit v5 on v1

--- a/solution.py
+++ b/solution.py
@@ -19,6 +19,7 @@
     down = perm(lambda y, c: 2 * ((y - 1) % ny) + c)
     swap = perm(lambda y, c: 2 * y + 1 - c)
     fwd = perm(lambda y, c: 2 * ((y + 1) % ny) if c == 0 else 2 * ((y - 1) % ny) + 1)
+    fwd_cross = perm(lambda y, c: 2 * ((y + 1) % ny) + 1 if c == 0 else 2 * ((y - 1) % ny))
 
     from_below = lax.ppermute(block, "dp", up)
     from_above = lax.ppermute(block, "dp", down)
@@ -28,7 +29,7 @@
     relay = jnp.where(c == 0, from_below, from_above)
     far = lax.ppermute(relay, "dp", fwd)
     partner_near = lax.ppermute(jnp.stack([from_below, from_above]), "dp", swap)
-    partner_far = lax.ppermute(far, "dp", swap)
+    partner_far = lax.ppermute(relay, "dp", fwd_cross)
     joined = jnp.concatenate(
         [block, partner, from_below, from_above, far, partner_near[0], partner_near[1], partner_far]
     )

time: 303 us -> 308 us (1.017)
  waiting for transfers between devices: 79.9 us -> 83.6 us
    all_to_all x2, waiting for transfers between devices: 64.5 us -> 69.4 us  [all_gather_pieces(): lax.all_to_all(jnp.broadcast_to(piece[None], (n,) + piece.shape), 'tensor...]
  transfers between devices with their start and end apart: 21 -> 21, of which waited for: 7 -> 8; matrix products, arithmetic and copies ran while one was open for 21% -> 21% of each run, Pallas kernels for 0% -> 0%
where the time goes in v5:
time: 308 us; the launch traced here: 307 us
  waiting for transfers between devices  83.6 us (27%)
  blocking collectives  67 us (22%)
  local copies, waits for them, and re-layouts  50.3 us (16%)
  matrix products  46.3 us (15%)
  starting transfers between devices  40.8 us (13%)
  other arithmetic  17.8 us (6%)
    all_to_all x2, waiting for transfers between devices, all_gather_pieces(): lax.all_to_all(jnp.broadcast_to(piece[None], (n,) + piece.shape), 'tensor...  69.4 us
    all_to_all x1, blocking collectives, reduce_scatter_pieces(): received = lax.all_to_all(pieces.astype(jnp.bfloat16), 'tensor', 0, 0)  67 us
    unnamed x36, local copies, waits for them, and re-layouts  33.4 us
    all_to_all x2, starting transfers between devices, all_gather_pieces(): lax.all_to_all(jnp.broadcast_to(piece[None], (n,) + piece.shape), 'tensor...  12.5 us
    ppermute x6, starting transfers between devices, psum_groups(): lax.ppermute(value, 'tensor', [(t, t ^ k * step) for t in range(n)])  9.47 us
    ppermute x2, waiting for transfers between devices, gather_dp(): from_below = lax.ppermute(block, 'dp', up)  9.18 us
    dot_general x1, matrix products, series(): jnp.einsum('pbh,sch->spbc', scaled, w_in_p, preferred_element_type=jnp.fl...  8.12 us
    all_to_all x1, starting transfers between devices, reduce_scatter_pieces(): received = lax.all_to_all(pieces.astype(jnp.bfloat16), 'tensor', 0, 0)  8.04 us
  transfers between devices with their start and end apart: 21, of which 8 were waited for; matrix products, arithmetic and copies ran while one was open for 21% of the time, Pallas kernels for 0%

profile of v5, /device:TPU:0, one launch (start us, length us, event | category | flops | bytes accessed | tf_op | source)
XLA Modules:
  0.0 306.8 jit_solution(1273346422466721129)
XLA Ops:
  4.0 3.5 %copy.39 = bf16[16,8,32,256]{3,2,1,0:T(8,128)(2,1)} copy(bf16[16,8,32,256]{3,1,2,0:T(8,128)(2,1)} %bitcast.148) | data formatting | bytes 4194304
  7.6 5.3 %convert_bitcast_fusion.2 = bf16[16,128,2,256]{3,1,0,2:T(8,128)(2,1)} fusion(bf16[128,2,16,256]{3,2,1,0:T(8,128)(2,1)} %bitcast.144, bf16[128,4096]{1,0:T(8,128)(2,1)S(1)} %copy-done, bf16[4096,128]{1,0:T(8,128)(2,1)} %param.10), kind=kOutput, calls=%fused_computation.18 | convolution fusion | flops 403783680 | bytes 6291456 | tf_op jit(solution)/shard_map/bk,kmsc->sbmc/dot_general | solution.py:104
  12.8 3.2 %copy.29 = bf16[16,128,2,256]{3,1,2,0:T(8,128)(2,1)} copy(bf16[16,128,2,256]{3,1,0,2:T(8,128)(2,1)} %convert_bitcast_fusion.2) | data formatting | bytes 4194304 | tf_op jit(solution)/shard_map/convert_element_type | solution.py:43
  16.0 8.0 %all-to-all-start = ((bf16[16,128,2,256]{3,1,2,0:T(8,128)(2,1)}), bf16[16,128,2,256]{3,1,2,0:T(8,128)(2,1)}, u32[]{:S(2)}, u32[]{:S(2)}) async-start(bf16[16,128,2,256]{3,1,2,0:T(8,128)(2,1)} %copy.29), calls=%async_computation | async-start | bytes 4194304 | tf_op jit(solution)/shard_map/all_to_all | solution.py:43
  24.5 2.9 collective-permute-start.8
  34.4 3.2 %broadcast_select_fusion.1 = (bf16[512,1024]{1,0:T(8,128)(2,1)}, bf16[4096,1024]{1,0:T(8,128)(2,1)}) fusion(bf16[512,1024]{1,0:T(8,128)(2,1)S(1)} %collective-permute-done.1, bf16[512,1024]{1,0:T(8,128)(2,1)} %collective-permute-done.2, pred[]{:T(512)S(6)} %eq.9, bf16[4096,1024]{1,0:T(8,128)(2,1)} %constant_dynamic-update-slice_fusion.3), kind=kLoop, calls=%fused_computation.44 | loop fusion | flops 524288 | bytes 4194305 | tf_op jit(solution)/shard_map/jit(_where)/select_n | solution.py:29
  37.6 2.8 pad_maximum_fusion.1
  41.2 9.2 %collective-permute-done.7 = bf16[512,1024]{1,0:T(8,128)(2,1)S(1)} collective-permute-done((bf16[512,1024]{1,0:T(8,128)(2,1)}, bf16[512,1024]{1,0:T(8,128)(2,1)S(1)}, u32[]{:S(2)}, u32[]{:S(2)}) %collective-permute-start.7) | collective-permute-done | bytes 1048608 | tf_op jit(solution)/shard_map/ppermute | solution.py:24
  54.4 3.2 %copy-done.5 = bf16[4096,1024]{1,0:T(8,128)(2,1)} copy-done((bf16[4096,1024]{1,0:T(8,128)(2,1)}, bf16[4096,1024]{1,0:T(8,128)(2,1)S(1)}, u32[]{:S(2)}) %copy-start.5) | copy-done | bytes 8388632
  62.3 7.9 %all-to-all-start.1 = ((bf16[16,128,256]{2,1,0:T(8,128)(2,1)}), bf16[16,128,256]{2,1,0:T(8,128)(2,1)}, u32[]{:S(2)}, u32[]{:S(2)}) async-start(bf16[16,128,256]{2,1,0:T(8,128)(2,1)} %broadcast_in_dim.15), calls=%async_computation.1 | async-start | bytes 2097152 | tf_op jit(solution)/shard_map/all_to_all | solution.py:49
  70.4 4.1 %copy.30 = bf16[2,128,4096]{1,2,0:T(8,128)(2,1)} copy(bf16[2,128,4096]{2,1,0:T(8,128)(2,1)} %param.15) | data formatting | bytes 4194304 | tf_op args[6]
  74.5 2.9 copy.31
  87.1 3.9 %all-to-all-done.1 = bf16[16,128,256]{2,1,0:T(8,128)(2,1)} async-done(((bf16[16,128,256]{2,1,0:T(8,128)(2,1)}), bf16[16,128,256]{2,1,0:T(8,128)(2,1)}, u32[]{:S(2)}, u32[]{:S(2)}) %all-to-all-start.1) | async-done | bytes 1048608 | tf_op jit(solution)/shard_map/all_to_all | solution.py:49
  103.0 4.8 %multiply_subtract_fusion = (f32[128,1024]{1,0:T(8,128)S(1)}, bf16[128,1024]{1,0:T(8,128)(2,1)S(1)}) fusion(bf16[16,128,256]{2,1,0:T(8,128)(2,1)S(1)} %gather_fusion.1, bf16[16,256,1024]{2,1,0:T(8,128)(2,1)} %bitcast.9), kind=kOutput, calls=%fused_computation.45 | convolution fusion | flops 1074135040 | bytes 10223616 | tf_op jit(solution)/shard_map/sbc,sch->bh/dot_general | solution.py:110
  112.0 5.8 %fusion.34 = bf16[2,128,1024,1]{2,1,0,3:T(8,128)(2,1)S(1)} fusion(bf16[16,256,1024,1]{2,1,3,0:T(8,128)(2,1)} %bitcast.11, bf16[16,2,128,256]{3,2,1,0:T(8,128)(2,1)S(1)} %copy-done.2, f32[128,1024]{1,0:T(8,128)S(1)} %get-tuple-element.12), kind=kOutput, calls=%fused_computation.33 | convolution fusion | flops 2148007936 | bytes 11534336 | tf_op jit(solution)/shard_map/pbsc,sch->pbh/dot_general | solution.py:67
  117.8 8.1 %convert_bitcast_fusion.1 = bf16[16,2,128,256]{2,3,1,0:T(8,128)(2,1)S(1)} fusion(bf16[16,256,1024,1]{2,1,3,0:T(8,128)(2,1)} %bitcast.11, bf16[2,128,1024,1]{2,1,0,3:T(8,128)(2,1)S(1)} %fusion.31), kind=kOutput, calls=%fused_computation.17 | convolution fusion | flops 2148532224 | bytes 11010048 | tf_op jit(solution)/shard_map/pbh,sch->spbc/dot_general | solution.py:66
  125.9 3.6 %convert_bitcast_fusion = bf16[16,2,128,256]{2,3,1,0:T(8,128)(2,1)} fusion(bf16[16,256,1024,1]{2,1,3,0:T(8,128)(2,1)S(1)} %bitcast.150, bf16[2,128,1024,1]{2,1,0,3:T(8,128)(2,1)S(1)} %fusion.34), kind=kOutput, calls=%fused_computation.16 | convolution fusion | flops 2148532224 | bytes 11010048 | tf_op jit(solution)/shard_map/pbh,sch->spbc/dot_general | solution.py:69
  129.6 3.3 %convolution_bitcast_fusion = bf16[16,128,256]{1,2,0:T(8,128)(2,1)} fusion(bf16[16,256,1024]{2,1,0:T(8,128)(2,1)S(1)} %bitcast.151, bf16[128,1024]{1,0:T(8,128)(2,1)S(1)} %get-tuple-element.13), kind=kOutput, calls=%fused_computation.19 | convolution fusion | flops 1073741824 | bytes 9699328 | tf_op jit(solution)/shard_map/bh,sch->sbc/dot_general | solution.py:114
  137.1 67.0 %all_to_all.20 = bf16[16,5,128,256]{2,3,1,0:T(8,128)(2,1)S(1)} all-to-all(bf16[16,5,128,256]{2,3,1,0:T(8,128)(2,1)S(1)} %pad_maximum_fusion), channel_id=1, replica_groups=mesh['dp'=8,'tensor'=16] {'tensor'}, dimensions={0} | all-to-all | bytes 10485760 | tf_op jit(solution)/shard_map/all_to_all | solution.py:43
  207.9 4.5 %all-to-all-start.3 = ((bf16[16,4,128,256]{3,2,1,0:T(8,128)(2,1)}), bf16[16,4,128,256]{3,2,1,0:T(8,128)(2,1)}, u32[]{:S(2)}, u32[]{:S(2)}) async-start(bf16[16,4,128,256]{3,2,1,0:T(8,128)(2,1)} %broadcast_in_dim.18), calls=%async_computation.3 | async-start | bytes 8388608 | tf_op jit(solution)/shard_map/all_to_all | solution.py:49
  213.5 65.5 %all-to-all-done.3 = bf16[16,4,128,256]{3,2,1,0:T(8,128)(2,1)} async-done(((bf16[16,4,128,256]{3,2,1,0:T(8,128)(2,1)}), bf16[16,4,128,256]{3,2,1,0:T(8,128)(2,1)}, u32[]{:S(2)}, u32[]{:S(2)}) %all-to-all-start.3) | async-done | bytes 4194336 | tf_op jit(solution)/shard_map/all_to_all | solution.py:49
  279.0 6.4 %fusion.30 = bf16[2,128,1024,1]{2,1,0,3:T(8,128)(2,1)S(1)} fusion(bf16[16,4,128,256]{3,2,1,0:T(8,128)(2,1)} %all-to-all-done.3, bf16[16,256,1024,1]{2,1,3,0:T(8,128)(2,1)} %bitcast.152, f32[128,1024]{1,0:T(8,128)S(1)} %copy-done.4), kind=kOutput, calls=%fused_computation.31 | convolution fusion | flops 2148007936 | bytes 13631488 | tf_op jit(solution)/shard_map/spbc,sch->pbh/dot_general | solution.py:80
  285.4 6.6 %fusion = f32[128]{0:T(128)S(1)} fusion(bf16[16,256,1024,1]{2,1,3,0:T(8,128)(2,1)} %bitcast.11, bf16[2,128,1024,1]{2,1,0,3:T(8,128)(2,1)S(1)} %fusion.30, bf16[16,4,128,256]{3,2,1,0:T(8,128)(2,1)} %all-to-all-done.3), kind=kOutput, calls=%fused_computation.6 | convolution fusion | flops 2150629376 | bytes 11010560 | tf_op jit(solution)/shard_map/pbh,sch->spbc/dot_general | solution.py:84
  293.4 3.3 %collective-permute-start.14 = (f32[128]{0:T(128)S(1)}, f32[128]{0:T(128)S(1)}, u32[]{:S(2)}, u32[]{:S(2)}) collective-permute-start(f32[128]{0:T(128)S(1)} %multiply_add_fusion), channel_id=1, source_target_pairs={{0,3},{1,2},{2,1},{3,0},{4,7},{5,6},{6,5},{7,4},{8,11},{9,10},{10,... | collective-permute-start | bytes 1544 | tf_op jit(solution)/shard_map/ppermute | solution.py:56
  (96 shorter events, 66.8 us)
Async XLA Ops:
  0.6 29.1 %collective-permute-start = (bf16[512,1024]{1,0:T(8,128)(2,1)}, bf16[512,1024]{1,0:T(8,128)(2,1)}, u32[]{:S(2)}, u32[]{:S(2)}) collective-permute-start(bf16[512,1024]{1,0:T(8,128)(2,1)} %param.13), channel_id=1, source_target_pairs={{0,16},{16,0},{32,48},{48,32},{64,80},{80,64},{96,112},{112,96},{1... | collective-permute-start | bytes 3145736 | tf_op jit(solution)/shard_map/ppermute | solution.py:26
  0.7 32.6 %collective-permute-start.1 = (bf16[512,1024]{1,0:T(8,128)(2,1)}, bf16[512,1024]{1,0:T(8,128)(2,1)S(1)}, u32[]{:S(2)}, u32[]{:S(2)}) collective-permute-start(bf16[512,1024]{1,0:T(8,128)(2,1)} %param.13), channel_id=1, source_target_pairs={{0,32},{16,48},{32,64},{48,80},{64,96},{80,112},{96,0},{112,16},{1... | collective-permute-start | bytes 3145736 | tf_op jit(solution)/shard_map/ppermute | solution.py:24
  2.5 31.9 %collective-permute-start.2 = (bf16[512,1024]{1,0:T(8,128)(2,1)}, bf16[512,1024]{1,0:T(8,128)(2,1)}, u32[]{:S(2)}, u32[]{:S(2)}) collective-permute-start(bf16[512,1024]{1,0:T(8,128)(2,1)} %param.13), channel_id=1, source_target_pairs={{0,96},{16,112},{32,0},{48,16},{64,32},{80,48},{96,64},{112,80},{1... | collective-permute-start | bytes 3145736 | tf_op jit(solution)/shard_map/ppermute | solution.py:25
  16.0 43.1 %all-to-all-start = ((bf16[16,128,2,256]{3,1,2,0:T(8,128)(2,1)}), bf16[16,128,2,256]{3,1,2,0:T(8,128)(2,1)}, u32[]{:S(2)}, u32[]{:S(2)}) async-start(bf16[16,128,2,256]{3,1,2,0:T(8,128)(2,1)} %copy.29), calls=%async_computation | async-start | bytes 4194304 | tf_op jit(solution)/shard_map/all_to_all | solution.py:43
  24.1 26.3 %collective-permute-start.7 = (bf16[512,1024]{1,0:T(8,128)(2,1)}, bf16[512,1024]{1,0:T(8,128)(2,1)S(1)}, u32[]{:S(2)}, u32[]{:S(2)}) collective-permute-start(bf16[512,1024]{1,0:T(8,128)(2,1)} %param.14), channel_id=1, source_target_pairs={{0,32},{16,48},{32,64},{48,80},{64,96},{80,112},{96,0},{112,16},{1... | collective-permute-start | bytes 3145736 | tf_op jit(solution)/shard_map/ppermute | solution.py:24
  24.5 26.7 %collective-permute-start.8 = (bf16[512,1024]{1,0:T(8,128)(2,1)}, bf16[512,1024]{1,0:T(8,128)(2,1)S(1)}, u32[]{:S(2)}, u32[]{:S(2)}) collective-permute-start(bf16[512,1024]{1,0:T(8,128)(2,1)} %param.14), channel_id=1, source_target_pairs={{0,96},{16,112},{32,0},{48,16},{64,32},{80,48},{96,64},{112,80},{1... | collective-permute-start | bytes 3145736 | tf_op jit(solution)/shard_map/ppermute | solution.py:25
  29.7 23.0 %collective-permute-start.6 = (bf16[512,1024]{1,0:T(8,128)(2,1)}, bf16[512,1024]{1,0:T(8,128)(2,1)S(1)}, u32[]{:S(2)}, u32[]{:S(2)}) collective-permute-start(bf16[512,1024]{1,0:T(8,128)(2,1)} %param.14), channel_id=1, source_target_pairs={{0,16},{16,0},{32,48},{48,32},{64,80},{80,64},{96,112},{112,96},{1... | collective-permute-start | bytes 3145736 | tf_op jit(solution)/shard_map/ppermute | solution.py:26
  37.6 43.1 %collective-permute-start.3 = (bf16[512,1024]{1,0:T(8,128)(2,1)}, bf16[512,1024]{1,0:T(8,128)(2,1)}, u32[]{:S(2)}, u32[]{:S(2)}) collective-permute-start(bf16[512,1024]{1,0:T(8,128)(2,1)} %get-tuple-element.8), channel_id=1, source_target_pairs={{0,32},{16,112},{32,64},{48,16},{64,96},{80,48},{96,0},{112,80},{1... | collective-permute-start | bytes 3145736 | tf_op jit(solution)/shard_map/ppermute | solution.py:30
  40.4 52.5 %collective-permute-start.4 = (bf16[2,512,1024]{2,1,0:T(8,128)(2,1)}, bf16[2,512,1024]{2,1,0:T(8,128)(2,1)}, u32[]{:S(2)}, u32[]{:S(2)}) collective-permute-start(bf16[2,512,1024]{2,1,0:T(8,128)(2,1)} %pad_maximum_fusion.1), channel_id=1, source_target_pairs={{0,16},{16,0},{32,48},{48,32},{64,80},{80,64},{96,112},{112,96},{1... | collective-permute-start | bytes 6291464 | tf_op jit(solution)/shard_map/ppermute | solution.py:31
  52.8 44.6 %collective-permute-start.10 = (bf16[2,512,1024]{2,1,0:T(8,128)(2,1)}, bf16[2,512,1024]{2,1,0:T(8,128)(2,1)}, u32[]{:S(2)}, u32[]{:S(2)}) collective-permute-start(bf16[2,512,1024]{2,1,0:T(8,128)(2,1)} %pad_maximum_fusion.2), channel_id=1, source_target_pairs={{0,16},{16,0},{32,48},{48,32},{64,80},{80,64},{96,112},{112,96},{1... | collective-permute-start | bytes 6291464 | tf_op jit(solution)/shard_map/ppermute | solution.py:31
  57.6 27.2 %collective-permute-start.9 = (bf16[512,1024]{1,0:T(8,128)(2,1)}, bf16[512,1024]{1,0:T(8,128)(2,1)}, u32[]{:S(2)}, u32[]{:S(2)}) collective-permute-start(bf16[512,1024]{1,0:T(8,128)(2,1)} %get-tuple-element.10), channel_id=1, source_target_pairs={{0,32},{16,112},{32,64},{48,16},{64,96},{80,48},{96,0},{112,80},{1... | collective-permute-start | bytes 3145736 | tf_op jit(solution)/shard_map/ppermute | solution.py:30
  62.3 28.7 %all-to-all-start.1 = ((bf16[16,128,256]{2,1,0:T(8,128)(2,1)}), bf16[16,128,256]{2,1,0:T(8,128)(2,1)}, u32[]{:S(2)}, u32[]{:S(2)}) async-start(bf16[16,128,256]{2,1,0:T(8,128)(2,1)} %broadcast_in_dim.15), calls=%async_computation.1 | async-start | bytes 2097152 | tf_op jit(solution)/shard_map/all_to_all | solution.py:49
  80.7 19.0 %collective-permute-start.5 = (bf16[512,1024]{1,0:T(8,128)(2,1)}, bf16[512,1024]{1,0:T(8,128)(2,1)S(1)}, u32[]{:S(2)}, u32[]{:S(2)}) collective-permute-start(bf16[512,1024]{1,0:T(8,128)(2,1)} %get-tuple-element.8), channel_id=1, source_target_pairs={{0,48},{16,96},{32,80},{48,0},{64,112},{80,32},{96,16},{112,64},{1... | collective-permute-start | bytes 3145736 | tf_op jit(solution)/shard_map/ppermute | solution.py:32
  80.7 27.1 %collective-permute-start.11 = (bf16[512,1024]{1,0:T(8,128)(2,1)}, bf16[512,1024]{1,0:T(8,128)(2,1)S(1)}, u32[]{:S(2)}, u32[]{:S(2)}) collective-permute-start(bf16[512,1024]{1,0:T(8,128)(2,1)} %get-tuple-element.10), channel_id=1, source_target_pairs={{0,48},{16,96},{32,80},{48,0},{64,112},{80,32},{96,16},{112,64},{1... | collective-permute-start | bytes 3145736 | tf_op jit(solution)/shard_map/ppermute | solution.py:32
  108.9 20.7 %copy-start.7 = (bf16[4096,1024]{1,0:T(8,128)(2,1)}, bf16[4096,1024]{1,0:T(8,128)(2,1)S(1)}, u32[]{:S(2)}) copy-start(bf16[4096,1024]{1,0:T(8,128)(2,1)S(1)} %constant_dynamic-update-slice_fusion.6) | copy-start | bytes 25165828
  205.1 73.9 %copy-start.4 = (f32[128,1024]{1,0:T(8,128)S(1)}, f32[128,1024]{1,0:T(8,128)}, u32[]{:S(2)}) copy-start(f32[128,1024]{1,0:T(8,128)} %copy-done.3) | copy-start | bytes 1572868
  207.9 71.1 %all-to-all-start.3 = ((bf16[16,4,128,256]{3,2,1,0:T(8,128)(2,1)}), bf16[16,4,128,256]{3,2,1,0:T(8,128)(2,1)}, u32[]{:S(2)}, u32[]{:S(2)}) async-start(bf16[16,4,128,256]{3,2,1,0:T(8,128)(2,1)} %broadcast_in_dim.18), calls=%async_computation.3 | async-start | bytes 8388608 | tf_op jit(solution)/shard_map/all_to_all | solution.py:49
  278.9 27.9 %copy-start.1 = (bf16[128,4096]{1,0:T(8,128)(2,1)S(1)}, bf16[128,4096]{1,0:T(8,128)(2,1)}, u32[]{:S(2)}) copy-start(bf16[128,4096]{1,0:T(8,128)(2,1)} %param.9) | copy-start | bytes 3145732
  292.0 4.8 %collective-permute-start.12 = (f32[128]{0:T(128)S(1)}, f32[128]{0:T(128)S(1)}, u32[]{:S(2)}, u32[]{:S(2)}) collective-permute-start(f32[128]{0:T(128)S(1)} %multiply_add_fusion), channel_id=1, source_target_pairs={{0,1},{1,0},{2,3},{3,2},{4,5},{5,4},{6,7},{7,6},{8,9},{9,8},{10,11... | collective-permute-start | bytes 1544 | tf_op jit(solution)/shard_map/ppermute | solution.py:56
  292.1 5.2 %collective-permute-start.13 = (f32[128]{0:T(128)S(1)}, f32[128]{0:T(128)S(1)}, u32[]{:S(2)}, u32[]{:S(2)}) collective-permute-start(f32[128]{0:T(128)S(1)} %multiply_add_fusion), channel_id=1, source_target_pairs={{0,2},{1,3},{2,0},{3,1},{4,6},{5,7},{6,4},{7,5},{8,10},{9,11},{10,... | collective-permute-start | bytes 1544 | tf_op jit(solution)/shard_map/ppermute | solution.py:56
  293.4 4.9 %collective-permute-start.14 = (f32[128]{0:T(128)S(1)}, f32[128]{0:T(128)S(1)}, u32[]{:S(2)}, u32[]{:S(2)}) collective-permute-start(f32[128]{0:T(128)S(1)} %multiply_add_fusion), channel_id=1, source_target_pairs={{0,3},{1,2},{2,1},{3,0},{4,7},{5,6},{6,5},{7,4},{8,11},{9,10},{10,... | collective-permute-start | bytes 1544 | tf_op jit(solution)/shard_map/ppermute | solution.py:56
  298.3 5.4 %collective-permute-start.15 = (f32[128]{0:T(128)S(1)}, f32[128]{0:T(128)S(1)}, u32[]{:S(2)}, u32[]{:S(2)}) collective-permute-start(f32[128]{0:T(128)S(1)} %add_add_fusion), channel_id=1, source_target_pairs={{0,4},{1,5},{2,6},{3,7},{4,0},{5,1},{6,2},{7,3},{8,12},{9,13},{10,... | collective-permute-start | bytes 1544 | tf_op jit(solution)/shard_map/ppermute | solution.py:56
  298.8 5.1 %collective-permute-start.16 = (f32[128]{0:T(128)S(1)}, f32[128]{0:T(128)S(1)}, u32[]{:S(2)}, u32[]{:S(2)}) collective-permute-start(f32[128]{0:T(128)S(1)} %add_add_fusion), channel_id=1, source_target_pairs={{0,8},{1,9},{2,10},{3,11},{4,12},{5,13},{6,14},{7,15},{8,0},{9,1},... | collective-permute-start | bytes 1544 | tf_op jit(solution)/shard_map/ppermute | solution.py:56
  301.5 4.8 %collective-permute-start.17 = (f32[128]{0:T(128)S(1)}, f32[128]{0:T(128)S(1)}, u32[]{:S(2)}, u32[]{:S(2)}) collective-permute-start(f32[128]{0:T(128)S(1)} %add_add_fusion), channel_id=1, source_target_pairs={{0,12},{1,13},{2,14},{3,15},{4,8},{5,9},{6,10},{7,11},{8,4},{9,5},... | collective-permute-start | bytes 1544 | tf_op jit(solution)/shard_map/ppermute | solution.py:56
  (8 other events, 85.3 us)

commit v6 on v1

--- a/solution.py
+++ b/solution.py
@@ -27,7 +27,7 @@
     y, c = d // 2, d % 2
     relay = jnp.where(c == 0, from_below, from_above)
     far = lax.ppermute(relay, "dp", fwd)
-    partner_near = lax.ppermute(jnp.stack([from_below, from_above]), "dp", swap)
+    partner_near = [lax.ppermute(from_below, "dp", swap), lax.ppermute(from_above, "dp", swap)]
     partner_far = lax.ppermute(far, "dp", swap)
     joined = jnp.concatenate(
         [block, partner, from_below, from_above, far, partner_near[0], partner_near[1], partner_far]
@@ -48,14 +48,10 @@
     return lax.all_to_all(jnp.broadcast_to(piece[None], (n,) + piece.shape), "tensor", 0, 0)
 
 
-def psum_groups(value):
+def psum_a2a(value):
     n = lax.axis_size("tensor")
-    step = 1
-    while step < n:
-        others = [lax.ppermute(value, "tensor", [(t, t ^ (k * step)) for t in range(n)]) for k in (1, 2, 3)]
-        value = (value + others[0]) + (others[1] + others[2])
-        step *= 4
-    return value
+    received = lax.all_to_all(jnp.broadcast_to(value[None], (n,) + value.shape), "tensor", 0, 0)
+    return jnp.sum(received, axis=0)
 
 
 def series(start_p, w_in_p, w_out_p, slope, side):
@@ -84,7 +80,7 @@
     third = jnp.sum(uv_pieces[:, probes_n:].astype(jnp.float32) * part3, axis=(0, 1, 3))
     coeffs = [(-1.0) ** k / (k + 1) for k in range(TERMS)]
     local_sum = coeffs[0] * first + coeffs[1] * second + coeffs[2] * third
-    return psum_groups(local_sum), side
+    return psum_a2a(local_sum), side
 
 
 def local(features, enc_in, enc_out, noise, in_weight, out_weight, probes):

time: 303 us -> 307 us (1.013)
  starting transfers between devices: 40.6 us -> 33.4 us
  waiting for transfers between devices: 79.9 us -> 84.4 us
  blocking collectives: 65.9 us -> 70.1 us
  other arithmetic: 17.7 us -> 13.8 us
    ppermute x8 -> x4, starting transfers between devices: 10.3 us -> 0.83 us  [the longest x2 0.65 us: gather_dp(): lax.ppermute(from_above, 'dp', swap)]
    all_to_all x0 -> x1, waiting for transfers between devices: none -> 6.91 us  [psum_a2a(): lax.all_to_all(jnp.broadcast_to(value[None], (n,) + value.shape), 'tensor...]
    ppermute x2, waiting for transfers between devices: 0.01 us -> 6.3 us  [gather_dp(): far = lax.ppermute(relay, 'dp', fwd)]
    dot_general x1, matrix products: 8.12 us -> 2.63 us  [series(): jnp.einsum('pbh,sch->spbc', scaled, w_in_p, preferred_element_type=jnp.fl...]
    dot_general x1, matrix products: 3.64 us -> 9.12 us  [series(): jnp.einsum('pbh,sch->spbc', scaled_t, w_out_p, preferred_element_type=jnp...]
    ppermute x8 -> x4, waiting for transfers between devices: 5.17 us -> 0.01 us  [the longest x2 0.01 us: gather_dp(): lax.ppermute(from_below, 'dp', swap)]
    all_to_all x0 -> x1, starting transfers between devices: none -> 4.62 us  [psum_a2a(): lax.all_to_all(jnp.broadcast_to(value[None], (n,) + value.shape), 'tensor...]
    all_to_all x2, waiting for transfers between devices: 64.5 us -> 60 us  [all_gather_pieces(): lax.all_to_all(jnp.broadcast_to(piece[None], (n,) + piece.shape), 'tensor...]
  transfers between devices with their start and end apart: 21 -> 18, of which waited for: 7 -> 5; matrix products, arithmetic and copies ran while one was open for 21% -> 22% of each run, Pallas kernels for 0% -> 0%
where the time goes in v6:
time: 307 us; the launch traced here: 304 us
  waiting for transfers between devices  84.4 us (27%)
  blocking collectives  70.1 us (23%)
  local copies, waits for them, and re-layouts  53.3 us (17%)
  matrix products  48.5 us (16%)
  starting transfers between devices  33.4 us (11%)
  other arithmetic  13.8 us (4%)
    all_to_all x1, blocking collectives, reduce_scatter_pieces(): received = lax.all_to_all(pieces.astype(jnp.bfloat16), 'tensor', 0, 0)  70.1 us
    all_to_all x2, waiting for transfers between devices, all_gather_pieces(): lax.all_to_all(jnp.broadcast_to(piece[None], (n,) + piece.shape), 'tensor...  60 us
    unnamed x34, local copies, waits for them, and re-layouts  35.1 us
    all_to_all x2, starting transfers between devices, all_gather_pieces(): lax.all_to_all(jnp.broadcast_to(piece[None], (n,) + piece.shape), 'tensor...  12.5 us
    ppermute x2, waiting for transfers between devices, gather_dp(): from_below = lax.ppermute(block, 'dp', up)  11.2 us
    dot_general x1, matrix products, series(): jnp.einsum('pbh,sch->spbc', scaled_t, w_out_p, preferred_element_type=jnp...  9.12 us
    all_to_all x1, starting transfers between devices, reduce_scatter_pieces(): received = lax.all_to_all(pieces.astype(jnp.bfloat16), 'tensor', 0, 0)  7.88 us
    all_to_all x1, waiting for transfers between devices, psum_a2a(): lax.all_to_all(jnp.broadcast_to(value[None], (n,) + value.shape), 'tensor...  6.91 us
  transfers between devices with their start and end apart: 18, of which 5 were waited for; matrix products, arithmetic and copies ran while one was open for 22% of the time, Pallas kernels for 0%

profile of v6, /device:TPU:0, one launch (start us, length us, event | category | flops | bytes accessed | tf_op | source)
XLA Modules:
  0.0 304.5 jit_solution(1117726944767095946)
XLA Ops:
  4.5 3.5 %copy.54 = bf16[16,8,32,256]{3,2,1,0:T(8,128)(2,1)} copy(bf16[16,8,32,256]{3,1,2,0:T(8,128)(2,1)} %bitcast.132) | data formatting | bytes 4194304
  8.1 3.9 %convert_bitcast_fusion.2 = bf16[16,128,2,256]{3,1,0,2:T(8,128)(2,1)S(1)} fusion(bf16[128,2,16,256]{3,2,1,0:T(8,128)(2,1)} %bitcast.129, bf16[128,4096]{1,0:T(8,128)(2,1)S(1)} %copy-done, bf16[4096,128]{1,0:T(8,128)(2,1)} %param.10), kind=kOutput, calls=%fused_computation.16 | convolution fusion | flops 403783680 | bytes 6291456 | tf_op jit(solution)/shard_map/bk,kmsc->sbmc/dot_general | solution.py:99
  13.5 7.9 %all-to-all-start = ((bf16[16,128,2,256]{3,1,2,0:T(8,128)(2,1)}), bf16[16,128,2,256]{3,1,2,0:T(8,128)(2,1)S(1)}, u32[]{:S(2)}, u32[]{:S(2)}) async-start(bf16[16,128,2,256]{3,1,2,0:T(8,128)(2,1)} %copy.43), calls=%async_computation | async-start | bytes 4194304 | tf_op jit(solution)/shard_map/all_to_all | solution.py:42
  21.4 2.9 collective-permute-start.9
  33.6 3.4 %broadcast_select_fusion.1 = (bf16[512,1024]{1,0:T(8,128)(2,1)}, bf16[4096,1024]{1,0:T(8,128)(2,1)}) fusion(bf16[512,1024]{1,0:T(8,128)(2,1)} %collective-permute-done.1, bf16[512,1024]{1,0:T(8,128)(2,1)} %collective-permute-done.2, pred[]{:T(512)S(6)} %eq.9, bf16[4096,1024]{1,0:T(8,128)(2,1)} %constant_dynamic-update-slice_fusion.5), kind=kLoop, calls=%fused_computation.34 | loop fusion | flops 524288 | bytes 4194305 | tf_op jit(solution)/shard_map/jit(_where)/select_n | solution.py:28
  39.3 11.2 %collective-permute-done.8 = bf16[512,1024]{1,0:T(8,128)(2,1)} collective-permute-done((bf16[512,1024]{1,0:T(8,128)(2,1)}, bf16[512,1024]{1,0:T(8,128)(2,1)}, u32[]{:S(2)}, u32[]{:S(2)}) %collective-permute-start.8) | collective-permute-done | bytes 1048608 | tf_op jit(solution)/shard_map/ppermute | solution.py:23
  52.8 3.1 %broadcast_select_fusion = (bf16[512,1024]{1,0:T(8,128)(2,1)}, bf16[4096,1024]{1,0:T(8,128)(2,1)}) fusion(bf16[512,1024]{1,0:T(8,128)(2,1)} %collective-permute-done.8, bf16[512,1024]{1,0:T(8,128)(2,1)S(1)} %collective-permute-done.9, pred[]{:T(512)S(6)} %eq.9, bf16[4096,1024]{1,0:T(8,128)(2,1)} %constant_dynamic-update-slice_fusion.13), kind=kLoop, calls=%fused_computation.33 | loop fusion | flops 524288 | bytes 4194305 | tf_op jit(solution)/shard_map/jit(_where)/select_n | solution.py:28
  57.4 4.3 %collective-permute-done.3 = bf16[512,1024]{1,0:T(8,128)(2,1)} collective-permute-done((bf16[512,1024]{1,0:T(8,128)(2,1)}, bf16[512,1024]{1,0:T(8,128)(2,1)}, u32[]{:S(2)}, u32[]{:S(2)}) %collective-permute-start.3) | collective-permute-done | bytes 1048608 | tf_op jit(solution)/shard_map/ppermute | solution.py:29
  63.0 7.9 %all-to-all-start.1 = ((bf16[16,128,256]{2,1,0:T(8,128)(2,1)}), bf16[16,128,256]{2,1,0:T(8,128)(2,1)}, u32[]{:S(2)}, u32[]{:S(2)}) async-start(bf16[16,128,256]{2,1,0:T(8,128)(2,1)} %broadcast_in_dim.17), calls=%async_computation.1 | async-start | bytes 2097152 | tf_op jit(solution)/shard_map/all_to_all | solution.py:48
  73.1 4.1 %copy.44 = bf16[2,128,4096]{1,2,0:T(8,128)(2,1)} copy(bf16[2,128,4096]{2,1,0:T(8,128)(2,1)} %param.15) | data formatting | bytes 4194304 | tf_op args[6]
  77.1 2.9 copy.45
  101.6 4.8 %multiply_subtract_fusion = (f32[128,1024]{1,0:T(8,128)S(1)}, bf16[128,1024]{1,0:T(8,128)(2,1)S(1)}) fusion(bf16[16,128,256]{2,1,0:T(8,128)(2,1)S(1)} %gather_fusion.1, bf16[16,256,1024]{2,1,0:T(8,128)(2,1)} %bitcast.123), kind=kOutput, calls=%fused_computation.35 | convolution fusion | flops 1074135040 | bytes 10223616 | tf_op jit(solution)/shard_map/sbc,sch->bh/dot_general | solution.py:105
  107.6 5.9 %fusion.31 = bf16[2,128,1024,1]{2,1,0,3:T(8,128)(2,1)S(1)} fusion(bf16[16,256,1024,1]{2,1,3,0:T(8,128)(2,1)} %bitcast.12, bf16[16,2,128,256]{3,2,1,0:T(8,128)(2,1)S(1)} %copy-done.2, f32[128,1024]{1,0:T(8,128)S(1)} %get-tuple-element.12), kind=kOutput, calls=%fused_computation.30 | convolution fusion | flops 2148007936 | bytes 11534336 | tf_op jit(solution)/shard_map/pbsc,sch->pbh/dot_general | solution.py:59
  115.9 2.6 convert_bitcast_fusion.1
  118.6 9.1 %convert_bitcast_fusion = bf16[16,2,128,256]{2,3,1,0:T(8,128)(2,1)} fusion(bf16[16,256,1024,1]{2,1,3,0:T(8,128)(2,1)} %bitcast.12, bf16[2,128,1024,1]{2,1,0,3:T(8,128)(2,1)S(1)} %fusion.34), kind=kOutput, calls=%fused_computation.14 | convolution fusion | flops 2148532224 | bytes 11010048 | tf_op jit(solution)/shard_map/pbh,sch->spbc/dot_general | solution.py:64
  127.7 6.7 %convolution_bitcast_fusion = bf16[16,128,256]{1,2,0:T(8,128)(2,1)} fusion(bf16[16,256,1024]{2,1,0:T(8,128)(2,1)} %bitcast.10, bf16[128,1024]{1,0:T(8,128)(2,1)S(1)} %get-tuple-element.13), kind=kOutput, calls=%fused_computation.17 | convolution fusion | flops 1073741824 | bytes 9699328 | tf_op jit(solution)/shard_map/bh,sch->sbc/dot_general | solution.py:109
  138.6 70.1 %all_to_all.26 = bf16[16,5,128,256]{2,3,1,0:T(8,128)(2,1)S(1)} all-to-all(bf16[16,5,128,256]{2,3,1,0:T(8,128)(2,1)S(1)} %pad_maximum_fusion), channel_id=1, replica_groups=mesh['dp'=8,'tensor'=16] {'tensor'}, dimensions={0} | all-to-all | bytes 10485760 | tf_op jit(solution)/shard_map/all_to_all | solution.py:42
  210.0 2.6 broadcast_in_dim.20
  212.6 4.5 %all-to-all-start.3 = ((bf16[16,4,128,256]{3,2,1,0:T(8,128)(2,1)}), bf16[16,4,128,256]{3,2,1,0:T(8,128)(2,1)}, u32[]{:S(2)}, u32[]{:S(2)}) async-start(bf16[16,4,128,256]{3,2,1,0:T(8,128)(2,1)} %broadcast_in_dim.20), calls=%async_computation.3 | async-start | bytes 8388608 | tf_op jit(solution)/shard_map/all_to_all | solution.py:48
  218.1 60.0 %all-to-all-done.3 = bf16[16,4,128,256]{3,2,1,0:T(8,128)(2,1)} async-done(((bf16[16,4,128,256]{3,2,1,0:T(8,128)(2,1)}), bf16[16,4,128,256]{3,2,1,0:T(8,128)(2,1)}, u32[]{:S(2)}, u32[]{:S(2)}) %all-to-all-start.3) | async-done | bytes 4194336 | tf_op jit(solution)/shard_map/all_to_all | solution.py:48
  278.1 6.4 %fusion.30 = bf16[2,128,1024,1]{2,1,0,3:T(8,128)(2,1)S(1)} fusion(bf16[16,4,128,256]{3,2,1,0:T(8,128)(2,1)} %all-to-all-done.3, bf16[16,256,1024,1]{2,1,3,0:T(8,128)(2,1)} %bitcast.12, f32[128,1024]{1,0:T(8,128)S(1)} %copy-done.4), kind=kOutput, calls=%fused_computation.29 | convolution fusion | flops 2148007936 | bytes 13631488 | tf_op jit(solution)/shard_map/spbc,sch->pbh/dot_general | solution.py:75
  284.5 6.6 %fusion = f32[128]{0:T(128)S(1)} fusion(bf16[16,256,1024,1]{2,1,3,0:T(8,128)(2,1)} %bitcast.124, bf16[2,128,1024,1]{2,1,0,3:T(8,128)(2,1)S(1)} %fusion.30, bf16[16,4,128,256]{3,2,1,0:T(8,128)(2,1)} %all-to-all-done.3), kind=kOutput, calls=%fused_computation.6 | convolution fusion | flops 2150629376 | bytes 11010560 | tf_op jit(solution)/shard_map/pbh,sch->spbc/dot_general | solution.py:79
  291.7 4.6 %all-to-all-start.4 = ((f32[16,1,128]{2,1,0:T(1,128)}), f32[16,1,128]{2,1,0:T(1,128)S(1)}, u32[]{:S(2)}, u32[]{:S(2)}) async-start(f32[16,1,128]{2,1,0:T(1,128)} %broadcast_in_dim.21), calls=%async_computation.4 | async-start | bytes 16384 | tf_op jit(solution)/shard_map/all_to_all | solution.py:53
  297.0 6.9 %all-to-all-done.4 = f32[16,1,128]{2,1,0:T(1,128)S(1)} async-done(((f32[16,1,128]{2,1,0:T(1,128)}), f32[16,1,128]{2,1,0:T(1,128)S(1)}, u32[]{:S(2)}, u32[]{:S(2)}) %all-to-all-start.4) | async-done | bytes 8224 | tf_op jit(solution)/shard_map/all_to_all | solution.py:53
  (88 shorter events, 57.5 us)
Async XLA Ops:
  0.6 7.4 %copy-start = (bf16[128,4096]{1,0:T(8,128)(2,1)S(1)}, bf16[128,4096]{1,0:T(8,128)(2,1)}, u32[]{:S(2)}) copy-start(bf16[128,4096]{1,0:T(8,128)(2,1)} %param.9) | copy-start | bytes 3145732
  0.6 20.7 %collective-permute-start = (bf16[512,1024]{1,0:T(8,128)(2,1)}, bf16[512,1024]{1,0:T(8,128)(2,1)}, u32[]{:S(2)}, u32[]{:S(2)}) collective-permute-start(bf16[512,1024]{1,0:T(8,128)(2,1)} %param.13), channel_id=1, source_target_pairs={{0,16},{16,0},{32,48},{48,32},{64,80},{80,64},{96,112},{112,96},{1... | collective-permute-start | bytes 3145736 | tf_op jit(solution)/shard_map/ppermute | solution.py:25
  0.7 30.5 %collective-permute-start.1 = (bf16[512,1024]{1,0:T(8,128)(2,1)}, bf16[512,1024]{1,0:T(8,128)(2,1)}, u32[]{:S(2)}, u32[]{:S(2)}) collective-permute-start(bf16[512,1024]{1,0:T(8,128)(2,1)} %param.13), channel_id=1, source_target_pairs={{0,32},{16,48},{32,64},{48,80},{64,96},{80,112},{96,0},{112,16},{1... | collective-permute-start | bytes 3145736 | tf_op jit(solution)/shard_map/ppermute | solution.py:23
  2.5 31.1 %collective-permute-start.2 = (bf16[512,1024]{1,0:T(8,128)(2,1)}, bf16[512,1024]{1,0:T(8,128)(2,1)}, u32[]{:S(2)}, u32[]{:S(2)}) collective-permute-start(bf16[512,1024]{1,0:T(8,128)(2,1)} %param.13), channel_id=1, source_target_pairs={{0,96},{16,112},{32,0},{48,16},{64,32},{80,48},{96,64},{112,80},{1... | collective-permute-start | bytes 3145736 | tf_op jit(solution)/shard_map/ppermute | solution.py:24
  4.0 46.4 %collective-permute-start.8 = (bf16[512,1024]{1,0:T(8,128)(2,1)}, bf16[512,1024]{1,0:T(8,128)(2,1)}, u32[]{:S(2)}, u32[]{:S(2)}) collective-permute-start(bf16[512,1024]{1,0:T(8,128)(2,1)} %param.14), channel_id=1, source_target_pairs={{0,32},{16,48},{32,64},{48,80},{64,96},{80,112},{96,0},{112,16},{1... | collective-permute-start | bytes 3145736 | tf_op jit(solution)/shard_map/ppermute | solution.py:23
  4.5 32.5 %collective-permute-start.7 = (bf16[512,1024]{1,0:T(8,128)(2,1)}, bf16[512,1024]{1,0:T(8,128)(2,1)}, u32[]{:S(2)}, u32[]{:S(2)}) collective-permute-start(bf16[512,1024]{1,0:T(8,128)(2,1)} %param.14), channel_id=1, source_target_pairs={{0,16},{16,0},{32,48},{48,32},{64,80},{80,64},{96,112},{112,96},{1... | collective-permute-start | bytes 3145736 | tf_op jit(solution)/shard_map/ppermute | solution.py:25
  13.5 43.6 %all-to-all-start = ((bf16[16,128,2,256]{3,1,2,0:T(8,128)(2,1)}), bf16[16,128,2,256]{3,1,2,0:T(8,128)(2,1)S(1)}, u32[]{:S(2)}, u32[]{:S(2)}) async-start(bf16[16,128,2,256]{3,1,2,0:T(8,128)(2,1)} %copy.43), calls=%async_computation | async-start | bytes 4194304 | tf_op jit(solution)/shard_map/all_to_all | solution.py:42
  21.4 31.4 %collective-permute-start.9 = (bf16[512,1024]{1,0:T(8,128)(2,1)}, bf16[512,1024]{1,0:T(8,128)(2,1)S(1)}, u32[]{:S(2)}, u32[]{:S(2)}) collective-permute-start(bf16[512,1024]{1,0:T(8,128)(2,1)} %param.14), channel_id=1, source_target_pairs={{0,96},{16,112},{32,0},{48,16},{64,32},{80,48},{96,64},{112,80},{1... | collective-permute-start | bytes 3145736 | tf_op jit(solution)/shard_map/ppermute | solution.py:24
  29.0 27.3 %copy-start.6 = (s32[8]{0:T(128)S(1)}, s32[8]{0:T(128)}, u32[]{:S(2)}) copy-start(s32[8]{0:T(128)} %constant.76.clone) | copy-start | bytes 100
  29.0 27.3 %copy-start.7 = (s32[8]{0:T(128)S(1)}, s32[8]{0:T(128)}, u32[]{:S(2)}) copy-start(s32[8]{0:T(128)} %constant.77.clone) | copy-start | bytes 100
  31.3 30.6 %copy-start.5 = (bf16[128,256]{1,0:T(8,128)(2,1)S(1)}, bf16[128,256]{1,0:T(8,128)(2,1)}, u32[]{:S(2)}) copy-start(bf16[128,256]{1,0:T(8,128)(2,1)} %param.12) | copy-start | bytes 196612
  37.0 24.7 %collective-permute-start.3 = (bf16[512,1024]{1,0:T(8,128)(2,1)}, bf16[512,1024]{1,0:T(8,128)(2,1)}, u32[]{:S(2)}, u32[]{:S(2)}) collective-permute-start(bf16[512,1024]{1,0:T(8,128)(2,1)} %get-tuple-element.8), channel_id=1, source_target_pairs={{0,32},{16,112},{32,64},{48,16},{64,96},{80,48},{96,0},{112,80},{1... | collective-permute-start | bytes 3145736 | tf_op jit(solution)/shard_map/ppermute | solution.py:29
  55.9 17.0 %collective-permute-start.10 = (bf16[512,1024]{1,0:T(8,128)(2,1)}, bf16[512,1024]{1,0:T(8,128)(2,1)}, u32[]{:S(2)}, u32[]{:S(2)}) collective-permute-start(bf16[512,1024]{1,0:T(8,128)(2,1)} %get-tuple-element.10), channel_id=1, source_target_pairs={{0,32},{16,112},{32,64},{48,16},{64,96},{80,48},{96,0},{112,80},{1... | collective-permute-start | bytes 3145736 | tf_op jit(solution)/shard_map/ppermute | solution.py:29
  56.2 31.7 %collective-permute-start.4 = (bf16[512,1024]{1,0:T(8,128)(2,1)}, bf16[512,1024]{1,0:T(8,128)(2,1)}, u32[]{:S(2)}, u32[]{:S(2)}) collective-permute-start(bf16[512,1024]{1,0:T(8,128)(2,1)} %collective-permute-done.1), channel_id=1, source_target_pairs={{0,16},{16,0},{32,48},{48,32},{64,80},{80,64},{96,112},{112,96},{1... | collective-permute-start | bytes 3145736 | tf_op jit(solution)/shard_map/ppermute | solution.py:30
  56.5 34.1 %collective-permute-start.5 = (bf16[512,1024]{1,0:T(8,128)(2,1)}, bf16[512,1024]{1,0:T(8,128)(2,1)}, u32[]{:S(2)}, u32[]{:S(2)}) collective-permute-start(bf16[512,1024]{1,0:T(8,128)(2,1)} %collective-permute-done.2), channel_id=1, source_target_pairs={{0,16},{16,0},{32,48},{48,32},{64,80},{80,64},{96,112},{112,96},{1... | collective-permute-start | bytes 3145736 | tf_op jit(solution)/shard_map/ppermute | solution.py:30
  57.0 35.9 %collective-permute-start.11 = (bf16[512,1024]{1,0:T(8,128)(2,1)}, bf16[512,1024]{1,0:T(8,128)(2,1)}, u32[]{:S(2)}, u32[]{:S(2)}) collective-permute-start(bf16[512,1024]{1,0:T(8,128)(2,1)} %collective-permute-done.8), channel_id=1, source_target_pairs={{0,16},{16,0},{32,48},{48,32},{64,80},{80,64},{96,112},{112,96},{1... | collective-permute-start | bytes 3145736 | tf_op jit(solution)/shard_map/ppermute | solution.py:30
  61.7 33.5 %collective-permute-start.12 = (bf16[512,1024]{1,0:T(8,128)(2,1)S(1)}, bf16[512,1024]{1,0:T(8,128)(2,1)}, u32[]{:S(2)}, u32[]{:S(2)}) collective-permute-start(bf16[512,1024]{1,0:T(8,128)(2,1)S(1)} %collective-permute-done.9), channel_id=1, source_target_pairs={{0,16},{16,0},{32,48},{48,32},{64,80},{80,64},{96,112},{112,96},{1... | collective-permute-start | bytes 3145736 | tf_op jit(solution)/shard_map/ppermute | solution.py:30
  63.0 34.4 %all-to-all-start.1 = ((bf16[16,128,256]{2,1,0:T(8,128)(2,1)}), bf16[16,128,256]{2,1,0:T(8,128)(2,1)}, u32[]{:S(2)}, u32[]{:S(2)}) async-start(bf16[16,128,256]{2,1,0:T(8,128)(2,1)} %broadcast_in_dim.17), calls=%async_computation.1 | async-start | bytes 2097152 | tf_op jit(solution)/shard_map/all_to_all | solution.py:48
  72.9 26.4 %collective-permute-start.6 = (bf16[512,1024]{1,0:T(8,128)(2,1)}, bf16[512,1024]{1,0:T(8,128)(2,1)}, u32[]{:S(2)}, u32[]{:S(2)}) collective-permute-start(bf16[512,1024]{1,0:T(8,128)(2,1)} %collective-permute-done.3), channel_id=1, source_target_pairs={{0,16},{16,0},{32,48},{48,32},{64,80},{80,64},{96,112},{112,96},{1... | collective-permute-start | bytes 3145736 | tf_op jit(solution)/shard_map/ppermute | solution.py:31
  87.9 18.5 %collective-permute-start.13 = (bf16[512,1024]{1,0:T(8,128)(2,1)}, bf16[512,1024]{1,0:T(8,128)(2,1)S(1)}, u32[]{:S(2)}, u32[]{:S(2)}) collective-permute-start(bf16[512,1024]{1,0:T(8,128)(2,1)} %collective-permute-done.10), channel_id=1, source_target_pairs={{0,16},{16,0},{32,48},{48,32},{64,80},{80,64},{96,112},{112,96},{1... | collective-permute-start | bytes 3145736 | tf_op jit(solution)/shard_map/ppermute | solution.py:31
  209.7 68.4 %copy-start.4 = (f32[128,1024]{1,0:T(8,128)S(1)}, f32[128,1024]{1,0:T(8,128)}, u32[]{:S(2)}) copy-start(f32[128,1024]{1,0:T(8,128)} %copy-done.3) | copy-start | bytes 1572868
  212.6 65.5 %all-to-all-start.3 = ((bf16[16,4,128,256]{3,2,1,0:T(8,128)(2,1)}), bf16[16,4,128,256]{3,2,1,0:T(8,128)(2,1)}, u32[]{:S(2)}, u32[]{:S(2)}) async-start(bf16[16,4,128,256]{3,2,1,0:T(8,128)(2,1)} %broadcast_in_dim.20), calls=%async_computation.3 | async-start | bytes 8388608 | tf_op jit(solution)/shard_map/all_to_all | solution.py:48
  278.1 26.4 %copy-start.1 = (bf16[128,4096]{1,0:T(8,128)(2,1)S(1)}, bf16[128,4096]{1,0:T(8,128)(2,1)}, u32[]{:S(2)}) copy-start(bf16[128,4096]{1,0:T(8,128)(2,1)} %param.9) | copy-start | bytes 3145732
  291.7 12.2 %all-to-all-start.4 = ((f32[16,1,128]{2,1,0:T(1,128)}), f32[16,1,128]{2,1,0:T(1,128)S(1)}, u32[]{:S(2)}, u32[]{:S(2)}) async-start(f32[16,1,128]{2,1,0:T(1,128)} %broadcast_in_dim.21), calls=%async_computation.4 | async-start | bytes 16384 | tf_op jit(solution)/shard_map/all_to_all | solution.py:53
  (4 other events, 24.9 us)

commit v7 on v1

--- a/solution.py
+++ b/solution.py
@@ -29,8 +29,8 @@
     far = lax.ppermute(relay, "dp", fwd)
     partner_near = lax.ppermute(jnp.stack([from_below, from_above]), "dp", swap)
     partner_far = lax.ppermute(far, "dp", swap)
-    joined = jnp.concatenate(
-        [block, partner, from_below, from_above, far, partner_near[0], partner_near[1], partner_far]
+    joined = jnp.stack(
+        [block, partner, from_below, from_above, far, partner_near[0], partner_near[1], partner_far], axis=1
     )
     rel_y = jnp.array([0, 0, -1, 1, 2, -1, 1, 2], jnp.int32)
     flip = jnp.array([0, 1, 0, 0, 0, 1, 1, 1], jnp.int32)
@@ -89,10 +89,9 @@
 
 def local(features, enc_in, enc_out, noise, in_weight, out_weight, probes):
     n = lax.axis_size("tensor")
-    w_in, block_ids = gather_dp(in_weight)
-    w_out, _ = gather_dp(out_weight)
-    w_in = w_in.reshape(n, -1, in_weight.shape[-1])
-    w_out = w_out.reshape(n, -1, out_weight.shape[-1])
+    both, block_ids = gather_dp(jnp.stack([in_weight, out_weight]))
+    w_in = both[0].reshape(n, -1, in_weight.shape[-1])
+    w_out = both[1].reshape(n, -1, out_weight.shape[-1])
     halves = n // block_ids.shape[0]
     order = (halves * block_ids[:, None] + jnp.arange(halves)[None, :]).reshape(-1)
     back = jnp.argsort(order)

time: 303 us -> 337 us (1.11)
  waiting for transfers between devices: 79.9 us -> 133 us
  matrix products: 46.4 us -> 34.2 us
  starting transfers between devices: 40.6 us -> 32.1 us
    ppermute x2 -> x1, waiting for transfers between devices: 9.28 us -> 43.7 us  [gather_dp(): from_below = lax.ppermute(block, 'dp', up)]
    all_to_all x1, waiting for transfers between devices: 0.01 us -> 12.2 us  [reduce_scatter_pieces(): received = lax.all_to_all(pieces.astype(jnp.bfloat16), 'tensor', 0, 0)]
    unnamed x36, local copies, waits for them, and re-layouts: 33.4 us -> 23.5 us
    all_to_all x2, waiting for transfers between devices: 64.5 us -> 72.8 us  [all_gather_pieces(): lax.all_to_all(jnp.broadcast_to(piece[None], (n,) + piece.shape), 'tensor...]
    slice x0 -> x1, local copies, waits for them, and re-layouts: none -> 6.85 us  [local(): w_in = both[0].reshape(n, -1, in_weight.shape[-1])]
    dot_general x1, matrix products: 8.12 us -> 3.68 us  [series(): jnp.einsum('pbh,sch->spbc', scaled, w_in_p, preferred_element_type=jnp.fl...]
    dot_general x1, matrix products: 4.8 us -> 1.33 us  [local(): jnp.einsum('sbc,sch->bh', u_pieces, w_in, preferred_element_type=jnp.floa...]
  transfers between devices with their start and end apart: 21 -> 15, of which waited for: 7 -> 8; matrix products, arithmetic and copies ran while one was open for 21% -> 15% of each run, Pallas kernels for 0% -> 0%
where the time goes in v7:
time: 337 us; the launch traced here: 336 us
  waiting for transfers between devices  133 us (39%)
  blocking collectives  65 us (19%)
  local copies, waits for them, and re-layouts  51.9 us (15%)
  matrix products  34.2 us (10%)
  starting transfers between devices  32.1 us (10%)
  other arithmetic  18.9 us (6%)
    all_to_all x2, waiting for transfers between devices, all_gather_pieces(): lax.all_to_all(jnp.broadcast_to(piece[None], (n,) + piece.shape), 'tensor...  72.8 us
    all_to_all x1, blocking collectives, reduce_scatter_pieces(): received = lax.all_to_all(pieces.astype(jnp.bfloat16), 'tensor', 0, 0)  65 us
    ppermute x1, waiting for transfers between devices, gather_dp(): from_below = lax.ppermute(block, 'dp', up)  43.7 us
    unnamed x36, local copies, waits for them, and re-layouts  23.5 us
    all_to_all x1, waiting for transfers between devices, reduce_scatter_pieces(): received = lax.all_to_all(pieces.astype(jnp.bfloat16), 'tensor', 0, 0)  12.2 us
    all_to_all x2, starting transfers between devices, all_gather_pieces(): lax.all_to_all(jnp.broadcast_to(piece[None], (n,) + piece.shape), 'tensor...  9.21 us
    all_to_all x1, starting transfers between devices, reduce_scatter_pieces(): received = lax.all_to_all(pieces.astype(jnp.bfloat16), 'tensor', 0, 0)  7.93 us
    ppermute x6, starting transfers between devices, psum_groups(): lax.ppermute(value, 'tensor', [(t, t ^ k * step) for t in range(n)])  7.14 us
  transfers between devices with their start and end apart: 15, of which 8 were waited for; matrix products, arithmetic and copies ran while one was open for 15% of the time, Pallas kernels for 0%

profile of v7, /device:TPU:0, one launch (start us, length us, event | category | flops | bytes accessed | tf_op | source)
XLA Modules:
  0.0 336.2 jit_solution(2191463443352619308)
XLA Ops:
  0.7 3.2 pad_maximum_fusion.2
  9.1 43.7 %collective-permute-done.1 = bf16[2,512,1024]{2,1,0:T(8,128)(2,1)S(1)} collective-permute-done((bf16[2,512,1024]{2,1,0:T(8,128)(2,1)}, bf16[2,512,1024]{2,1,0:T(8,128)(2,1)S(1)}, u32[]{:S(2)}, u32[]{:S(2)}) %collective-permute-start.1) | collective-permute-done | bytes 2097184 | tf_op jit(solution)/shard_map/ppermute | solution.py:23
  55.4 5.3 %convert_bitcast_fusion.2 = bf16[16,128,2,256]{3,1,0,2:T(8,128)(2,1)} fusion(bf16[128,2,16,256]{3,2,1,0:T(8,128)(2,1)} %bitcast.152, bf16[128,4096]{1,0:T(8,128)(2,1)S(1)} %copy-done, bf16[4096,128]{1,0:T(8,128)(2,1)} %param.10), kind=kOutput, calls=%fused_computation.28 | convolution fusion | flops 403783680 | bytes 6291456 | tf_op jit(solution)/shard_map/bk,kmsc->sbmc/dot_general | solution.py:102
  60.7 3.1 copy.29
  63.8 7.9 %all-to-all-start = ((bf16[16,128,2,256]{3,1,2,0:T(8,128)(2,1)}), bf16[16,128,2,256]{3,1,2,0:T(8,128)(2,1)}, u32[]{:S(2)}, u32[]{:S(2)}) async-start(bf16[16,128,2,256]{3,1,2,0:T(8,128)(2,1)} %copy.29), calls=%async_computation | async-start | bytes 4194304 | tf_op jit(solution)/shard_map/all_to_all | solution.py:42
  78.0 4.1 %copy.30 = bf16[2,128,4096]{1,2,0:T(8,128)(2,1)} copy(bf16[2,128,4096]{2,1,0:T(8,128)(2,1)} %param.15) | data formatting | bytes 4194304 | tf_op args[6]
  82.1 4.0 %copy.31 = bf16[2,128,16,256]{3,1,2,0:T(8,128)(2,1)} copy(bf16[2,128,16,256]{1,3,2,0:T(8,128)(2,1)} %bitcast.153) | data formatting | bytes 4194304 | tf_op jit(solution)/shard_map/reshape | solution.py:114
  87.4 3.6 %gather_fusion = bf16[16,2,128,256]{3,2,1,0:T(8,128)(2,1)} fusion(bf16[2,128,16,256]{3,1,2,0:T(8,128)(2,1)} %copy.31, s32[1024]{0:T(1024)S(1)} %pad_clamp_fusion.1), kind=kCustom, calls=%fused_computation | custom fusion | bytes 4194368 | tf_op jit(solution)/shard_map/jit(_take)/gather | solution.py:115
  93.8 12.2 %all-to-all-done = bf16[16,128,2,256]{3,1,2,0:T(8,128)(2,1)} async-done(((bf16[16,128,2,256]{3,1,2,0:T(8,128)(2,1)}), bf16[16,128,2,256]{3,1,2,0:T(8,128)(2,1)}, u32[]{:S(2)}, u32[]{:S(2)}) %all-to-all-start) | async-done | bytes 2097184 | tf_op jit(solution)/shard_map/all_to_all | solution.py:42
  109.2 4.5 %all-to-all-start.1 = ((bf16[16,128,256]{2,1,0:T(8,128)(2,1)}), bf16[16,128,256]{2,1,0:T(8,128)(2,1)}, u32[]{:S(2)}, u32[]{:S(2)}) async-start(bf16[16,128,256]{2,1,0:T(8,128)(2,1)} %broadcast_in_dim.15), calls=%async_computation.1 | async-start | bytes 2097152 | tf_op jit(solution)/shard_map/all_to_all | solution.py:48
  113.7 3.2 bitcast_dynamic-update-slice_fusion.4
  119.9 13.2 %all-to-all-done.1 = bf16[16,128,256]{2,1,0:T(8,128)(2,1)} async-done(((bf16[16,128,256]{2,1,0:T(8,128)(2,1)}), bf16[16,128,256]{2,1,0:T(8,128)(2,1)}, u32[]{:S(2)}, u32[]{:S(2)}) %all-to-all-start.1) | async-done | bytes 1048608 | tf_op jit(solution)/shard_map/all_to_all | solution.py:48
  135.0 3.1 bitcast_dynamic-update-slice_fusion.1
  138.1 3.1 fusion.2
  141.2 3.1 fusion.1
  144.3 3.1 bitcast_dynamic-update-slice_fusion
  147.3 6.9 %fusion.53 = (bf16[1,8,512,1024]{3,2,0,1:T(8,128)(2,1)S(1)}, bf16[1,8,512,1024]{3,2,0,1:T(8,128)(2,1)S(1)}) fusion(bf16[2,8,512,1024]{3,2,0,1:T(8,128)(2,1)} %bitcast_dynamic-update-slice_fusion), kind=kLoop, calls=%fused_computation.77 | loop fusion | bytes 33554432 | tf_op jit(solution)/shard_map/slice | solution.py:93
  165.1 3.7 %convert_bitcast_fusion.1 = bf16[16,2,128,256]{2,3,1,0:T(8,128)(2,1)} fusion(bf16[16,256,1024,1]{2,1,3,0:T(8,128)(2,1)S(1)} %bitcast.148, bf16[2,128,1024,1]{2,1,0,3:T(8,128)(2,1)S(1)} %fusion.33), kind=kOutput, calls=%fused_computation.27 | convolution fusion | flops 2148532224 | bytes 11010048 | tf_op jit(solution)/shard_map/pbh,sch->spbc/dot_general | solution.py:65
  168.8 3.3 convolution_bitcast_fusion
  176.3 65.0 %all_to_all.20 = bf16[16,5,128,256]{2,3,1,0:T(8,128)(2,1)S(1)} all-to-all(bf16[16,5,128,256]{2,3,1,0:T(8,128)(2,1)S(1)} %pad_maximum_fusion), channel_id=1, replica_groups=mesh['dp'=8,'tensor'=16] {'tensor'}, dimensions={0} | all-to-all | bytes 10485760 | tf_op jit(solution)/shard_map/all_to_all | solution.py:42
  245.1 4.7 %all-to-all-start.3 = ((bf16[16,4,128,256]{3,2,1,0:T(8,128)(2,1)}), bf16[16,4,128,256]{3,2,1,0:T(8,128)(2,1)}, u32[]{:S(2)}, u32[]{:S(2)}) async-start(bf16[16,4,128,256]{3,2,1,0:T(8,128)(2,1)} %broadcast_in_dim.18), calls=%async_computation.3 | async-start | bytes 8388608 | tf_op jit(solution)/shard_map/all_to_all | solution.py:48
  250.8 59.6 %all-to-all-done.3 = bf16[16,4,128,256]{3,2,1,0:T(8,128)(2,1)} async-done(((bf16[16,4,128,256]{3,2,1,0:T(8,128)(2,1)}), bf16[16,4,128,256]{3,2,1,0:T(8,128)(2,1)}, u32[]{:S(2)}, u32[]{:S(2)}) %all-to-all-start.3) | async-done | bytes 4194336 | tf_op jit(solution)/shard_map/all_to_all | solution.py:48
  310.4 6.3 %fusion.32 = bf16[2,128,1024,1]{2,1,0,3:T(8,128)(2,1)S(1)} fusion(bf16[16,4,128,256]{3,2,1,0:T(8,128)(2,1)} %all-to-all-done.3, bf16[16,256,1024,1]{2,1,3,0:T(8,128)(2,1)} %bitcast.157, f32[128,1024]{1,0:T(8,128)S(1)} %copy-done.10), kind=kOutput, calls=%fused_computation.42 | convolution fusion | flops 2148007936 | bytes 13631488 | tf_op jit(solution)/shard_map/spbc,sch->pbh/dot_general | solution.py:79
  316.8 6.6 %fusion = f32[128]{0:T(128)S(1)} fusion(bf16[16,256,1024,1]{2,1,3,0:T(8,128)(2,1)} %bitcast.149, bf16[2,128,1024,1]{2,1,0,3:T(8,128)(2,1)S(1)} %fusion.32, bf16[16,4,128,256]{3,2,1,0:T(8,128)(2,1)} %all-to-all-done.3), kind=kOutput, calls=%fused_computation.7 | convolution fusion | flops 2150629376 | bytes 11010560 | tf_op jit(solution)/shard_map/pbh,sch->spbc/dot_general | solution.py:83
  (84 shorter events, 58.7 us)
Async XLA Ops:
  0.6 54.8 %copy-start = (bf16[128,4096]{1,0:T(8,128)(2,1)S(1)}, bf16[128,4096]{1,0:T(8,128)(2,1)}, u32[]{:S(2)}) copy-start(bf16[128,4096]{1,0:T(8,128)(2,1)} %param.9) | copy-start | bytes 3145732
  0.6 6.4 %copy-start.8 = (bf16[128,8192]{1,0:T(8,128)(2,1)S(1)}, bf16[128,8192]{1,0:T(8,128)(2,1)}, u32[]{:S(2)}) copy-start(bf16[128,8192]{1,0:T(8,128)(2,1)} %param.11) | copy-start | bytes 6291460
  3.8 49.0 %collective-permute-start.1 = (bf16[2,512,1024]{2,1,0:T(8,128)(2,1)}, bf16[2,512,1024]{2,1,0:T(8,128)(2,1)S(1)}, u32[]{:S(2)}, u32[]{:S(2)}) collective-permute-start(bf16[2,512,1024]{2,1,0:T(8,128)(2,1)} %pad_maximum_fusion.2), channel_id=1, source_target_pairs={{0,32},{16,48},{32,64},{48,80},{64,96},{80,112},{96,0},{112,16},{1... | collective-permute-start | bytes 6291464 | tf_op jit(solution)/shard_map/ppermute | solution.py:23
  5.5 47.3 %collective-permute-start.2 = (bf16[2,512,1024]{2,1,0:T(8,128)(2,1)}, bf16[2,512,1024]{2,1,0:T(8,128)(2,1)S(1)}, u32[]{:S(2)}, u32[]{:S(2)}) collective-permute-start(bf16[2,512,1024]{2,1,0:T(8,128)(2,1)} %pad_maximum_fusion.2), channel_id=1, source_target_pairs={{0,96},{16,112},{32,0},{48,16},{64,32},{80,48},{96,64},{112,80},{1... | collective-permute-start | bytes 6291464 | tf_op jit(solution)/shard_map/ppermute | solution.py:24
  55.4 82.7 %collective-permute-start.4 = (bf16[2,2,512,1024]{3,2,1,0:T(8,128)(2,1)}, bf16[2,2,512,1024]{3,2,1,0:T(8,128)(2,1)}, u32[]{:S(2)}, u32[]{:S(2)}) collective-permute-start(bf16[2,2,512,1024]{3,2,1,0:T(8,128)(2,1)} %pad_maximum_fusion.1), channel_id=1, source_target_pairs={{0,16},{16,0},{32,48},{48,32},{64,80},{80,64},{96,112},{112,96},{1... | collective-permute-start | bytes 12582920 | tf_op jit(solution)/shard_map/ppermute | solution.py:30
  63.8 42.1 %all-to-all-start = ((bf16[16,128,2,256]{3,1,2,0:T(8,128)(2,1)}), bf16[16,128,2,256]{3,1,2,0:T(8,128)(2,1)}, u32[]{:S(2)}, u32[]{:S(2)}) async-start(bf16[16,128,2,256]{3,1,2,0:T(8,128)(2,1)} %copy.29), calls=%async_computation | async-start | bytes 4194304 | tf_op jit(solution)/shard_map/all_to_all | solution.py:42
  71.8 6.1 %copy-start.12 = (s32[8]{0:T(128)S(1)}, s32[8]{0:T(128)}, u32[]{:S(2)}) copy-start(s32[8]{0:T(128)} %constant.74.clone) | copy-start | bytes 100
  73.4 34.5 %collective-permute-start.3 = (bf16[2,512,1024]{2,1,0:T(8,128)(2,1)}, bf16[2,512,1024]{2,1,0:T(8,128)(2,1)}, u32[]{:S(2)}, u32[]{:S(2)}) collective-permute-start(bf16[2,512,1024]{2,1,0:T(8,128)(2,1)} %broadcast_select_fusion), channel_id=1, source_target_pairs={{0,32},{16,112},{32,64},{48,16},{64,96},{80,48},{96,0},{112,80},{1... | collective-permute-start | bytes 6291464 | tf_op jit(solution)/shard_map/ppermute | solution.py:29
  75.0 38.8 %collective-permute-start = (bf16[2,512,1024]{2,1,0:T(8,128)(2,1)}, bf16[2,512,1024]{2,1,0:T(8,128)(2,1)}, u32[]{:S(2)}, u32[]{:S(2)}) collective-permute-start(bf16[2,512,1024]{2,1,0:T(8,128)(2,1)} %pad_maximum_fusion.2), channel_id=1, source_target_pairs={{0,16},{16,0},{32,48},{48,32},{64,80},{80,64},{96,112},{112,96},{1... | collective-permute-start | bytes 6291464 | tf_op jit(solution)/shard_map/ppermute | solution.py:25
  82.1 9.0 %copy-start.6 = (bf16[512,1024]{1,0:T(8,128)(2,1)S(1)}, bf16[512,1024]{1,0:T(8,128)(2,1)}, u32[]{:S(2)}) copy-start(bf16[512,1024]{1,0:T(8,128)(2,1)} %param.14) | copy-start | bytes 3145732
  91.1 17.0 %copy-start.11 = (bf16[128,256]{1,0:T(8,128)(2,1)S(1)}, bf16[128,256]{1,0:T(8,128)(2,1)}, u32[]{:S(2)}) copy-start(bf16[128,256]{1,0:T(8,128)(2,1)} %param.12) | copy-start | bytes 196612
  107.9 36.4 %collective-permute-start.5 = (bf16[2,512,1024]{2,1,0:T(8,128)(2,1)}, bf16[2,512,1024]{2,1,0:T(8,128)(2,1)}, u32[]{:S(2)}, u32[]{:S(2)}) collective-permute-start(bf16[2,512,1024]{2,1,0:T(8,128)(2,1)} %collective-permute-done.3), channel_id=1, source_target_pairs={{0,16},{16,0},{32,48},{48,32},{64,80},{80,64},{96,112},{112,96},{1... | collective-permute-start | bytes 6291464 | tf_op jit(solution)/shard_map/ppermute | solution.py:31
  109.2 24.0 %all-to-all-start.1 = ((bf16[16,128,256]{2,1,0:T(8,128)(2,1)}), bf16[16,128,256]{2,1,0:T(8,128)(2,1)}, u32[]{:S(2)}, u32[]{:S(2)}) async-start(bf16[16,128,256]{2,1,0:T(8,128)(2,1)} %broadcast_in_dim.15), calls=%async_computation.1 | async-start | bytes 2097152 | tf_op jit(solution)/shard_map/all_to_all | solution.py:48
  154.2 10.9 %copy-start.2 = (bf16[1,8,512,1024]{3,2,0,1:T(8,128)(2,1)}, bf16[1,8,512,1024]{3,2,0,1:T(8,128)(2,1)S(1)}, u32[]{:S(2)}) copy-start(bf16[1,8,512,1024]{3,2,0,1:T(8,128)(2,1)S(1)} %get-tuple-element.8) | copy-start | bytes 25165828
  154.2 14.6 %copy-start.5 = (bf16[1,8,512,1024]{3,2,0,1:T(8,128)(2,1)}, bf16[1,8,512,1024]{3,2,0,1:T(8,128)(2,1)S(1)}, u32[]{:S(2)}) copy-start(bf16[1,8,512,1024]{3,2,0,1:T(8,128)(2,1)S(1)} %get-tuple-element.9) | copy-start | bytes 25165828
  245.1 65.3 %copy-start.10 = (f32[128,1024]{1,0:T(8,128)S(1)}, f32[128,1024]{1,0:T(8,128)}, u32[]{:S(2)}) copy-start(f32[128,1024]{1,0:T(8,128)} %copy-done.9) | copy-start | bytes 1572868
  245.1 65.3 %all-to-all-start.3 = ((bf16[16,4,128,256]{3,2,1,0:T(8,128)(2,1)}), bf16[16,4,128,256]{3,2,1,0:T(8,128)(2,1)}, u32[]{:S(2)}, u32[]{:S(2)}) async-start(bf16[16,4,128,256]{3,2,1,0:T(8,128)(2,1)} %broadcast_in_dim.18), calls=%async_computation.3 | async-start | bytes 8388608 | tf_op jit(solution)/shard_map/all_to_all | solution.py:48
  316.7 19.5 %copy-start.1 = (bf16[128,4096]{1,0:T(8,128)(2,1)S(1)}, bf16[128,4096]{1,0:T(8,128)(2,1)}, u32[]{:S(2)}) copy-start(bf16[128,4096]{1,0:T(8,128)(2,1)} %param.9) | copy-start | bytes 3145732
  323.4 5.2 %collective-permute-start.7 = (f32[128]{0:T(128)S(1)}, f32[128]{0:T(128)S(1)}, u32[]{:S(2)}, u32[]{:S(2)}) collective-permute-start(f32[128]{0:T(128)S(1)} %multiply_add_fusion), channel_id=1, source_target_pairs={{0,2},{1,3},{2,0},{3,1},{4,6},{5,7},{6,4},{7,5},{8,10},{9,11},{10,... | collective-permute-start | bytes 1544 | tf_op jit(solution)/shard_map/ppermute | solution.py:55
  323.5 5.1 %collective-permute-start.8 = (f32[128]{0:T(128)S(1)}, f32[128]{0:T(128)S(1)}, u32[]{:S(2)}, u32[]{:S(2)}) collective-permute-start(f32[128]{0:T(128)S(1)} %multiply_add_fusion), channel_id=1, source_target_pairs={{0,3},{1,2},{2,1},{3,0},{4,7},{5,6},{6,5},{7,4},{8,11},{9,10},{10,... | collective-permute-start | bytes 1544 | tf_op jit(solution)/shard_map/ppermute | solution.py:55
  324.1 4.4 %collective-permute-start.6 = (f32[128]{0:T(128)S(1)}, f32[128]{0:T(128)S(1)}, u32[]{:S(2)}, u32[]{:S(2)}) collective-permute-start(f32[128]{0:T(128)S(1)} %multiply_add_fusion), channel_id=1, source_target_pairs={{0,1},{1,0},{2,3},{3,2},{4,5},{5,4},{6,7},{7,6},{8,9},{9,8},{10,11... | collective-permute-start | bytes 1544 | tf_op jit(solution)/shard_map/ppermute | solution.py:55
  328.5 5.2 %collective-permute-start.10 = (f32[128]{0:T(128)S(1)}, f32[128]{0:T(128)S(1)}, u32[]{:S(2)}, u32[]{:S(2)}) collective-permute-start(f32[128]{0:T(128)S(1)} %add_add_fusion), channel_id=1, source_target_pairs={{0,8},{1,9},{2,10},{3,11},{4,12},{5,13},{6,14},{7,15},{8,0},{9,1},... | collective-permute-start | bytes 1544 | tf_op jit(solution)/shard_map/ppermute | solution.py:55
  330.6 4.8 %collective-permute-start.11 = (f32[128]{0:T(128)S(1)}, f32[128]{0:T(128)S(1)}, u32[]{:S(2)}, u32[]{:S(2)}) collective-permute-start(f32[128]{0:T(128)S(1)} %add_add_fusion), channel_id=1, source_target_pairs={{0,12},{1,13},{2,14},{3,15},{4,8},{5,9},{6,10},{7,11},{8,4},{9,5},... | collective-permute-start | bytes 1544 | tf_op jit(solution)/shard_map/ppermute | solution.py:55
  332.1 3.6 %collective-permute-start.9 = (f32[128]{0:T(128)S(1)}, f32[128]{0:T(128)S(1)}, u32[]{:S(2)}, u32[]{:S(2)}) collective-permute-start(f32[128]{0:T(128)S(1)} %add_add_fusion), channel_id=1, source_target_pairs={{0,4},{1,5},{2,6},{3,7},{4,0},{5,1},{6,2},{7,3},{8,12},{9,13},{10,... | collective-permute-start | bytes 1544 | tf_op jit(solution)/shard_map/ppermute | solution.py:55
  (5 other events, 20.9 us)

commit v8 on v6

--- a/solution.py
+++ b/solution.py
@@ -27,7 +27,7 @@
     y, c = d // 2, d % 2
     relay = jnp.where(c == 0, from_below, from_above)
     far = lax.ppermute(relay, "dp", fwd)
-    partner_near = [lax.ppermute(from_below, "dp", swap), lax.ppermute(from_above, "dp", swap)]
+    partner_near = lax.ppermute(jnp.stack([from_below, from_above]), "dp", swap)
     partner_far = lax.ppermute(far, "dp", swap)
     joined = jnp.concatenate(
         [block, partner, from_below, from_above, far, partner_near[0], partner_near[1], partner_far]

time: 307 us -> 301 us (0.980)
  blocking collectives: 70.1 us -> 65.9 us
  other arithmetic: 13.8 us -> 17.7 us
    ppermute x2, waiting for transfers between devices: 6.3 us -> 0.01 us  [gather_dp(): far = lax.ppermute(relay, 'dp', fwd)]
    dot_general x1, matrix products: 9.12 us -> 3.57 us  [series(): jnp.einsum('pbh,sch->spbc', scaled_t, w_out_p, preferred_element_type=jnp...]
    dot_general x1, matrix products: 2.63 us -> 8.12 us  [series(): jnp.einsum('pbh,sch->spbc', scaled, w_in_p, preferred_element_type=jnp.fl...]
    all_to_all x2, waiting for transfers between devices: 60 us -> 64.6 us  [all_gather_pieces(): lax.all_to_all(jnp.broadcast_to(piece[None], (n,) + piece.shape), 'tensor...]
    another operation x1 -> x3, other arithmetic: 0.03 us -> 4.29 us  [the longest x2 4.26 us: gather_dp(): partner_near = lax.ppermute(jnp.stack([from_below, from_above]), 'dp', swap)]
    all_to_all x1, blocking collectives: 70.1 us -> 65.9 us  [reduce_scatter_pieces(): received = lax.all_to_all(pieces.astype(jnp.bfloat16), 'tensor', 0, 0)]
    dot_general x1, matrix products: 5.93 us -> 2.41 us  [series(): jnp.einsum('pbsc,sch->pbh', start_p, w_out_p, preferred_element_type=jnp....]
    dot_general x1, matrix products: 6.71 us -> 3.33 us  [local(): jnp.einsum('bh,sch->sbc', squash, w_out, preferred_element_type=jnp.float32)]
  transfers between devices with their start and end apart: 18 -> 16, of which waited for: 5 -> 5; matrix products, arithmetic and copies ran while one was open for 22% -> 22% of each run, Pallas kernels for 0% -> 0%
where the time goes in v8:
time: 301 us; the launch traced here: 299 us
  waiting for transfers between devices  81.6 us (27%)
  blocking collectives  65.9 us (22%)
  local copies, waits for them, and re-layouts  50.8 us (17%)
  matrix products  46.3 us (15%)
  starting transfers between devices  36.1 us (12%)
  other arithmetic  17.7 us (6%)
    all_to_all x1, blocking collectives, reduce_scatter_pieces(): received = lax.all_to_all(pieces.astype(jnp.bfloat16), 'tensor', 0, 0)  65.9 us
    all_to_all x2, waiting for transfers between devices, all_gather_pieces(): lax.all_to_all(jnp.broadcast_to(piece[None], (n,) + piece.shape), 'tensor...  64.6 us
    unnamed x36, local copies, waits for them, and re-layouts  33.3 us
    all_to_all x2, starting transfers between devices, all_gather_pieces(): lax.all_to_all(jnp.broadcast_to(piece[None], (n,) + piece.shape), 'tensor...  12.5 us
    ppermute x2, waiting for transfers between devices, gather_dp(): from_below = lax.ppermute(block, 'dp', up)  9.33 us
    dot_general x1, matrix products, series(): jnp.einsum('pbh,sch->spbc', scaled, w_in_p, preferred_element_type=jnp.fl...  8.12 us
    all_to_all x1, starting transfers between devices, reduce_scatter_pieces(): received = lax.all_to_all(pieces.astype(jnp.bfloat16), 'tensor', 0, 0)  8.04 us
    all_to_all x1, waiting for transfers between devices, psum_a2a(): lax.all_to_all(jnp.broadcast_to(value[None], (n,) + value.shape), 'tensor...  6.76 us
  transfers between devices with their start and end apart: 16, of which 5 were waited for; matrix products, arithmetic and copies ran while one was open for 22% of the time, Pallas kernels for 0%

profile of v8, /device:TPU:0, one launch (start us, length us, event | category | flops | bytes accessed | tf_op | source)
XLA Modules:
  0.0 299.3 jit_solution(7380741629755704533)
XLA Ops:
  4.0 3.5 %copy.54 = bf16[16,8,32,256]{3,2,1,0:T(8,128)(2,1)} copy(bf16[16,8,32,256]{3,1,2,0:T(8,128)(2,1)} %bitcast.149) | data formatting | bytes 4194304
  7.6 5.3 %convert_bitcast_fusion.2 = bf16[16,128,2,256]{3,1,0,2:T(8,128)(2,1)} fusion(bf16[128,2,16,256]{3,2,1,0:T(8,128)(2,1)} %bitcast.145, bf16[128,4096]{1,0:T(8,128)(2,1)S(1)} %copy-done, bf16[4096,128]{1,0:T(8,128)(2,1)} %param.10), kind=kOutput, calls=%fused_computation.18 | convolution fusion | flops 403783680 | bytes 6291456 | tf_op jit(solution)/shard_map/bk,kmsc->sbmc/dot_general | solution.py:99
  12.8 3.2 %copy.43 = bf16[16,128,2,256]{3,1,2,0:T(8,128)(2,1)} copy(bf16[16,128,2,256]{3,1,0,2:T(8,128)(2,1)} %convert_bitcast_fusion.2) | data formatting | bytes 4194304 | tf_op jit(solution)/shard_map/convert_element_type | solution.py:42
  16.0 8.0 %all-to-all-start = ((bf16[16,128,2,256]{3,1,2,0:T(8,128)(2,1)}), bf16[16,128,2,256]{3,1,2,0:T(8,128)(2,1)}, u32[]{:S(2)}, u32[]{:S(2)}) async-start(bf16[16,128,2,256]{3,1,2,0:T(8,128)(2,1)} %copy.43), calls=%async_computation | async-start | bytes 4194304 | tf_op jit(solution)/shard_map/all_to_all | solution.py:42
  24.5 2.9 collective-permute-start.8
  34.3 3.1 %broadcast_select_fusion.1 = (bf16[512,1024]{1,0:T(8,128)(2,1)}, bf16[4096,1024]{1,0:T(8,128)(2,1)}) fusion(bf16[512,1024]{1,0:T(8,128)(2,1)S(1)} %collective-permute-done.1, bf16[512,1024]{1,0:T(8,128)(2,1)} %collective-permute-done.2, pred[]{:T(512)S(6)} %eq.9, bf16[4096,1024]{1,0:T(8,128)(2,1)} %constant_dynamic-update-slice_fusion.3), kind=kLoop, calls=%fused_computation.44 | loop fusion | flops 524288 | bytes 4194305 | tf_op jit(solution)/shard_map/jit(_where)/select_n | solution.py:28
  41.0 9.3 %collective-permute-done.7 = bf16[512,1024]{1,0:T(8,128)(2,1)S(1)} collective-permute-done((bf16[512,1024]{1,0:T(8,128)(2,1)}, bf16[512,1024]{1,0:T(8,128)(2,1)S(1)}, u32[]{:S(2)}, u32[]{:S(2)}) %collective-permute-start.7) | collective-permute-done | bytes 1048608 | tf_op jit(solution)/shard_map/ppermute | solution.py:23
  54.3 3.2 %copy-done.5 = bf16[4096,1024]{1,0:T(8,128)(2,1)} copy-done((bf16[4096,1024]{1,0:T(8,128)(2,1)}, bf16[4096,1024]{1,0:T(8,128)(2,1)S(1)}, u32[]{:S(2)}) %copy-start.5) | copy-done | bytes 8388632
  62.3 7.9 %all-to-all-start.1 = ((bf16[16,128,256]{2,1,0:T(8,128)(2,1)}), bf16[16,128,256]{2,1,0:T(8,128)(2,1)}, u32[]{:S(2)}, u32[]{:S(2)}) async-start(bf16[16,128,256]{2,1,0:T(8,128)(2,1)} %broadcast_in_dim.17), calls=%async_computation.1 | async-start | bytes 2097152 | tf_op jit(solution)/shard_map/all_to_all | solution.py:48
  70.4 4.1 %copy.44 = bf16[2,128,4096]{1,2,0:T(8,128)(2,1)} copy(bf16[2,128,4096]{2,1,0:T(8,128)(2,1)} %param.15) | data formatting | bytes 4194304 | tf_op args[6]
  74.5 2.9 copy.45
  86.8 4.1 %all-to-all-done.1 = bf16[16,128,256]{2,1,0:T(8,128)(2,1)} async-done(((bf16[16,128,256]{2,1,0:T(8,128)(2,1)}), bf16[16,128,256]{2,1,0:T(8,128)(2,1)}, u32[]{:S(2)}, u32[]{:S(2)}) %all-to-all-start.1) | async-done | bytes 1048608 | tf_op jit(solution)/shard_map/all_to_all | solution.py:48
  103.0 4.8 %multiply_subtract_fusion = (f32[128,1024]{1,0:T(8,128)S(1)}, bf16[128,1024]{1,0:T(8,128)(2,1)S(1)}) fusion(bf16[16,128,256]{2,1,0:T(8,128)(2,1)S(1)} %gather_fusion.1, bf16[16,256,1024]{2,1,0:T(8,128)(2,1)} %bitcast.9), kind=kOutput, calls=%fused_computation.45 | convolution fusion | flops 1074135040 | bytes 10223616 | tf_op jit(solution)/shard_map/sbc,sch->bh/dot_general | solution.py:105
  112.0 5.8 %fusion.34 = bf16[2,128,1024,1]{2,1,0,3:T(8,128)(2,1)S(1)} fusion(bf16[16,256,1024,1]{2,1,3,0:T(8,128)(2,1)} %bitcast.11, bf16[16,2,128,256]{3,2,1,0:T(8,128)(2,1)S(1)} %copy-done.2, f32[128,1024]{1,0:T(8,128)S(1)} %get-tuple-element.12), kind=kOutput, calls=%fused_computation.33 | convolution fusion | flops 2148007936 | bytes 11534336 | tf_op jit(solution)/shard_map/pbsc,sch->pbh/dot_general | solution.py:62
  117.8 8.1 %convert_bitcast_fusion.1 = bf16[16,2,128,256]{2,3,1,0:T(8,128)(2,1)S(1)} fusion(bf16[16,256,1024,1]{2,1,3,0:T(8,128)(2,1)} %bitcast.11, bf16[2,128,1024,1]{2,1,0,3:T(8,128)(2,1)S(1)} %fusion.31), kind=kOutput, calls=%fused_computation.17 | convolution fusion | flops 2148532224 | bytes 11010048 | tf_op jit(solution)/shard_map/pbh,sch->spbc/dot_general | solution.py:61
  125.9 3.6 %convert_bitcast_fusion = bf16[16,2,128,256]{2,3,1,0:T(8,128)(2,1)} fusion(bf16[16,256,1024,1]{2,1,3,0:T(8,128)(2,1)S(1)} %bitcast.151, bf16[2,128,1024,1]{2,1,0,3:T(8,128)(2,1)S(1)} %fusion.34), kind=kOutput, calls=%fused_computation.16 | convolution fusion | flops 2148532224 | bytes 11010048 | tf_op jit(solution)/shard_map/pbh,sch->spbc/dot_general | solution.py:64
  129.5 3.3 %convolution_bitcast_fusion = bf16[16,128,256]{1,2,0:T(8,128)(2,1)} fusion(bf16[16,256,1024]{2,1,0:T(8,128)(2,1)S(1)} %bitcast.152, bf16[128,1024]{1,0:T(8,128)(2,1)S(1)} %get-tuple-element.13), kind=kOutput, calls=%fused_computation.19 | convolution fusion | flops 1073741824 | bytes 9699328 | tf_op jit(solution)/shard_map/bh,sch->sbc/dot_general | solution.py:109
  137.0 65.9 %all_to_all.26 = bf16[16,5,128,256]{2,3,1,0:T(8,128)(2,1)S(1)} all-to-all(bf16[16,5,128,256]{2,3,1,0:T(8,128)(2,1)S(1)} %pad_maximum_fusion), channel_id=1, replica_groups=mesh['dp'=8,'tensor'=16] {'tensor'}, dimensions={0} | all-to-all | bytes 10485760 | tf_op jit(solution)/shard_map/all_to_all | solution.py:42
  206.7 4.5 %all-to-all-start.3 = ((bf16[16,4,128,256]{3,2,1,0:T(8,128)(2,1)}), bf16[16,4,128,256]{3,2,1,0:T(8,128)(2,1)}, u32[]{:S(2)}, u32[]{:S(2)}) async-start(bf16[16,4,128,256]{3,2,1,0:T(8,128)(2,1)} %broadcast_in_dim.20), calls=%async_computation.3 | async-start | bytes 8388608 | tf_op jit(solution)/shard_map/all_to_all | solution.py:48
  212.3 60.5 %all-to-all-done.3 = bf16[16,4,128,256]{3,2,1,0:T(8,128)(2,1)} async-done(((bf16[16,4,128,256]{3,2,1,0:T(8,128)(2,1)}), bf16[16,4,128,256]{3,2,1,0:T(8,128)(2,1)}, u32[]{:S(2)}, u32[]{:S(2)}) %all-to-all-start.3) | async-done | bytes 4194336 | tf_op jit(solution)/shard_map/all_to_all | solution.py:48
  272.8 6.4 %fusion.30 = bf16[2,128,1024,1]{2,1,0,3:T(8,128)(2,1)S(1)} fusion(bf16[16,4,128,256]{3,2,1,0:T(8,128)(2,1)} %all-to-all-done.3, bf16[16,256,1024,1]{2,1,3,0:T(8,128)(2,1)} %bitcast.153, f32[128,1024]{1,0:T(8,128)S(1)} %copy-done.4), kind=kOutput, calls=%fused_computation.31 | convolution fusion | flops 2148007936 | bytes 13631488 | tf_op jit(solution)/shard_map/spbc,sch->pbh/dot_general | solution.py:75
  279.2 6.6 %fusion = f32[128]{0:T(128)S(1)} fusion(bf16[16,256,1024,1]{2,1,3,0:T(8,128)(2,1)} %bitcast.11, bf16[2,128,1024,1]{2,1,0,3:T(8,128)(2,1)S(1)} %fusion.30, bf16[16,4,128,256]{3,2,1,0:T(8,128)(2,1)} %all-to-all-done.3), kind=kOutput, calls=%fused_computation.6 | convolution fusion | flops 2150629376 | bytes 11010560 | tf_op jit(solution)/shard_map/pbh,sch->spbc/dot_general | solution.py:79
  286.4 4.9 %all-to-all-start.4 = ((f32[16,1,128]{2,1,0:T(1,128)}), f32[16,1,128]{2,1,0:T(1,128)S(1)}, u32[]{:S(2)}, u32[]{:S(2)}) async-start(f32[16,1,128]{2,1,0:T(1,128)} %broadcast_in_dim.21), calls=%async_computation.4 | async-start | bytes 16384 | tf_op jit(solution)/shard_map/all_to_all | solution.py:53
  292.0 6.8 %all-to-all-done.4 = f32[16,1,128]{2,1,0:T(1,128)S(1)} async-done(((f32[16,1,128]{2,1,0:T(1,128)}), f32[16,1,128]{2,1,0:T(1,128)S(1)}, u32[]{:S(2)}, u32[]{:S(2)}) %all-to-all-start.4) | async-done | bytes 8224 | tf_op jit(solution)/shard_map/all_to_all | solution.py:53
  (87 shorter events, 59.6 us)
Async XLA Ops:
  0.6 6.9 %copy-start = (bf16[128,4096]{1,0:T(8,128)(2,1)S(1)}, bf16[128,4096]{1,0:T(8,128)(2,1)}, u32[]{:S(2)}) copy-start(bf16[128,4096]{1,0:T(8,128)(2,1)} %param.9) | copy-start | bytes 3145732
  0.6 29.1 %collective-permute-start = (bf16[512,1024]{1,0:T(8,128)(2,1)}, bf16[512,1024]{1,0:T(8,128)(2,1)}, u32[]{:S(2)}, u32[]{:S(2)}) collective-permute-start(bf16[512,1024]{1,0:T(8,128)(2,1)} %param.13), channel_id=1, source_target_pairs={{0,16},{16,0},{32,48},{48,32},{64,80},{80,64},{96,112},{112,96},{1... | collective-permute-start | bytes 3145736 | tf_op jit(solution)/shard_map/ppermute | solution.py:25
  0.7 32.5 %collective-permute-start.1 = (bf16[512,1024]{1,0:T(8,128)(2,1)}, bf16[512,1024]{1,0:T(8,128)(2,1)S(1)}, u32[]{:S(2)}, u32[]{:S(2)}) collective-permute-start(bf16[512,1024]{1,0:T(8,128)(2,1)} %param.13), channel_id=1, source_target_pairs={{0,32},{16,48},{32,64},{48,80},{64,96},{80,112},{96,0},{112,16},{1... | collective-permute-start | bytes 3145736 | tf_op jit(solution)/shard_map/ppermute | solution.py:23
  2.5 31.8 %collective-permute-start.2 = (bf16[512,1024]{1,0:T(8,128)(2,1)}, bf16[512,1024]{1,0:T(8,128)(2,1)}, u32[]{:S(2)}, u32[]{:S(2)}) collective-permute-start(bf16[512,1024]{1,0:T(8,128)(2,1)} %param.13), channel_id=1, source_target_pairs={{0,96},{16,112},{32,0},{48,16},{64,32},{80,48},{96,64},{112,80},{1... | collective-permute-start | bytes 3145736 | tf_op jit(solution)/shard_map/ppermute | solution.py:24
  16.0 43.1 %all-to-all-start = ((bf16[16,128,2,256]{3,1,2,0:T(8,128)(2,1)}), bf16[16,128,2,256]{3,1,2,0:T(8,128)(2,1)}, u32[]{:S(2)}, u32[]{:S(2)}) async-start(bf16[16,128,2,256]{3,1,2,0:T(8,128)(2,1)} %copy.43), calls=%async_computation | async-start | bytes 4194304 | tf_op jit(solution)/shard_map/all_to_all | solution.py:42
  24.1 26.3 %collective-permute-start.7 = (bf16[512,1024]{1,0:T(8,128)(2,1)}, bf16[512,1024]{1,0:T(8,128)(2,1)S(1)}, u32[]{:S(2)}, u32[]{:S(2)}) collective-permute-start(bf16[512,1024]{1,0:T(8,128)(2,1)} %param.14), channel_id=1, source_target_pairs={{0,32},{16,48},{32,64},{48,80},{64,96},{80,112},{96,0},{112,16},{1... | collective-permute-start | bytes 3145736 | tf_op jit(solution)/shard_map/ppermute | solution.py:23
  24.5 26.7 %collective-permute-start.8 = (bf16[512,1024]{1,0:T(8,128)(2,1)}, bf16[512,1024]{1,0:T(8,128)(2,1)S(1)}, u32[]{:S(2)}, u32[]{:S(2)}) collective-permute-start(bf16[512,1024]{1,0:T(8,128)(2,1)} %param.14), channel_id=1, source_target_pairs={{0,96},{16,112},{32,0},{48,16},{64,32},{80,48},{96,64},{112,80},{1... | collective-permute-start | bytes 3145736 | tf_op jit(solution)/shard_map/ppermute | solution.py:24
  29.7 23.0 %collective-permute-start.6 = (bf16[512,1024]{1,0:T(8,128)(2,1)}, bf16[512,1024]{1,0:T(8,128)(2,1)S(1)}, u32[]{:S(2)}, u32[]{:S(2)}) collective-permute-start(bf16[512,1024]{1,0:T(8,128)(2,1)} %param.14), channel_id=1, source_target_pairs={{0,16},{16,0},{32,48},{48,32},{64,80},{80,64},{96,112},{112,96},{1... | collective-permute-start | bytes 3145736 | tf_op jit(solution)/shard_map/ppermute | solution.py:25
  37.4 43.2 %collective-permute-start.3 = (bf16[512,1024]{1,0:T(8,128)(2,1)}, bf16[512,1024]{1,0:T(8,128)(2,1)}, u32[]{:S(2)}, u32[]{:S(2)}) collective-permute-start(bf16[512,1024]{1,0:T(8,128)(2,1)} %get-tuple-element.8), channel_id=1, source_target_pairs={{0,32},{16,112},{32,64},{48,16},{64,96},{80,48},{96,0},{112,80},{1... | collective-permute-start | bytes 3145736 | tf_op jit(solution)/shard_map/ppermute | solution.py:29
  40.2 20.8 %copy-start.8 = (bf16[128,256]{1,0:T(8,128)(2,1)S(1)}, bf16[128,256]{1,0:T(8,128)(2,1)}, u32[]{:S(2)}) copy-start(bf16[128,256]{1,0:T(8,128)(2,1)} %param.12) | copy-start | bytes 196612
  40.2 52.6 %collective-permute-start.4 = (bf16[2,512,1024]{2,1,0:T(8,128)(2,1)}, bf16[2,512,1024]{2,1,0:T(8,128)(2,1)}, u32[]{:S(2)}, u32[]{:S(2)}) collective-permute-start(bf16[2,512,1024]{2,1,0:T(8,128)(2,1)} %pad_maximum_fusion.1), channel_id=1, source_target_pairs={{0,16},{16,0},{32,48},{48,32},{64,80},{80,64},{96,112},{112,96},{1... | collective-permute-start | bytes 6291464 | tf_op jit(solution)/shard_map/ppermute | solution.py:30
  51.2 19.0 %copy-start.9 = (s32[8]{0:T(128)S(1)}, s32[8]{0:T(128)}, u32[]{:S(2)}) copy-start(s32[8]{0:T(128)} %constant.76.clone) | copy-start | bytes 100
  51.2 19.0 %copy-start.10 = (s32[8]{0:T(128)S(1)}, s32[8]{0:T(128)}, u32[]{:S(2)}) copy-start(s32[8]{0:T(128)} %constant.77.clone) | copy-start | bytes 100
  52.7 44.6 %collective-permute-start.10 = (bf16[2,512,1024]{2,1,0:T(8,128)(2,1)}, bf16[2,512,1024]{2,1,0:T(8,128)(2,1)}, u32[]{:S(2)}, u32[]{:S(2)}) collective-permute-start(bf16[2,512,1024]{2,1,0:T(8,128)(2,1)} %pad_maximum_fusion.2), channel_id=1, source_target_pairs={{0,16},{16,0},{32,48},{48,32},{64,80},{80,64},{96,112},{112,96},{1... | collective-permute-start | bytes 6291464 | tf_op jit(solution)/shard_map/ppermute | solution.py:30
  57.6 24.4 %collective-permute-start.9 = (bf16[512,1024]{1,0:T(8,128)(2,1)}, bf16[512,1024]{1,0:T(8,128)(2,1)}, u32[]{:S(2)}, u32[]{:S(2)}) collective-permute-start(bf16[512,1024]{1,0:T(8,128)(2,1)} %get-tuple-element.10), channel_id=1, source_target_pairs={{0,32},{16,112},{32,64},{48,16},{64,96},{80,48},{96,0},{112,80},{1... | collective-permute-start | bytes 3145736 | tf_op jit(solution)/shard_map/ppermute | solution.py:29
  62.3 28.7 %all-to-all-start.1 = ((bf16[16,128,256]{2,1,0:T(8,128)(2,1)}), bf16[16,128,256]{2,1,0:T(8,128)(2,1)}, u32[]{:S(2)}, u32[]{:S(2)}) async-start(bf16[16,128,256]{2,1,0:T(8,128)(2,1)} %broadcast_in_dim.17), calls=%async_computation.1 | async-start | bytes 2097152 | tf_op jit(solution)/shard_map/all_to_all | solution.py:48
  80.6 19.0 %collective-permute-start.5 = (bf16[512,1024]{1,0:T(8,128)(2,1)}, bf16[512,1024]{1,0:T(8,128)(2,1)S(1)}, u32[]{:S(2)}, u32[]{:S(2)}) collective-permute-start(bf16[512,1024]{1,0:T(8,128)(2,1)} %collective-permute-done.3), channel_id=1, source_target_pairs={{0,16},{16,0},{32,48},{48,32},{64,80},{80,64},{96,112},{112,96},{1... | collective-permute-start | bytes 3145736 | tf_op jit(solution)/shard_map/ppermute | solution.py:31
  82.0 25.9 %collective-permute-start.11 = (bf16[512,1024]{1,0:T(8,128)(2,1)}, bf16[512,1024]{1,0:T(8,128)(2,1)S(1)}, u32[]{:S(2)}, u32[]{:S(2)}) collective-permute-start(bf16[512,1024]{1,0:T(8,128)(2,1)} %collective-permute-done.9), channel_id=1, source_target_pairs={{0,16},{16,0},{32,48},{48,32},{64,80},{80,64},{96,112},{112,96},{1... | collective-permute-start | bytes 3145736 | tf_op jit(solution)/shard_map/ppermute | solution.py:31
  103.0 6.6 %copy-start.2 = (bf16[16,2,128,256]{3,2,1,0:T(8,128)(2,1)S(1)}, bf16[16,2,128,256]{3,2,1,0:T(8,128)(2,1)}, u32[]{:S(2)}) copy-start(bf16[16,2,128,256]{3,2,1,0:T(8,128)(2,1)} %gather_fusion) | copy-start | bytes 6291460
  108.8 20.6 %copy-start.7 = (bf16[4096,1024]{1,0:T(8,128)(2,1)}, bf16[4096,1024]{1,0:T(8,128)(2,1)S(1)}, u32[]{:S(2)}) copy-start(bf16[4096,1024]{1,0:T(8,128)(2,1)S(1)} %constant_dynamic-update-slice_fusion.6) | copy-start | bytes 25165828
  203.9 68.9 %copy-start.4 = (f32[128,1024]{1,0:T(8,128)S(1)}, f32[128,1024]{1,0:T(8,128)}, u32[]{:S(2)}) copy-start(f32[128,1024]{1,0:T(8,128)} %copy-done.3) | copy-start | bytes 1572868
  206.7 66.1 %all-to-all-start.3 = ((bf16[16,4,128,256]{3,2,1,0:T(8,128)(2,1)}), bf16[16,4,128,256]{3,2,1,0:T(8,128)(2,1)}, u32[]{:S(2)}, u32[]{:S(2)}) async-start(bf16[16,4,128,256]{3,2,1,0:T(8,128)(2,1)} %broadcast_in_dim.20), calls=%async_computation.3 | async-start | bytes 8388608 | tf_op jit(solution)/shard_map/all_to_all | solution.py:48
  272.8 26.5 %copy-start.1 = (bf16[128,4096]{1,0:T(8,128)(2,1)S(1)}, bf16[128,4096]{1,0:T(8,128)(2,1)}, u32[]{:S(2)}) copy-start(bf16[128,4096]{1,0:T(8,128)(2,1)} %param.9) | copy-start | bytes 3145732
  286.4 12.4 %all-to-all-start.4 = ((f32[16,1,128]{2,1,0:T(1,128)}), f32[16,1,128]{2,1,0:T(1,128)S(1)}, u32[]{:S(2)}, u32[]{:S(2)}) async-start(f32[16,1,128]{2,1,0:T(1,128)} %broadcast_in_dim.21), calls=%async_computation.4 | async-start | bytes 16384 | tf_op jit(solution)/shard_map/all_to_all | solution.py:53
  (3 other events, 13.2 us)

commit v9 on v8

--- a/solution.py
+++ b/solution.py
@@ -54,14 +54,16 @@
     return jnp.sum(received, axis=0)
 
 
-def series(start_p, w_in_p, w_out_p, slope, side):
+def series(start_p, order, w_in_p, w_out_p, slope, squash, pushed):
     t = lax.axis_index("tensor")
     pulled = jnp.einsum("pbsc,sch->pbh", start_p, w_out_p, preferred_element_type=jnp.float32)
     scaled = (pulled * slope[None]).astype(jnp.bfloat16)
     part_u = jnp.einsum("pbh,sch->spbc", scaled, w_in_p, preferred_element_type=jnp.float32)
-    pushed = jnp.einsum("pbsc,sch->pbh", start_p, w_in_p, preferred_element_type=jnp.float32)
     scaled_t = (pushed * slope[None]).astype(jnp.bfloat16)
-    part_v = jnp.einsum("pbh,sch->spbc", scaled_t, w_out_p, preferred_element_type=jnp.float32)
+    rows_in = jnp.concatenate([squash[None], scaled_t], axis=0)
+    rows_out = jnp.einsum("pbh,sch->spbc", rows_in, w_out_p, preferred_element_type=jnp.float32)
+    side, part_v = rows_out[:, 0], rows_out[:, 1:]
+    side = jnp.take(side, jnp.argsort(order), axis=0, mode="clip")
     summed = reduce_scatter_pieces(jnp.concatenate([part_u, part_v, side[:, None]], axis=1))
     probes_n = start_p.shape[0]
     uv_here = summed[: 2 * probes_n].astype(jnp.bfloat16)
@@ -91,7 +93,6 @@
     w_out = w_out.reshape(n, -1, out_weight.shape[-1])
     halves = n // block_ids.shape[0]
     order = (halves * block_ids[:, None] + jnp.arange(halves)[None, :]).reshape(-1)
-    back = jnp.argsort(order)
     hidden = jax.nn.silu(jnp.dot(features, enc_in, preferred_element_type=jnp.float32)).astype(
         jnp.bfloat16
     )
@@ -102,15 +103,15 @@
         jnp.bfloat16
     )
     u_pieces = jnp.take(all_gather_pieces(u_slice), order, axis=0, mode="clip")
-    pre_act = jnp.einsum("sbc,sch->bh", u_pieces, w_in, preferred_element_type=jnp.float32)
+    start_p = probes.reshape(probes.shape[0], probes.shape[1], n, -1)
+    start_p = jnp.take(start_p, order, axis=2, mode="clip")
+    rows_in = jnp.concatenate([jnp.moveaxis(u_pieces, 1, 0)[None], start_p], axis=0)
+    rows_out = jnp.einsum("pbsc,sch->pbh", rows_in, w_in, preferred_element_type=jnp.float32)
+    pre_act, pushed = rows_out[0], rows_out[1:]
     tanh_val = jnp.tanh(pre_act)
     squash = tanh_val.astype(jnp.bfloat16)
     slope = 1.0 - tanh_val * tanh_val
-    branch_part = jnp.einsum("bh,sch->sbc", squash, w_out, preferred_element_type=jnp.float32)
-    branch_part = jnp.take(branch_part, back, axis=0, mode="clip")
-    start_p = probes.reshape(probes.shape[0], probes.shape[1], n, -1)
-    start_p = jnp.take(start_p, order, axis=2, mode="clip")
-    running, branch = series(start_p, w_in, w_out, slope, branch_part)
+    running, branch = series(start_p, order, w_in, w_out, slope, squash, pushed)
     flowed = u_slice.astype(jnp.float32) + branch
     logdet = running / PROBES
     return (flowed, logdet)

time: 301 us -> 299 us (level)
  matrix products: 46.3 us -> 38.3 us
  local copies, waits for them, and re-layouts: 50.8 us -> 54.4 us
    dot_general x4 -> x2, matrix products: 17.5 us -> 10.9 us  [the longest x1 5.98 us: local(): jnp.einsum('pbsc,sch->pbh', rows_in, w_in, preferred_element_type=jnp.flo...]
    unnamed x36 -> x44, local copies, waits for them, and re-layouts: 33.3 us -> 29 us
    ppermute x2, waiting for transfers between devices: 9.33 us -> 13 us  [gather_dp(): from_below = lax.ppermute(block, 'dp', up)]
    all_to_all x2, waiting for transfers between devices: 64.6 us -> 61.2 us  [all_gather_pieces(): lax.all_to_all(jnp.broadcast_to(piece[None], (n,) + piece.shape), 'tensor...]
where the time goes in v9:
time: 299 us; the launch traced here: 296 us
  waiting for transfers between devices  83.6 us (28%)
  blocking collectives  68.1 us (23%)
  local copies, waits for them, and re-layouts  54.4 us (18%)
  matrix products  38.3 us (13%)
  starting transfers between devices  34.6 us (12%)
  other arithmetic  15.7 us (5%)
    all_to_all x1, blocking collectives, reduce_scatter_pieces(): received = lax.all_to_all(pieces.astype(jnp.bfloat16), 'tensor', 0, 0)  68.1 us
    all_to_all x2, waiting for transfers between devices, all_gather_pieces(): lax.all_to_all(jnp.broadcast_to(piece[None], (n,) + piece.shape), 'tensor...  61.2 us
    unnamed x44, local copies, waits for them, and re-layouts  29 us
    ppermute x2, waiting for transfers between devices, gather_dp(): from_below = lax.ppermute(block, 'dp', up)  13 us
    all_to_all x2, starting transfers between devices, all_gather_pieces(): lax.all_to_all(jnp.broadcast_to(piece[None], (n,) + piece.shape), 'tensor...  11.9 us
    all_to_all x1, starting transfers between devices, reduce_scatter_pieces(): received = lax.all_to_all(pieces.astype(jnp.bfloat16), 'tensor', 0, 0)  8.04 us
    dot_general x1, matrix products, series(): jnp.einsum('pbh,sch->spbc', scaled3, w_in_p, preferred_element_type=jnp.f...  6.52 us
    dot_general x1, matrix products, series(): jnp.einsum('spbc,sch->pbh', uv_pieces[:, :probes_n], w_out_p, preferred_e...  6.48 us
  transfers between devices with their start and end apart: 16, of which 5 were waited for; matrix products, arithmetic and copies ran while one was open for 22% of the time, Pallas kernels for 0%

profile of v9, /device:TPU:0, one launch (start us, length us, event | category | flops | bytes accessed | tf_op | source)
XLA Modules:
  0.0 295.8 jit_solution(13837089758343956637)
XLA Ops:
  4.0 3.5 %copy.70 = bf16[16,8,32,256]{3,2,1,0:T(8,128)(2,1)} copy(bf16[16,8,32,256]{3,1,2,0:T(8,128)(2,1)} %bitcast.138) | data formatting | bytes 4194304
  7.6 5.3 %convert_bitcast_fusion.1 = bf16[16,128,2,256]{3,1,0,2:T(8,128)(2,1)} fusion(bf16[128,2,16,256]{3,2,1,0:T(8,128)(2,1)} %bitcast.133, bf16[128,4096]{1,0:T(8,128)(2,1)S(1)} %copy-done, bf16[4096,128]{1,0:T(8,128)(2,1)} %param.10), kind=kOutput, calls=%fused_computation.23 | convolution fusion | flops 403783680 | bytes 6291456 | tf_op jit(solution)/shard_map/bk,kmsc->sbmc/dot_general | solution.py:100
  12.8 3.1 %copy.52 = bf16[16,128,2,256]{3,1,2,0:T(8,128)(2,1)} copy(bf16[16,128,2,256]{3,1,0,2:T(8,128)(2,1)} %convert_bitcast_fusion.1) | data formatting | bytes 4194304 | tf_op jit(solution)/shard_map/convert_element_type | solution.py:42
  16.0 8.0 %all-to-all-start = ((bf16[16,128,2,256]{3,1,2,0:T(8,128)(2,1)}), bf16[16,128,2,256]{3,1,2,0:T(8,128)(2,1)}, u32[]{:S(2)}, u32[]{:S(2)}) async-start(bf16[16,128,2,256]{3,1,2,0:T(8,128)(2,1)} %copy.52), calls=%async_computation | async-start | bytes 4194304 | tf_op jit(solution)/shard_map/all_to_all | solution.py:42
  27.1 2.9 collective-permute-start.8
  37.3 13.0 %collective-permute-done.7 = bf16[512,1024]{1,0:T(8,128)(2,1)S(1)} collective-permute-done((bf16[512,1024]{1,0:T(8,128)(2,1)}, bf16[512,1024]{1,0:T(8,128)(2,1)S(1)}, u32[]{:S(2)}, u32[]{:S(2)}) %collective-permute-start.7) | collective-permute-done | bytes 1048608 | tf_op jit(solution)/shard_map/ppermute | solution.py:23
  50.5 3.5 %collective-permute-done.8 = bf16[512,1024]{1,0:T(8,128)(2,1)S(1)} collective-permute-done((bf16[512,1024]{1,0:T(8,128)(2,1)}, bf16[512,1024]{1,0:T(8,128)(2,1)S(1)}, u32[]{:S(2)}, u32[]{:S(2)}) %collective-permute-start.8) | collective-permute-done | bytes 1048608 | tf_op jit(solution)/shard_map/ppermute | solution.py:24
  56.4 3.2 %copy-done.7 = bf16[4096,1024]{1,0:T(8,128)(2,1)} copy-done((bf16[4096,1024]{1,0:T(8,128)(2,1)}, bf16[4096,1024]{1,0:T(8,128)(2,1)S(1)}, u32[]{:S(2)}) %copy-start.7) | copy-done | bytes 8388632
  63.9 7.2 %all-to-all-start.1 = ((bf16[16,128,256]{2,1,0:T(8,128)(2,1)}), bf16[16,128,256]{2,1,0:T(8,128)(2,1)}, u32[]{:S(2)}, u32[]{:S(2)}) async-start(bf16[16,128,256]{2,1,0:T(8,128)(2,1)} %broadcast_in_dim.19), calls=%async_computation.1 | async-start | bytes 2097152 | tf_op jit(solution)/shard_map/all_to_all | solution.py:48
  73.7 3.1 %copy.53 = bf16[2,128,4096]{1,2,0:T(8,128)(2,1)S(1)} copy(bf16[2,128,4096]{2,1,0:T(8,128)(2,1)} %param.15) | data formatting | bytes 4194304 | tf_op args[6]
  76.8 2.6 copy.54
  83.2 2.8 pad_maximum_fusion.2
  101.0 6.0 %fusion.11 = f32[3,128,1024]{2,1,0:T(8,128)S(1)} fusion(bf16[16,256,1024,1]{2,1,0,3:T(8,128)(2,1)} %bitcast.146, bf16[2,128,16,256]{3,1,2,0:T(8,128)(2,1)S(1)} %bitcast.139, bf16[1,128,16,256]{3,1,2,0:T(8,128)(2,1)S(1)} %bitcast.140), kind=kOutput, calls=%fused_computation.24 | convolution fusion | flops 3222798336 | bytes 13107200 | tf_op jit(solution)/shard_map/pbsc,sch->pbh/dot_general | solution.py:109
  111.2 4.9 %convolution_bitcast_fusion = bf16[16,3,128,256]{2,3,1,0:T(8,128)(2,1)S(1)} fusion(bf16[16,256,1024,1]{2,1,3,0:T(8,128)(2,1)S(1)} %bitcast.143, bf16[2,128,1024]{2,1,0:T(8,128)(2,1)S(1)} %fusion.29, bf16[1,128,1024]{2,1,0:T(8,128)(2,1)S(1)} %get-tuple-element.8), kind=kOutput, calls=%fused_computation.13 | convolution fusion | flops 3222798336 | bytes 12320768 | tf_op jit(solution)/shard_map/pbh,sch->spbc/dot_general | solution.py:64
  118.8 3.2 %fusion.26 = bf16[2,128,1024,1]{2,1,0,3:T(8,128)(2,1)} fusion(bf16[16,256,1024,1]{2,1,3,0:T(8,128)(2,1)S(1)} %bitcast.144, bf16[16,2,128,256]{3,2,1,0:T(8,128)(2,1)S(1)} %gather_fusion, f32[128,1024]{1,0:T(8,128)S(1)} %get-tuple-element.9), kind=kOutput, calls=%fused_computation.32 | convolution fusion | flops 2148007936 | bytes 11534336 | tf_op jit(solution)/shard_map/pbsc,sch->pbh/dot_general | solution.py:59
  124.0 6.0 %convert_bitcast_fusion = bf16[16,2,128,256]{2,3,1,0:T(8,128)(2,1)S(1)} fusion(bf16[16,256,1024,1]{2,1,3,0:T(8,128)(2,1)} %bitcast.147, bf16[2,128,1024,1]{2,1,0,3:T(8,128)(2,1)} %fusion.26), kind=kOutput, calls=%fused_computation.22 | convolution fusion | flops 2148532224 | bytes 11010048 | tf_op jit(solution)/shard_map/pbh,sch->spbc/dot_general | solution.py:61
  130.6 68.1 %all_to_all.26 = bf16[16,5,128,256]{2,3,1,0:T(8,128)(2,1)S(1)} all-to-all(bf16[16,5,128,256]{2,3,1,0:T(8,128)(2,1)S(1)} %pad_maximum_fusion), channel_id=1, replica_groups=mesh['dp'=8,'tensor'=16] {'tensor'}, dimensions={0} | all-to-all | bytes 10485760 | tf_op jit(solution)/shard_map/all_to_all | solution.py:42
  202.0 2.5 broadcast_in_dim.23
  204.5 4.8 %all-to-all-start.3 = ((bf16[16,4,128,256]{3,2,1,0:T(8,128)(2,1)}), bf16[16,4,128,256]{3,2,1,0:T(8,128)(2,1)}, u32[]{:S(2)}, u32[]{:S(2)}) async-start(bf16[16,4,128,256]{3,2,1,0:T(8,128)(2,1)} %broadcast_in_dim.23), calls=%async_computation.3 | async-start | bytes 8388608 | tf_op jit(solution)/shard_map/all_to_all | solution.py:48
  209.4 60.4 %all-to-all-done.3 = bf16[16,4,128,256]{3,2,1,0:T(8,128)(2,1)} async-done(((bf16[16,4,128,256]{3,2,1,0:T(8,128)(2,1)}), bf16[16,4,128,256]{3,2,1,0:T(8,128)(2,1)}, u32[]{:S(2)}, u32[]{:S(2)}) %all-to-all-start.3) | async-done | bytes 4194336 | tf_op jit(solution)/shard_map/all_to_all | solution.py:48
  269.8 6.5 %fusion.25 = bf16[2,128,1024,1]{2,1,0,3:T(8,128)(2,1)S(1)} fusion(bf16[16,4,128,256]{3,2,1,0:T(8,128)(2,1)} %all-to-all-done.3, bf16[16,256,1024,1]{2,1,3,0:T(8,128)(2,1)} %bitcast.145, f32[128,1024]{1,0:T(8,128)} %copy-done.6), kind=kOutput, calls=%fused_computation.31 | convolution fusion | flops 2148007936 | bytes 13631488 | tf_op jit(solution)/shard_map/spbc,sch->pbh/dot_general | solution.py:77
  276.2 6.5 %fusion = f32[128]{0:T(128)S(1)} fusion(bf16[16,256,1024,1]{2,1,3,0:T(8,128)(2,1)} %bitcast.148, bf16[2,128,1024,1]{2,1,0,3:T(8,128)(2,1)S(1)} %fusion.25, bf16[16,4,128,256]{3,2,1,0:T(8,128)(2,1)} %all-to-all-done.3), kind=kOutput, calls=%fused_computation.7 | convolution fusion | flops 2150629376 | bytes 11010560 | tf_op jit(solution)/shard_map/pbh,sch->spbc/dot_general | solution.py:81
  283.4 4.4 %all-to-all-start.4 = ((f32[16,1,128]{2,1,0:T(1,128)}), f32[16,1,128]{2,1,0:T(1,128)S(1)}, u32[]{:S(2)}, u32[]{:S(2)}) async-start(f32[16,1,128]{2,1,0:T(1,128)} %broadcast_in_dim.24), calls=%async_computation.4 | async-start | bytes 16384 | tf_op jit(solution)/shard_map/all_to_all | solution.py:53
  289.4 5.9 %all-to-all-done.4 = f32[16,1,128]{2,1,0:T(1,128)S(1)} async-done(((f32[16,1,128]{2,1,0:T(1,128)}), f32[16,1,128]{2,1,0:T(1,128)S(1)}, u32[]{:S(2)}, u32[]{:S(2)}) %all-to-all-start.4) | async-done | bytes 8224 | tf_op jit(solution)/shard_map/all_to_all | solution.py:53
  (99 shorter events, 57.3 us)
Async XLA Ops:
  0.6 26.5 %collective-permute-start = (bf16[512,1024]{1,0:T(8,128)(2,1)}, bf16[512,1024]{1,0:T(8,128)(2,1)}, u32[]{:S(2)}, u32[]{:S(2)}) collective-permute-start(bf16[512,1024]{1,0:T(8,128)(2,1)} %param.13), channel_id=1, source_target_pairs={{0,16},{16,0},{32,48},{48,32},{64,80},{80,64},{96,112},{112,96},{1... | collective-permute-start | bytes 3145736 | tf_op jit(solution)/shard_map/ppermute | solution.py:25
  0.7 30.6 %collective-permute-start.1 = (bf16[512,1024]{1,0:T(8,128)(2,1)}, bf16[512,1024]{1,0:T(8,128)(2,1)S(1)}, u32[]{:S(2)}, u32[]{:S(2)}) collective-permute-start(bf16[512,1024]{1,0:T(8,128)(2,1)} %param.13), channel_id=1, source_target_pairs={{0,32},{16,48},{32,64},{48,80},{64,96},{80,112},{96,0},{112,16},{1... | collective-permute-start | bytes 3145736 | tf_op jit(solution)/shard_map/ppermute | solution.py:23
  2.5 28.9 %collective-permute-start.2 = (bf16[512,1024]{1,0:T(8,128)(2,1)}, bf16[512,1024]{1,0:T(8,128)(2,1)S(1)}, u32[]{:S(2)}, u32[]{:S(2)}) collective-permute-start(bf16[512,1024]{1,0:T(8,128)(2,1)} %param.13), channel_id=1, source_target_pairs={{0,96},{16,112},{32,0},{48,16},{64,32},{80,48},{96,64},{112,80},{1... | collective-permute-start | bytes 3145736 | tf_op jit(solution)/shard_map/ppermute | solution.py:24
  16.0 44.8 %all-to-all-start = ((bf16[16,128,2,256]{3,1,2,0:T(8,128)(2,1)}), bf16[16,128,2,256]{3,1,2,0:T(8,128)(2,1)}, u32[]{:S(2)}, u32[]{:S(2)}) async-start(bf16[16,128,2,256]{3,1,2,0:T(8,128)(2,1)} %copy.52), calls=%async_computation | async-start | bytes 4194304 | tf_op jit(solution)/shard_map/all_to_all | solution.py:42
  24.0 26.3 %collective-permute-start.7 = (bf16[512,1024]{1,0:T(8,128)(2,1)}, bf16[512,1024]{1,0:T(8,128)(2,1)S(1)}, u32[]{:S(2)}, u32[]{:S(2)}) collective-permute-start(bf16[512,1024]{1,0:T(8,128)(2,1)} %param.14), channel_id=1, source_target_pairs={{0,32},{16,48},{32,64},{48,80},{64,96},{80,112},{96,0},{112,16},{1... | collective-permute-start | bytes 3145736 | tf_op jit(solution)/shard_map/ppermute | solution.py:23
  24.5 10.7 %collective-permute-start.6 = (bf16[512,1024]{1,0:T(8,128)(2,1)}, bf16[512,1024]{1,0:T(8,128)(2,1)}, u32[]{:S(2)}, u32[]{:S(2)}) collective-permute-start(bf16[512,1024]{1,0:T(8,128)(2,1)} %param.14), channel_id=1, source_target_pairs={{0,16},{16,0},{32,48},{48,32},{64,80},{80,64},{96,112},{112,96},{1... | collective-permute-start | bytes 3145736 | tf_op jit(solution)/shard_map/ppermute | solution.py:25
  27.1 26.8 %collective-permute-start.8 = (bf16[512,1024]{1,0:T(8,128)(2,1)}, bf16[512,1024]{1,0:T(8,128)(2,1)S(1)}, u32[]{:S(2)}, u32[]{:S(2)}) collective-permute-start(bf16[512,1024]{1,0:T(8,128)(2,1)} %param.14), channel_id=1, source_target_pairs={{0,96},{16,112},{32,0},{48,16},{64,32},{80,48},{96,64},{112,80},{1... | collective-permute-start | bytes 3145736 | tf_op jit(solution)/shard_map/ppermute | solution.py:24
  32.9 23.6 %copy-start.9 = (bf16[4096,1024]{1,0:T(8,128)(2,1)}, bf16[4096,1024]{1,0:T(8,128)(2,1)S(1)}, u32[]{:S(2)}) copy-start(bf16[4096,1024]{1,0:T(8,128)(2,1)S(1)} %get-tuple-element.11) | copy-start | bytes 25165828
  32.9 39.6 %collective-permute-start.3 = (bf16[512,1024]{1,0:T(8,128)(2,1)}, bf16[512,1024]{1,0:T(8,128)(2,1)}, u32[]{:S(2)}, u32[]{:S(2)}) collective-permute-start(bf16[512,1024]{1,0:T(8,128)(2,1)} %get-tuple-element.10), channel_id=1, source_target_pairs={{0,32},{16,112},{32,64},{48,16},{64,96},{80,48},{96,0},{112,80},{1... | collective-permute-start | bytes 3145736 | tf_op jit(solution)/shard_map/ppermute | solution.py:29
  34.5 28.2 %copy-start.10 = (bf16[128,256]{1,0:T(8,128)(2,1)S(1)}, bf16[128,256]{1,0:T(8,128)(2,1)}, u32[]{:S(2)}) copy-start(bf16[128,256]{1,0:T(8,128)(2,1)} %param.12) | copy-start | bytes 196612
  34.5 59.3 %collective-permute-start.4 = (bf16[2,512,1024]{2,1,0:T(8,128)(2,1)}, bf16[2,512,1024]{2,1,0:T(8,128)(2,1)}, u32[]{:S(2)}, u32[]{:S(2)}) collective-permute-start(bf16[2,512,1024]{2,1,0:T(8,128)(2,1)} %pad_maximum_fusion.1), channel_id=1, source_target_pairs={{0,16},{16,0},{32,48},{48,32},{64,80},{80,64},{96,112},{112,96},{1... | collective-permute-start | bytes 6291464 | tf_op jit(solution)/shard_map/ppermute | solution.py:30
  50.4 20.6 %copy-start.11 = (s32[8]{0:T(128)S(1)}, s32[8]{0:T(128)}, u32[]{:S(2)}) copy-start(s32[8]{0:T(128)} %constant.76.clone) | copy-start | bytes 100
  50.5 20.6 %copy-start.12 = (s32[8]{0:T(128)S(1)}, s32[8]{0:T(128)}, u32[]{:S(2)}) copy-start(s32[8]{0:T(128)} %constant.77.clone) | copy-start | bytes 100
  59.7 26.3 %collective-permute-start.9 = (bf16[512,1024]{1,0:T(8,128)(2,1)}, bf16[512,1024]{1,0:T(8,128)(2,1)}, u32[]{:S(2)}, u32[]{:S(2)}) collective-permute-start(bf16[512,1024]{1,0:T(8,128)(2,1)} %get-tuple-element.12), channel_id=1, source_target_pairs={{0,32},{16,112},{32,64},{48,16},{64,96},{80,48},{96,0},{112,80},{1... | collective-permute-start | bytes 3145736 | tf_op jit(solution)/shard_map/ppermute | solution.py:29
  63.9 28.1 %all-to-all-start.1 = ((bf16[16,128,256]{2,1,0:T(8,128)(2,1)}), bf16[16,128,256]{2,1,0:T(8,128)(2,1)}, u32[]{:S(2)}, u32[]{:S(2)}) async-start(bf16[16,128,256]{2,1,0:T(8,128)(2,1)} %broadcast_in_dim.19), calls=%async_computation.1 | async-start | bytes 2097152 | tf_op jit(solution)/shard_map/all_to_all | solution.py:48
  72.5 26.1 %collective-permute-start.5 = (bf16[512,1024]{1,0:T(8,128)(2,1)}, bf16[512,1024]{1,0:T(8,128)(2,1)}, u32[]{:S(2)}, u32[]{:S(2)}) collective-permute-start(bf16[512,1024]{1,0:T(8,128)(2,1)} %collective-permute-done.3), channel_id=1, source_target_pairs={{0,16},{16,0},{32,48},{48,32},{64,80},{80,64},{96,112},{112,96},{1... | collective-permute-start | bytes 3145736 | tf_op jit(solution)/shard_map/ppermute | solution.py:31
  86.0 21.3 %collective-permute-start.10 = (bf16[2,512,1024]{2,1,0:T(8,128)(2,1)}, bf16[2,512,1024]{2,1,0:T(8,128)(2,1)}, u32[]{:S(2)}, u32[]{:S(2)}) collective-permute-start(bf16[2,512,1024]{2,1,0:T(8,128)(2,1)} %pad_maximum_fusion.2), channel_id=1, source_target_pairs={{0,16},{16,0},{32,48},{48,32},{64,80},{80,64},{96,112},{112,96},{1... | collective-permute-start | bytes 6291464 | tf_op jit(solution)/shard_map/ppermute | solution.py:30
  86.0 23.9 %collective-permute-start.11 = (bf16[512,1024]{1,0:T(8,128)(2,1)}, bf16[512,1024]{1,0:T(8,128)(2,1)}, u32[]{:S(2)}, u32[]{:S(2)}) collective-permute-start(bf16[512,1024]{1,0:T(8,128)(2,1)} %collective-permute-done.9), channel_id=1, source_target_pairs={{0,16},{16,0},{32,48},{48,32},{64,80},{80,64},{96,112},{112,96},{1... | collective-permute-start | bytes 3145736 | tf_op jit(solution)/shard_map/ppermute | solution.py:31
  98.6 8.7 %slice-start = ((s8[8388608]{0:T(1024)(128)(4,1)}), s8[4194304]{0:T(1024)(128)(4,1)S(1)}, s32[]{:S(2)}) async-start(s8[8388608]{0:T(1024)(128)(4,1)} %bitcast.141), calls=%async_computation.5 | async-start | bytes 8388608
  107.1 11.6 %copy-start.6 = (f32[128,1024]{1,0:T(8,128)}, f32[128,1024]{1,0:T(8,128)S(1)}, u32[]{:S(2)}) copy-start(f32[128,1024]{1,0:T(8,128)S(1)} %get-tuple-element.9) | copy-start | bytes 1572868
  111.2 7.5 %copy-start.8 = (bf16[4096,1024]{1,0:T(8,128)(2,1)}, bf16[4096,1024]{1,0:T(8,128)(2,1)S(1)}, u32[]{:S(2)}) copy-start(bf16[4096,1024]{1,0:T(8,128)(2,1)S(1)} %constant_dynamic-update-slice_fusion.6) | copy-start | bytes 25165828
  204.5 65.3 %all-to-all-start.3 = ((bf16[16,4,128,256]{3,2,1,0:T(8,128)(2,1)}), bf16[16,4,128,256]{3,2,1,0:T(8,128)(2,1)}, u32[]{:S(2)}, u32[]{:S(2)}) async-start(bf16[16,4,128,256]{3,2,1,0:T(8,128)(2,1)} %broadcast_in_dim.23), calls=%async_computation.3 | async-start | bytes 8388608 | tf_op jit(solution)/shard_map/all_to_all | solution.py:48
  269.8 26.0 %copy-start.1 = (bf16[128,4096]{1,0:T(8,128)(2,1)S(1)}, bf16[128,4096]{1,0:T(8,128)(2,1)}, u32[]{:S(2)}) copy-start(bf16[128,4096]{1,0:T(8,128)(2,1)} %param.9) | copy-start | bytes 3145732
  283.4 11.9 %all-to-all-start.4 = ((f32[16,1,128]{2,1,0:T(1,128)}), f32[16,1,128]{2,1,0:T(1,128)S(1)}, u32[]{:S(2)}, u32[]{:S(2)}) async-start(f32[16,1,128]{2,1,0:T(1,128)} %broadcast_in_dim.24), calls=%async_computation.4 | async-start | bytes 16384 | tf_op jit(solution)/shard_map/all_to_all | solution.py:53
  (7 other events, 33.2 us)

commit v10 on v9

--- a/solution.py
+++ b/solution.py
@@ -96,9 +96,10 @@
     hidden = jax.nn.silu(jnp.dot(features, enc_in, preferred_element_type=jnp.float32)).astype(
         jnp.bfloat16
     )
-    enc_out_p = enc_out.reshape(enc_out.shape[0], 2, n, -1)
-    stats_p = jnp.einsum("bk,kmsc->sbmc", hidden, enc_out_p, preferred_element_type=jnp.float32)
-    moments = reduce_scatter_pieces(stats_p)
+    stats = jnp.dot(hidden, enc_out, preferred_element_type=jnp.float32)
+    stats = stats.astype(jnp.bfloat16).reshape(stats.shape[0], 2, n, -1)
+    received = lax.all_to_all(stats, "tensor", 2, 2)
+    moments = jnp.sum(received.astype(jnp.float32), axis=2)
     u_slice = (moments[:, 0] + jax.nn.softplus(moments[:, 1]) * noise.astype(jnp.float32)).astype(
         jnp.bfloat16
     )

time: 299 us -> 300 us (level)
  local copies, waits for them, and re-layouts: 54.4 us -> 50.3 us
    reduce_sum x0 -> x1, other arithmetic: none -> 4.57 us  [local(): moments = jnp.sum(received.astype(jnp.float32), axis=2)]
    unnamed x44 -> x40, local copies, waits for them, and re-layouts: 29 us -> 24.6 us
    ppermute x2, waiting for transfers between devices: 13 us -> 17.3 us  [gather_dp(): from_below = lax.ppermute(block, 'dp', up)]
    reshape x0 -> x1, local copies, waits for them, and re-layouts: none -> 3.24 us  [local(): stats = stats.astype(jnp.bfloat16).reshape(stats.shape[0], 2, n, -1)]
    convert_element_type x1 -> x0, local copies, waits for them, and re-layouts: 3.15 us -> none  [reduce_scatter_pieces(): received = lax.all_to_all(pieces.astype(jnp.bfloat16), 'tensor', 0, 0)]
  transfers between devices with their start and end apart: 16 -> 16, of which waited for: 5 -> 6; matrix products, arithmetic and copies ran while one was open for 22% -> 21% of each run, Pallas kernels for 0% -> 0%
where the time goes in v10:
time: 300 us; the launch traced here: 298 us
  waiting for transfers between devices  85.8 us (29%)
  blocking collectives  68.5 us (23%)
  local copies, waits for them, and re-layouts  50.3 us (17%)
  matrix products  37.1 us (12%)
  starting transfers between devices  36.9 us (12%)
  other arithmetic  18.5 us (6%)
    all_to_all x1, blocking collectives, reduce_scatter_pieces(): received = lax.all_to_all(pieces.astype(jnp.bfloat16), 'tensor', 0, 0)  68.5 us
    all_to_all x2, waiting for transfers between devices, all_gather_pieces(): lax.all_to_all(jnp.broadcast_to(piece[None], (n,) + piece.shape), 'tensor...  60.8 us
    unnamed x40, local copies, waits for them, and re-layouts  24.6 us
    ppermute x2, waiting for transfers between devices, gather_dp(): from_below = lax.ppermute(block, 'dp', up)  17.3 us
    all_to_all x2, starting transfers between devices, all_gather_pieces(): lax.all_to_all(jnp.broadcast_to(piece[None], (n,) + piece.shape), 'tensor...  12.7 us
    all_to_all x1, starting transfers between devices, local(): received = lax.all_to_all(stats, 'tensor', 2, 2)  8.04 us
    all_to_all x1, waiting for transfers between devices, psum_a2a(): lax.all_to_all(jnp.broadcast_to(value[None], (n,) + value.shape), 'tensor...  6.76 us
    dot_general x1, matrix products, series(): jnp.einsum('spbc,sch->pbh', uv_pieces[:, :probes_n], w_out_p, preferred_e...  6.54 us
  transfers between devices with their start and end apart: 16, of which 6 were waited for; matrix products, arithmetic and copies ran while one was open for 21% of the time, Pallas kernels for 0%

profile of v10, /device:TPU:0, one launch (start us, length us, event | category | flops | bytes accessed | tf_op | source)
XLA Modules:
  0.0 298.1 jit_solution(13990591904194188846)
XLA Ops:
  4.1 4.0 %convolution_convert_fusion = bf16[128,8192]{1,0:T(8,128)(2,1)} fusion(bf16[128,8192]{1,0:T(8,128)(2,1)S(1)} %copy-done, bf16[128,4096]{1,0:T(8,128)(2,1)} %param.9, bf16[4096,128]{1,0:T(8,128)(2,1)} %param.10), kind=kOutput, calls=%fused_computation.4 | convolution fusion | flops 403783680 | bytes 6291456 | tf_op jit(solution)/shard_map/dot_general | solution.py:99
  10.2 3.2 %copy.50 = bf16[128,2,16,256]{3,1,0,2:T(2,128)(2,1)} copy(bf16[128,2,16,256]{3,2,1,0:T(8,128)(2,1)S(1)} %bitcast.140) | data formatting | bytes 4194304 | tf_op jit(solution)/shard_map/reshape | solution.py:100
  13.4 8.0 %all-to-all-start = ((bf16[128,2,16,256]{3,1,0,2:T(2,128)(2,1)}), bf16[128,2,16,256]{3,1,0,2:T(2,128)(2,1)}, u32[]{:S(2)}, u32[]{:S(2)}) async-start(bf16[128,2,16,256]{3,1,0,2:T(2,128)(2,1)} %copy.50), calls=%async_computation | async-start | bytes 4194304 | tf_op jit(solution)/shard_map/all_to_all | solution.py:101
  21.9 2.9 collective-permute-start.2
  28.8 2.7 broadcast_select_fusion
  33.1 17.3 %collective-permute-done.1 = bf16[512,1024]{1,0:T(8,128)(2,1)S(1)} collective-permute-done((bf16[512,1024]{1,0:T(8,128)(2,1)}, bf16[512,1024]{1,0:T(8,128)(2,1)S(1)}, u32[]{:S(2)}, u32[]{:S(2)}) %collective-permute-start.1) | collective-permute-done | bytes 1048608 | tf_op jit(solution)/shard_map/ppermute | solution.py:23
  54.4 3.2 %copy-done.5 = bf16[4096,1024]{1,0:T(8,128)(2,1)} copy-done((bf16[4096,1024]{1,0:T(8,128)(2,1)}, bf16[4096,1024]{1,0:T(8,128)(2,1)S(1)}, u32[]{:S(2)}) %copy-start.5) | copy-done | bytes 8388632
  59.2 4.6 %convert_reduce_fusion.1 = f32[128,2,256]{2,1,0:T(2,128)S(1)} fusion(bf16[128,2,16,256]{3,1,0,2:T(2,128)(2,1)} %all-to-all-done), kind=kLoop, calls=%fused_computation.9 | loop fusion | flops 2031616 | bytes 2359296 | tf_op jit(solution)/shard_map/reduce_sum | solution.py:102
  65.2 7.9 %all-to-all-start.1 = ((bf16[16,128,256]{2,1,0:T(8,128)(2,1)}), bf16[16,128,256]{2,1,0:T(8,128)(2,1)}, u32[]{:S(2)}, u32[]{:S(2)}) async-start(bf16[16,128,256]{2,1,0:T(8,128)(2,1)} %broadcast_in_dim.19), calls=%async_computation.1 | async-start | bytes 2097152 | tf_op jit(solution)/shard_map/all_to_all | solution.py:48
  75.9 3.1 %copy.53 = bf16[2,128,4096]{1,2,0:T(8,128)(2,1)S(1)} copy(bf16[2,128,4096]{2,1,0:T(8,128)(2,1)} %param.15) | data formatting | bytes 4194304 | tf_op args[6]
  79.0 2.6 copy.54
  85.5 2.8 pad_maximum_fusion.2
  102.9 6.0 %fusion.7 = f32[3,128,1024]{2,1,0:T(8,128)S(1)} fusion(bf16[16,256,1024,1]{2,1,0,3:T(8,128)(2,1)} %bitcast.146, bf16[2,128,16,256]{3,1,2,0:T(8,128)(2,1)S(1)} %bitcast.144, bf16[1,128,16,256]{3,1,2,0:T(8,128)(2,1)S(1)} %bitcast.145), kind=kOutput, calls=%fused_computation.22 | convolution fusion | flops 3222798336 | bytes 13107200 | tf_op jit(solution)/shard_map/pbsc,sch->pbh/dot_general | solution.py:110
  113.1 4.9 %convolution_bitcast_fusion = bf16[16,3,128,256]{2,3,1,0:T(8,128)(2,1)S(1)} fusion(bf16[16,256,1024,1]{2,1,3,0:T(8,128)(2,1)S(1)} %bitcast.151, bf16[2,128,1024]{2,1,0:T(8,128)(2,1)S(1)} %fusion.25, bf16[1,128,1024]{2,1,0:T(8,128)(2,1)S(1)} %get-tuple-element.6), kind=kOutput, calls=%fused_computation.14 | convolution fusion | flops 3222798336 | bytes 12320768 | tf_op jit(solution)/shard_map/pbh,sch->spbc/dot_general | solution.py:64
  120.6 3.2 %fusion.22 = bf16[2,128,1024,1]{2,1,0,3:T(8,128)(2,1)} fusion(bf16[16,256,1024,1]{2,1,3,0:T(8,128)(2,1)S(1)} %bitcast.152, bf16[16,2,128,256]{3,2,1,0:T(8,128)(2,1)S(1)} %gather_fusion, f32[128,1024]{1,0:T(8,128)S(1)} %get-tuple-element.7), kind=kOutput, calls=%fused_computation.30 | convolution fusion | flops 2148007936 | bytes 11534336 | tf_op jit(solution)/shard_map/pbsc,sch->pbh/dot_general | solution.py:59
  125.8 6.0 %convert_bitcast_fusion = bf16[16,2,128,256]{2,3,1,0:T(8,128)(2,1)S(1)} fusion(bf16[16,256,1024,1]{2,1,3,0:T(8,128)(2,1)} %bitcast.147, bf16[2,128,1024,1]{2,1,0,3:T(8,128)(2,1)} %fusion.22), kind=kOutput, calls=%fused_computation.21 | convolution fusion | flops 2148532224 | bytes 11010048 | tf_op jit(solution)/shard_map/pbh,sch->spbc/dot_general | solution.py:61
  132.5 68.5 %all_to_all.26 = bf16[16,5,128,256]{2,3,1,0:T(8,128)(2,1)S(1)} all-to-all(bf16[16,5,128,256]{2,3,1,0:T(8,128)(2,1)S(1)} %pad_maximum_fusion), channel_id=1, replica_groups=mesh['dp'=8,'tensor'=16] {'tensor'}, dimensions={0} | all-to-all | bytes 10485760 | tf_op jit(solution)/shard_map/all_to_all | solution.py:42
  204.2 2.5 broadcast_in_dim.23
  206.7 4.8 %all-to-all-start.3 = ((bf16[16,4,128,256]{3,2,1,0:T(8,128)(2,1)}), bf16[16,4,128,256]{3,2,1,0:T(8,128)(2,1)}, u32[]{:S(2)}, u32[]{:S(2)}) async-start(bf16[16,4,128,256]{3,2,1,0:T(8,128)(2,1)} %broadcast_in_dim.23), calls=%async_computation.3 | async-start | bytes 8388608 | tf_op jit(solution)/shard_map/all_to_all | solution.py:48
  211.7 60.3 %all-to-all-done.3 = bf16[16,4,128,256]{3,2,1,0:T(8,128)(2,1)} async-done(((bf16[16,4,128,256]{3,2,1,0:T(8,128)(2,1)}), bf16[16,4,128,256]{3,2,1,0:T(8,128)(2,1)}, u32[]{:S(2)}, u32[]{:S(2)}) %all-to-all-start.3) | async-done | bytes 4194336 | tf_op jit(solution)/shard_map/all_to_all | solution.py:48
  272.0 6.5 %fusion.21 = bf16[2,128,1024,1]{2,1,0,3:T(8,128)(2,1)S(1)} fusion(bf16[16,4,128,256]{3,2,1,0:T(8,128)(2,1)} %all-to-all-done.3, bf16[16,256,1024,1]{2,1,3,0:T(8,128)(2,1)} %bitcast.153, f32[128,1024]{1,0:T(8,128)} %copy-done.4), kind=kOutput, calls=%fused_computation.29 | convolution fusion | flops 2148007936 | bytes 13631488 | tf_op jit(solution)/shard_map/spbc,sch->pbh/dot_general | solution.py:77
  278.5 6.5 %fusion = f32[128]{0:T(128)S(1)} fusion(bf16[16,256,1024,1]{2,1,3,0:T(8,128)(2,1)} %bitcast.148, bf16[2,128,1024,1]{2,1,0,3:T(8,128)(2,1)S(1)} %fusion.21, bf16[16,4,128,256]{3,2,1,0:T(8,128)(2,1)} %all-to-all-done.3), kind=kOutput, calls=%fused_computation.8 | convolution fusion | flops 2150629376 | bytes 11010560 | tf_op jit(solution)/shard_map/pbh,sch->spbc/dot_general | solution.py:81
  285.7 4.4 %all-to-all-start.4 = ((f32[16,1,128]{2,1,0:T(1,128)}), f32[16,1,128]{2,1,0:T(1,128)S(1)}, u32[]{:S(2)}, u32[]{:S(2)}) async-start(f32[16,1,128]{2,1,0:T(1,128)} %broadcast_in_dim.24), calls=%async_computation.4 | async-start | bytes 16384 | tf_op jit(solution)/shard_map/all_to_all | solution.py:53
  290.8 6.8 %all-to-all-done.4 = f32[16,1,128]{2,1,0:T(1,128)S(1)} async-done(((f32[16,1,128]{2,1,0:T(1,128)}), f32[16,1,128]{2,1,0:T(1,128)S(1)}, u32[]{:S(2)}, u32[]{:S(2)}) %all-to-all-start.4) | async-done | bytes 8224 | tf_op jit(solution)/shard_map/all_to_all | solution.py:53
  (96 shorter events, 54.3 us)
Async XLA Ops:
  0.6 24.2 %collective-permute-start.6 = (bf16[512,1024]{1,0:T(8,128)(2,1)}, bf16[512,1024]{1,0:T(8,128)(2,1)}, u32[]{:S(2)}, u32[]{:S(2)}) collective-permute-start(bf16[512,1024]{1,0:T(8,128)(2,1)} %param.14), channel_id=1, source_target_pairs={{0,16},{16,0},{32,48},{48,32},{64,80},{80,64},{96,112},{112,96},{1... | collective-permute-start | bytes 3145736 | tf_op jit(solution)/shard_map/ppermute | solution.py:25
  0.7 28.0 %collective-permute-start.7 = (bf16[512,1024]{1,0:T(8,128)(2,1)}, bf16[512,1024]{1,0:T(8,128)(2,1)S(1)}, u32[]{:S(2)}, u32[]{:S(2)}) collective-permute-start(bf16[512,1024]{1,0:T(8,128)(2,1)} %param.14), channel_id=1, source_target_pairs={{0,32},{16,48},{32,64},{48,80},{64,96},{80,112},{96,0},{112,16},{1... | collective-permute-start | bytes 3145736 | tf_op jit(solution)/shard_map/ppermute | solution.py:23
  2.5 26.3 %collective-permute-start.8 = (bf16[512,1024]{1,0:T(8,128)(2,1)}, bf16[512,1024]{1,0:T(8,128)(2,1)}, u32[]{:S(2)}, u32[]{:S(2)}) collective-permute-start(bf16[512,1024]{1,0:T(8,128)(2,1)} %param.14), channel_id=1, source_target_pairs={{0,96},{16,112},{32,0},{48,16},{64,32},{80,48},{96,64},{112,80},{1... | collective-permute-start | bytes 3145736 | tf_op jit(solution)/shard_map/ppermute | solution.py:24
  13.4 45.7 %all-to-all-start = ((bf16[128,2,16,256]{3,1,0,2:T(2,128)(2,1)}), bf16[128,2,16,256]{3,1,0,2:T(2,128)(2,1)}, u32[]{:S(2)}, u32[]{:S(2)}) async-start(bf16[128,2,16,256]{3,1,0,2:T(2,128)(2,1)} %copy.50), calls=%async_computation | async-start | bytes 4194304 | tf_op jit(solution)/shard_map/all_to_all | solution.py:101
  21.5 28.9 %collective-permute-start.1 = (bf16[512,1024]{1,0:T(8,128)(2,1)}, bf16[512,1024]{1,0:T(8,128)(2,1)S(1)}, u32[]{:S(2)}, u32[]{:S(2)}) collective-permute-start(bf16[512,1024]{1,0:T(8,128)(2,1)} %param.13), channel_id=1, source_target_pairs={{0,32},{16,48},{32,64},{48,80},{64,96},{80,112},{96,0},{112,16},{1... | collective-permute-start | bytes 3145736 | tf_op jit(solution)/shard_map/ppermute | solution.py:23
  21.9 29.3 %collective-permute-start.2 = (bf16[512,1024]{1,0:T(8,128)(2,1)}, bf16[512,1024]{1,0:T(8,128)(2,1)S(1)}, u32[]{:S(2)}, u32[]{:S(2)}) collective-permute-start(bf16[512,1024]{1,0:T(8,128)(2,1)} %param.13), channel_id=1, source_target_pairs={{0,96},{16,112},{32,0},{48,16},{64,32},{80,48},{96,64},{112,80},{1... | collective-permute-start | bytes 3145736 | tf_op jit(solution)/shard_map/ppermute | solution.py:24
  24.8 27.9 %collective-permute-start = (bf16[512,1024]{1,0:T(8,128)(2,1)}, bf16[512,1024]{1,0:T(8,128)(2,1)S(1)}, u32[]{:S(2)}, u32[]{:S(2)}) collective-permute-start(bf16[512,1024]{1,0:T(8,128)(2,1)} %param.13), channel_id=1, source_target_pairs={{0,16},{16,0},{32,48},{48,32},{64,80},{80,64},{96,112},{112,96},{1... | collective-permute-start | bytes 3145736 | tf_op jit(solution)/shard_map/ppermute | solution.py:25
  31.5 22.8 %copy-start.6 = (bf16[4096,1024]{1,0:T(8,128)(2,1)}, bf16[4096,1024]{1,0:T(8,128)(2,1)S(1)}, u32[]{:S(2)}) copy-start(bf16[4096,1024]{1,0:T(8,128)(2,1)S(1)} %get-tuple-element.11) | copy-start | bytes 25165828
  31.5 56.8 %collective-permute-start.9 = (bf16[512,1024]{1,0:T(8,128)(2,1)}, bf16[512,1024]{1,0:T(8,128)(2,1)}, u32[]{:S(2)}, u32[]{:S(2)}) collective-permute-start(bf16[512,1024]{1,0:T(8,128)(2,1)} %get-tuple-element.10), channel_id=1, source_target_pairs={{0,32},{16,112},{32,64},{48,16},{64,96},{80,48},{96,0},{112,80},{1... | collective-permute-start | bytes 3145736 | tf_op jit(solution)/shard_map/ppermute | solution.py:29
  52.7 11.3 %copy-start.8 = (bf16[128,256]{1,0:T(8,128)(2,1)S(1)}, bf16[128,256]{1,0:T(8,128)(2,1)}, u32[]{:S(2)}) copy-start(bf16[128,256]{1,0:T(8,128)(2,1)} %param.12) | copy-start | bytes 196612
  52.7 43.0 %collective-permute-start.4 = (bf16[2,512,1024]{2,1,0:T(8,128)(2,1)}, bf16[2,512,1024]{2,1,0:T(8,128)(2,1)}, u32[]{:S(2)}, u32[]{:S(2)}) collective-permute-start(bf16[2,512,1024]{2,1,0:T(8,128)(2,1)} %pad_maximum_fusion.1), channel_id=1, source_target_pairs={{0,16},{16,0},{32,48},{48,32},{64,80},{80,64},{96,112},{112,96},{1... | collective-permute-start | bytes 6291464 | tf_op jit(solution)/shard_map/ppermute | solution.py:30
  52.9 20.2 %copy-start.9 = (s32[8]{0:T(128)S(1)}, s32[8]{0:T(128)}, u32[]{:S(2)}) copy-start(s32[8]{0:T(128)} %constant.76.clone) | copy-start | bytes 100
  52.9 20.2 %copy-start.10 = (s32[8]{0:T(128)S(1)}, s32[8]{0:T(128)}, u32[]{:S(2)}) copy-start(s32[8]{0:T(128)} %constant.77.clone) | copy-start | bytes 100
  57.6 17.0 %collective-permute-start.3 = (bf16[512,1024]{1,0:T(8,128)(2,1)}, bf16[512,1024]{1,0:T(8,128)(2,1)}, u32[]{:S(2)}, u32[]{:S(2)}) collective-permute-start(bf16[512,1024]{1,0:T(8,128)(2,1)} %get-tuple-element.8), channel_id=1, source_target_pairs={{0,32},{16,112},{32,64},{48,16},{64,96},{80,48},{96,0},{112,80},{1... | collective-permute-start | bytes 3145736 | tf_op jit(solution)/shard_map/ppermute | solution.py:29
  65.2 28.7 %all-to-all-start.1 = ((bf16[16,128,256]{2,1,0:T(8,128)(2,1)}), bf16[16,128,256]{2,1,0:T(8,128)(2,1)}, u32[]{:S(2)}, u32[]{:S(2)}) async-start(bf16[16,128,256]{2,1,0:T(8,128)(2,1)} %broadcast_in_dim.19), calls=%async_computation.1 | async-start | bytes 2097152 | tf_op jit(solution)/shard_map/all_to_all | solution.py:48
  74.6 25.9 %collective-permute-start.5 = (bf16[512,1024]{1,0:T(8,128)(2,1)}, bf16[512,1024]{1,0:T(8,128)(2,1)}, u32[]{:S(2)}, u32[]{:S(2)}) collective-permute-start(bf16[512,1024]{1,0:T(8,128)(2,1)} %collective-permute-done.3), channel_id=1, source_target_pairs={{0,16},{16,0},{32,48},{48,32},{64,80},{80,64},{96,112},{112,96},{1... | collective-permute-start | bytes 3145736 | tf_op jit(solution)/shard_map/ppermute | solution.py:31
  88.3 20.8 %collective-permute-start.10 = (bf16[2,512,1024]{2,1,0:T(8,128)(2,1)}, bf16[2,512,1024]{2,1,0:T(8,128)(2,1)}, u32[]{:S(2)}, u32[]{:S(2)}) collective-permute-start(bf16[2,512,1024]{2,1,0:T(8,128)(2,1)} %pad_maximum_fusion.2), channel_id=1, source_target_pairs={{0,16},{16,0},{32,48},{48,32},{64,80},{80,64},{96,112},{112,96},{1... | collective-permute-start | bytes 6291464 | tf_op jit(solution)/shard_map/ppermute | solution.py:30
  88.3 23.4 %collective-permute-start.11 = (bf16[512,1024]{1,0:T(8,128)(2,1)}, bf16[512,1024]{1,0:T(8,128)(2,1)}, u32[]{:S(2)}, u32[]{:S(2)}) collective-permute-start(bf16[512,1024]{1,0:T(8,128)(2,1)} %collective-permute-done.9), channel_id=1, source_target_pairs={{0,16},{16,0},{32,48},{48,32},{64,80},{80,64},{96,112},{112,96},{1... | collective-permute-start | bytes 3145736 | tf_op jit(solution)/shard_map/ppermute | solution.py:31
  100.5 8.6 %slice-start = ((s8[8388608]{0:T(1024)(128)(4,1)}), s8[4194304]{0:T(1024)(128)(4,1)S(1)}, s32[]{:S(2)}) async-start(s8[8388608]{0:T(1024)(128)(4,1)} %bitcast.149), calls=%async_computation.5 | async-start | bytes 8388608
  109.0 11.7 %copy-start.4 = (f32[128,1024]{1,0:T(8,128)}, f32[128,1024]{1,0:T(8,128)S(1)}, u32[]{:S(2)}) copy-start(f32[128,1024]{1,0:T(8,128)S(1)} %get-tuple-element.7) | copy-start | bytes 1572868
  113.1 7.6 %copy-start.7 = (bf16[4096,1024]{1,0:T(8,128)(2,1)}, bf16[4096,1024]{1,0:T(8,128)(2,1)S(1)}, u32[]{:S(2)}) copy-start(bf16[4096,1024]{1,0:T(8,128)(2,1)S(1)} %constant_dynamic-update-slice_fusion.6) | copy-start | bytes 25165828
  206.7 65.3 %all-to-all-start.3 = ((bf16[16,4,128,256]{3,2,1,0:T(8,128)(2,1)}), bf16[16,4,128,256]{3,2,1,0:T(8,128)(2,1)}, u32[]{:S(2)}, u32[]{:S(2)}) async-start(bf16[16,4,128,256]{3,2,1,0:T(8,128)(2,1)} %broadcast_in_dim.23), calls=%async_computation.3 | async-start | bytes 8388608 | tf_op jit(solution)/shard_map/all_to_all | solution.py:48
  272.0 26.1 %copy-start.1 = (bf16[128,8192]{1,0:T(8,128)(2,1)S(1)}, bf16[128,8192]{1,0:T(8,128)(2,1)}, u32[]{:S(2)}) copy-start(bf16[128,8192]{1,0:T(8,128)(2,1)} %param.11) | copy-start | bytes 6291460
  285.7 11.9 %all-to-all-start.4 = ((f32[16,1,128]{2,1,0:T(1,128)}), f32[16,1,128]{2,1,0:T(1,128)S(1)}, u32[]{:S(2)}, u32[]{:S(2)}) async-start(f32[16,1,128]{2,1,0:T(1,128)} %broadcast_in_dim.24), calls=%async_computation.4 | async-start | bytes 16384 | tf_op jit(solution)/shard_map/all_to_all | solution.py:53
  (5 other events, 26.0 us)

commit v11 on v9

--- a/solution.py
+++ b/solution.py
@@ -78,8 +78,10 @@
         "spbc,sch->pbh", uv_pieces[:, :probes_n], w_out_p, preferred_element_type=jnp.float32
     )
     scaled3 = (pulled3 * slope[None]).astype(jnp.bfloat16)
-    part3 = jnp.einsum("pbh,sch->spbc", scaled3, w_in_p, preferred_element_type=jnp.float32)
-    third = jnp.sum(uv_pieces[:, probes_n:].astype(jnp.float32) * part3, axis=(0, 1, 3))
+    v_win = jnp.einsum(
+        "spbc,sch->pbh", uv_pieces[:, probes_n:], w_in_p, preferred_element_type=jnp.float32
+    )
+    third = jnp.sum(v_win * scaled3.astype(jnp.float32), axis=(0, 2))
     coeffs = [(-1.0) ** k / (k + 1) for k in range(TERMS)]
     local_sum = coeffs[0] * first + coeffs[1] * second + coeffs[2] * third
     return psum_a2a(local_sum), side

time: 299 us -> 299 us (level)
  no operation moved by 1% of the time
where the time goes in v11:
time: 299 us; the launch traced here: 296 us
  waiting for transfers between devices  83.6 us (28%)
  blocking collectives  68.1 us (23%)
  local copies, waits for them, and re-layouts  54.4 us (18%)
  matrix products  38.3 us (13%)
  starting transfers between devices  34.6 us (12%)
  other arithmetic  15.7 us (5%)
    all_to_all x1, blocking collectives, reduce_scatter_pieces(): received = lax.all_to_all(pieces.astype(jnp.bfloat16), 'tensor', 0, 0)  68.1 us
    all_to_all x2, waiting for transfers between devices, all_gather_pieces(): lax.all_to_all(jnp.broadcast_to(piece[None], (n,) + piece.shape), 'tensor...  61.2 us
    unnamed x44, local copies, waits for them, and re-layouts  29 us
    ppermute x2, waiting for transfers between devices, gather_dp(): from_below = lax.ppermute(block, 'dp', up)  13 us
    all_to_all x2, starting transfers between devices, all_gather_pieces(): lax.all_to_all(jnp.broadcast_to(piece[None], (n,) + piece.shape), 'tensor...  11.9 us
    all_to_all x1, starting transfers between devices, reduce_scatter_pieces(): received = lax.all_to_all(pieces.astype(jnp.bfloat16), 'tensor', 0, 0)  8.04 us
    dot_general x1, matrix products, series(): jnp.einsum('spbc,sch->pbh', uv_pieces[:, :probes_n], w_out_p, preferred_e...  6.48 us
    dot_general x1, matrix products, series(): jnp.einsum('spbc,sch->pbh', uv_pieces[:, probes_n:], w_in_p, preferred_el...  6.47 us
  transfers between devices with their start and end apart: 16, of which 5 were waited for; matrix products, arithmetic and copies ran while one was open for 22% of the time, Pallas kernels for 0%

profile of v11, /device:TPU:0, one launch (start us, length us, event | category | flops | bytes accessed | tf_op | source)
XLA Modules:
  0.0 295.7 jit_solution(6087953044549974457)
XLA Ops:
  4.0 3.5 %copy.74 = bf16[16,8,32,256]{3,2,1,0:T(8,128)(2,1)} copy(bf16[16,8,32,256]{3,1,2,0:T(8,128)(2,1)} %bitcast.147) | data formatting | bytes 4194304
  7.6 5.3 %convert_bitcast_fusion.1 = bf16[16,128,2,256]{3,1,0,2:T(8,128)(2,1)} fusion(bf16[128,2,16,256]{3,2,1,0:T(8,128)(2,1)} %bitcast.142, bf16[128,4096]{1,0:T(8,128)(2,1)S(1)} %copy-done, bf16[4096,128]{1,0:T(8,128)(2,1)} %param.10), kind=kOutput, calls=%fused_computation.21 | convolution fusion | flops 403783680 | bytes 6291456 | tf_op jit(solution)/shard_map/bk,kmsc->sbmc/dot_general | solution.py:102
  12.8 3.1 %copy.52 = bf16[16,128,2,256]{3,1,2,0:T(8,128)(2,1)} copy(bf16[16,128,2,256]{3,1,0,2:T(8,128)(2,1)} %convert_bitcast_fusion.1) | data formatting | bytes 4194304 | tf_op jit(solution)/shard_map/convert_element_type | solution.py:42
  16.0 8.0 %all-to-all-start = ((bf16[16,128,2,256]{3,1,2,0:T(8,128)(2,1)}), bf16[16,128,2,256]{3,1,2,0:T(8,128)(2,1)}, u32[]{:S(2)}, u32[]{:S(2)}) async-start(bf16[16,128,2,256]{3,1,2,0:T(8,128)(2,1)} %copy.52), calls=%async_computation | async-start | bytes 4194304 | tf_op jit(solution)/shard_map/all_to_all | solution.py:42
  27.1 2.9 collective-permute-start.8
  37.3 13.0 %collective-permute-done.7 = bf16[512,1024]{1,0:T(8,128)(2,1)S(1)} collective-permute-done((bf16[512,1024]{1,0:T(8,128)(2,1)}, bf16[512,1024]{1,0:T(8,128)(2,1)S(1)}, u32[]{:S(2)}, u32[]{:S(2)}) %collective-permute-start.7) | collective-permute-done | bytes 1048608 | tf_op jit(solution)/shard_map/ppermute | solution.py:23
  50.5 3.5 %collective-permute-done.8 = bf16[512,1024]{1,0:T(8,128)(2,1)S(1)} collective-permute-done((bf16[512,1024]{1,0:T(8,128)(2,1)}, bf16[512,1024]{1,0:T(8,128)(2,1)S(1)}, u32[]{:S(2)}, u32[]{:S(2)}) %collective-permute-start.8) | collective-permute-done | bytes 1048608 | tf_op jit(solution)/shard_map/ppermute | solution.py:24
  56.4 3.2 %copy-done.7 = bf16[4096,1024]{1,0:T(8,128)(2,1)} copy-done((bf16[4096,1024]{1,0:T(8,128)(2,1)}, bf16[4096,1024]{1,0:T(8,128)(2,1)S(1)}, u32[]{:S(2)}) %copy-start.7) | copy-done | bytes 8388632
  63.9 7.2 %all-to-all-start.1 = ((bf16[16,128,256]{2,1,0:T(8,128)(2,1)}), bf16[16,128,256]{2,1,0:T(8,128)(2,1)}, u32[]{:S(2)}, u32[]{:S(2)}) async-start(bf16[16,128,256]{2,1,0:T(8,128)(2,1)} %broadcast_in_dim.19), calls=%async_computation.1 | async-start | bytes 2097152 | tf_op jit(solution)/shard_map/all_to_all | solution.py:48
  73.7 3.1 %copy.53 = bf16[2,128,4096]{1,2,0:T(8,128)(2,1)S(1)} copy(bf16[2,128,4096]{2,1,0:T(8,128)(2,1)} %param.15) | data formatting | bytes 4194304 | tf_op args[6]
  76.8 2.6 copy.54
  83.2 2.8 pad_maximum_fusion.2
  101.0 6.0 %fusion.10 = f32[3,128,1024]{2,1,0:T(8,128)S(1)} fusion(bf16[16,256,1024,1]{2,1,0,3:T(8,128)(2,1)} %bitcast.155, bf16[2,128,16,256]{3,1,2,0:T(8,128)(2,1)S(1)} %bitcast.148, bf16[1,128,16,256]{3,1,2,0:T(8,128)(2,1)S(1)} %bitcast.149), kind=kOutput, calls=%fused_computation.22 | convolution fusion | flops 3222798336 | bytes 13107200 | tf_op jit(solution)/shard_map/pbsc,sch->pbh/dot_general | solution.py:111
  111.2 4.9 %convolution_bitcast_fusion = bf16[16,3,128,256]{2,3,1,0:T(8,128)(2,1)S(1)} fusion(bf16[16,256,1024,1]{2,1,3,0:T(8,128)(2,1)S(1)} %bitcast.152, bf16[2,128,1024]{2,1,0:T(8,128)(2,1)S(1)} %fusion.30, bf16[1,128,1024]{2,1,0:T(8,128)(2,1)S(1)} %get-tuple-element.8), kind=kOutput, calls=%fused_computation.11 | convolution fusion | flops 3222798336 | bytes 12320768 | tf_op jit(solution)/shard_map/pbh,sch->spbc/dot_general | solution.py:64
  118.8 3.2 %fusion.27 = bf16[2,128,1024,1]{2,1,0,3:T(8,128)(2,1)} fusion(bf16[16,256,1024,1]{2,1,3,0:T(8,128)(2,1)S(1)} %bitcast.153, bf16[16,2,128,256]{3,2,1,0:T(8,128)(2,1)S(1)} %gather_fusion, f32[128,1024]{1,0:T(8,128)S(1)} %get-tuple-element.9), kind=kOutput, calls=%fused_computation.33 | convolution fusion | flops 2148007936 | bytes 11534336 | tf_op jit(solution)/shard_map/pbsc,sch->pbh/dot_general | solution.py:59
  124.0 6.0 %convert_bitcast_fusion = bf16[16,2,128,256]{2,3,1,0:T(8,128)(2,1)S(1)} fusion(bf16[16,256,1024,1]{2,1,3,0:T(8,128)(2,1)} %bitcast.156, bf16[2,128,1024,1]{2,1,0,3:T(8,128)(2,1)} %fusion.27), kind=kOutput, calls=%fused_computation.20 | convolution fusion | flops 2148532224 | bytes 11010048 | tf_op jit(solution)/shard_map/pbh,sch->spbc/dot_general | solution.py:61
  130.6 68.1 %all_to_all.26 = bf16[16,5,128,256]{2,3,1,0:T(8,128)(2,1)S(1)} all-to-all(bf16[16,5,128,256]{2,3,1,0:T(8,128)(2,1)S(1)} %pad_maximum_fusion), channel_id=1, replica_groups=mesh['dp'=8,'tensor'=16] {'tensor'}, dimensions={0} | all-to-all | bytes 10485760 | tf_op jit(solution)/shard_map/all_to_all | solution.py:42
  202.0 2.5 broadcast_in_dim.23
  204.5 4.8 %all-to-all-start.3 = ((bf16[16,4,128,256]{3,2,1,0:T(8,128)(2,1)}), bf16[16,4,128,256]{3,2,1,0:T(8,128)(2,1)}, u32[]{:S(2)}, u32[]{:S(2)}) async-start(bf16[16,4,128,256]{3,2,1,0:T(8,128)(2,1)} %broadcast_in_dim.23), calls=%async_computation.3 | async-start | bytes 8388608 | tf_op jit(solution)/shard_map/all_to_all | solution.py:48
  209.4 60.4 %all-to-all-done.3 = bf16[16,4,128,256]{3,2,1,0:T(8,128)(2,1)} async-done(((bf16[16,4,128,256]{3,2,1,0:T(8,128)(2,1)}), bf16[16,4,128,256]{3,2,1,0:T(8,128)(2,1)}, u32[]{:S(2)}, u32[]{:S(2)}) %all-to-all-start.3) | async-done | bytes 4194336 | tf_op jit(solution)/shard_map/all_to_all | solution.py:48
  269.8 6.5 %fusion.25 = f32[2,128,1024]{2,1,0:T(8,128)S(1)} fusion(bf16[16,4,128,256]{3,2,1,0:T(8,128)(2,1)} %all-to-all-done.3, bf16[16,256,1024,1]{2,1,3,0:T(8,128)(2,1)} %bitcast.154, f32[128,1024]{1,0:T(8,128)} %copy-done.6), kind=kOutput, calls=%fused_computation.31 | convolution fusion | flops 2148270080 | bytes 14155776 | tf_op jit(solution)/shard_map/spbc,sch->pbh/dot_general | solution.py:77
  276.2 6.5 %fusion.26 = f32[128]{0:T(128)S(1)} fusion(f32[2,128,1024]{2,1,0:T(8,128)S(1)} %fusion.25, bf16[16,4,128,256]{3,2,1,0:T(8,128)(2,1)} %all-to-all-done.3, bf16[16,256,1024,1]{2,1,3,0:T(8,128)(2,1)} %bitcast.157), kind=kOutput, calls=%fused_computation.32 | convolution fusion | flops 2148007936 | bytes 13632000 | tf_op jit(solution)/shard_map/spbc,sch->pbh/dot_general | solution.py:81
  283.3 4.4 %all-to-all-start.4 = ((f32[16,1,128]{2,1,0:T(1,128)}), f32[16,1,128]{2,1,0:T(1,128)S(1)}, u32[]{:S(2)}, u32[]{:S(2)}) async-start(f32[16,1,128]{2,1,0:T(1,128)} %broadcast_in_dim.24), calls=%async_computation.4 | async-start | bytes 16384 | tf_op jit(solution)/shard_map/all_to_all | solution.py:53
  289.4 5.9 %all-to-all-done.4 = f32[16,1,128]{2,1,0:T(1,128)S(1)} async-done(((f32[16,1,128]{2,1,0:T(1,128)}), f32[16,1,128]{2,1,0:T(1,128)S(1)}, u32[]{:S(2)}, u32[]{:S(2)}) %all-to-all-start.4) | async-done | bytes 8224 | tf_op jit(solution)/shard_map/all_to_all | solution.py:53
  (99 shorter events, 57.3 us)
Async XLA Ops:
  0.6 26.5 %collective-permute-start = (bf16[512,1024]{1,0:T(8,128)(2,1)}, bf16[512,1024]{1,0:T(8,128)(2,1)}, u32[]{:S(2)}, u32[]{:S(2)}) collective-permute-start(bf16[512,1024]{1,0:T(8,128)(2,1)} %param.13), channel_id=1, source_target_pairs={{0,16},{16,0},{32,48},{48,32},{64,80},{80,64},{96,112},{112,96},{1... | collective-permute-start | bytes 3145736 | tf_op jit(solution)/shard_map/ppermute | solution.py:25
  0.7 30.6 %collective-permute-start.1 = (bf16[512,1024]{1,0:T(8,128)(2,1)}, bf16[512,1024]{1,0:T(8,128)(2,1)S(1)}, u32[]{:S(2)}, u32[]{:S(2)}) collective-permute-start(bf16[512,1024]{1,0:T(8,128)(2,1)} %param.13), channel_id=1, source_target_pairs={{0,32},{16,48},{32,64},{48,80},{64,96},{80,112},{96,0},{112,16},{1... | collective-permute-start | bytes 3145736 | tf_op jit(solution)/shard_map/ppermute | solution.py:23
  2.5 28.9 %collective-permute-start.2 = (bf16[512,1024]{1,0:T(8,128)(2,1)}, bf16[512,1024]{1,0:T(8,128)(2,1)S(1)}, u32[]{:S(2)}, u32[]{:S(2)}) collective-permute-start(bf16[512,1024]{1,0:T(8,128)(2,1)} %param.13), channel_id=1, source_target_pairs={{0,96},{16,112},{32,0},{48,16},{64,32},{80,48},{96,64},{112,80},{1... | collective-permute-start | bytes 3145736 | tf_op jit(solution)/shard_map/ppermute | solution.py:24
  16.0 44.8 %all-to-all-start = ((bf16[16,128,2,256]{3,1,2,0:T(8,128)(2,1)}), bf16[16,128,2,256]{3,1,2,0:T(8,128)(2,1)}, u32[]{:S(2)}, u32[]{:S(2)}) async-start(bf16[16,128,2,256]{3,1,2,0:T(8,128)(2,1)} %copy.52), calls=%async_computation | async-start | bytes 4194304 | tf_op jit(solution)/shard_map/all_to_all | solution.py:42
  24.0 26.3 %collective-permute-start.7 = (bf16[512,1024]{1,0:T(8,128)(2,1)}, bf16[512,1024]{1,0:T(8,128)(2,1)S(1)}, u32[]{:S(2)}, u32[]{:S(2)}) collective-permute-start(bf16[512,1024]{1,0:T(8,128)(2,1)} %param.14), channel_id=1, source_target_pairs={{0,32},{16,48},{32,64},{48,80},{64,96},{80,112},{96,0},{112,16},{1... | collective-permute-start | bytes 3145736 | tf_op jit(solution)/shard_map/ppermute | solution.py:23
  24.5 10.7 %collective-permute-start.6 = (bf16[512,1024]{1,0:T(8,128)(2,1)}, bf16[512,1024]{1,0:T(8,128)(2,1)}, u32[]{:S(2)}, u32[]{:S(2)}) collective-permute-start(bf16[512,1024]{1,0:T(8,128)(2,1)} %param.14), channel_id=1, source_target_pairs={{0,16},{16,0},{32,48},{48,32},{64,80},{80,64},{96,112},{112,96},{1... | collective-permute-start | bytes 3145736 | tf_op jit(solution)/shard_map/ppermute | solution.py:25
  27.1 26.8 %collective-permute-start.8 = (bf16[512,1024]{1,0:T(8,128)(2,1)}, bf16[512,1024]{1,0:T(8,128)(2,1)S(1)}, u32[]{:S(2)}, u32[]{:S(2)}) collective-permute-start(bf16[512,1024]{1,0:T(8,128)(2,1)} %param.14), channel_id=1, source_target_pairs={{0,96},{16,112},{32,0},{48,16},{64,32},{80,48},{96,64},{112,80},{1... | collective-permute-start | bytes 3145736 | tf_op jit(solution)/shard_map/ppermute | solution.py:24
  32.9 23.6 %copy-start.9 = (bf16[4096,1024]{1,0:T(8,128)(2,1)}, bf16[4096,1024]{1,0:T(8,128)(2,1)S(1)}, u32[]{:S(2)}) copy-start(bf16[4096,1024]{1,0:T(8,128)(2,1)S(1)} %get-tuple-element.11) | copy-start | bytes 25165828
  32.9 39.6 %collective-permute-start.3 = (bf16[512,1024]{1,0:T(8,128)(2,1)}, bf16[512,1024]{1,0:T(8,128)(2,1)}, u32[]{:S(2)}, u32[]{:S(2)}) collective-permute-start(bf16[512,1024]{1,0:T(8,128)(2,1)} %get-tuple-element.10), channel_id=1, source_target_pairs={{0,32},{16,112},{32,64},{48,16},{64,96},{80,48},{96,0},{112,80},{1... | collective-permute-start | bytes 3145736 | tf_op jit(solution)/shard_map/ppermute | solution.py:29
  34.5 28.2 %copy-start.10 = (bf16[128,256]{1,0:T(8,128)(2,1)S(1)}, bf16[128,256]{1,0:T(8,128)(2,1)}, u32[]{:S(2)}) copy-start(bf16[128,256]{1,0:T(8,128)(2,1)} %param.12) | copy-start | bytes 196612
  34.5 59.3 %collective-permute-start.4 = (bf16[2,512,1024]{2,1,0:T(8,128)(2,1)}, bf16[2,512,1024]{2,1,0:T(8,128)(2,1)}, u32[]{:S(2)}, u32[]{:S(2)}) collective-permute-start(bf16[2,512,1024]{2,1,0:T(8,128)(2,1)} %pad_maximum_fusion.1), channel_id=1, source_target_pairs={{0,16},{16,0},{32,48},{48,32},{64,80},{80,64},{96,112},{112,96},{1... | collective-permute-start | bytes 6291464 | tf_op jit(solution)/shard_map/ppermute | solution.py:30
  50.4 20.6 %copy-start.11 = (s32[8]{0:T(128)S(1)}, s32[8]{0:T(128)}, u32[]{:S(2)}) copy-start(s32[8]{0:T(128)} %constant.76.clone) | copy-start | bytes 100
  50.5 20.6 %copy-start.12 = (s32[8]{0:T(128)S(1)}, s32[8]{0:T(128)}, u32[]{:S(2)}) copy-start(s32[8]{0:T(128)} %constant.77.clone) | copy-start | bytes 100
  59.7 26.3 %collective-permute-start.9 = (bf16[512,1024]{1,0:T(8,128)(2,1)}, bf16[512,1024]{1,0:T(8,128)(2,1)}, u32[]{:S(2)}, u32[]{:S(2)}) collective-permute-start(bf16[512,1024]{1,0:T(8,128)(2,1)} %get-tuple-element.12), channel_id=1, source_target_pairs={{0,32},{16,112},{32,64},{48,16},{64,96},{80,48},{96,0},{112,80},{1... | collective-permute-start | bytes 3145736 | tf_op jit(solution)/shard_map/ppermute | solution.py:29
  63.9 28.1 %all-to-all-start.1 = ((bf16[16,128,256]{2,1,0:T(8,128)(2,1)}), bf16[16,128,256]{2,1,0:T(8,128)(2,1)}, u32[]{:S(2)}, u32[]{:S(2)}) async-start(bf16[16,128,256]{2,1,0:T(8,128)(2,1)} %broadcast_in_dim.19), calls=%async_computation.1 | async-start | bytes 2097152 | tf_op jit(solution)/shard_map/all_to_all | solution.py:48
  72.5 26.1 %collective-permute-start.5 = (bf16[512,1024]{1,0:T(8,128)(2,1)}, bf16[512,1024]{1,0:T(8,128)(2,1)}, u32[]{:S(2)}, u32[]{:S(2)}) collective-permute-start(bf16[512,1024]{1,0:T(8,128)(2,1)} %collective-permute-done.3), channel_id=1, source_target_pairs={{0,16},{16,0},{32,48},{48,32},{64,80},{80,64},{96,112},{112,96},{1... | collective-permute-start | bytes 3145736 | tf_op jit(solution)/shard_map/ppermute | solution.py:31
  86.0 21.3 %collective-permute-start.10 = (bf16[2,512,1024]{2,1,0:T(8,128)(2,1)}, bf16[2,512,1024]{2,1,0:T(8,128)(2,1)}, u32[]{:S(2)}, u32[]{:S(2)}) collective-permute-start(bf16[2,512,1024]{2,1,0:T(8,128)(2,1)} %pad_maximum_fusion.2), channel_id=1, source_target_pairs={{0,16},{16,0},{32,48},{48,32},{64,80},{80,64},{96,112},{112,96},{1... | collective-permute-start | bytes 6291464 | tf_op jit(solution)/shard_map/ppermute | solution.py:30
  86.0 23.9 %collective-permute-start.11 = (bf16[512,1024]{1,0:T(8,128)(2,1)}, bf16[512,1024]{1,0:T(8,128)(2,1)}, u32[]{:S(2)}, u32[]{:S(2)}) collective-permute-start(bf16[512,1024]{1,0:T(8,128)(2,1)} %collective-permute-done.9), channel_id=1, source_target_pairs={{0,16},{16,0},{32,48},{48,32},{64,80},{80,64},{96,112},{112,96},{1... | collective-permute-start | bytes 3145736 | tf_op jit(solution)/shard_map/ppermute | solution.py:31
  98.6 8.7 %slice-start = ((s8[8388608]{0:T(1024)(128)(4,1)}), s8[4194304]{0:T(1024)(128)(4,1)S(1)}, s32[]{:S(2)}) async-start(s8[8388608]{0:T(1024)(128)(4,1)} %bitcast.150), calls=%async_computation.5 | async-start | bytes 8388608
  107.1 11.6 %copy-start.6 = (f32[128,1024]{1,0:T(8,128)}, f32[128,1024]{1,0:T(8,128)S(1)}, u32[]{:S(2)}) copy-start(f32[128,1024]{1,0:T(8,128)S(1)} %get-tuple-element.9) | copy-start | bytes 1572868
  111.2 7.5 %copy-start.8 = (bf16[4096,1024]{1,0:T(8,128)(2,1)}, bf16[4096,1024]{1,0:T(8,128)(2,1)S(1)}, u32[]{:S(2)}) copy-start(bf16[4096,1024]{1,0:T(8,128)(2,1)S(1)} %constant_dynamic-update-slice_fusion.6) | copy-start | bytes 25165828
  204.5 65.3 %all-to-all-start.3 = ((bf16[16,4,128,256]{3,2,1,0:T(8,128)(2,1)}), bf16[16,4,128,256]{3,2,1,0:T(8,128)(2,1)}, u32[]{:S(2)}, u32[]{:S(2)}) async-start(bf16[16,4,128,256]{3,2,1,0:T(8,128)(2,1)} %broadcast_in_dim.23), calls=%async_computation.3 | async-start | bytes 8388608 | tf_op jit(solution)/shard_map/all_to_all | solution.py:48
  269.8 26.0 %copy-start.1 = (bf16[128,4096]{1,0:T(8,128)(2,1)S(1)}, bf16[128,4096]{1,0:T(8,128)(2,1)}, u32[]{:S(2)}) copy-start(bf16[128,4096]{1,0:T(8,128)(2,1)} %param.9) | copy-start | bytes 3145732
  283.3 11.9 %all-to-all-start.4 = ((f32[16,1,128]{2,1,0:T(1,128)}), f32[16,1,128]{2,1,0:T(1,128)S(1)}, u32[]{:S(2)}, u32[]{:S(2)}) async-start(f32[16,1,128]{2,1,0:T(1,128)} %broadcast_in_dim.24), calls=%async_computation.4 | async-start | bytes 16384 | tf_op jit(solution)/shard_map/all_to_all | solution.py:53
  (7 other events, 33.2 us)
